TPU v7x, 1024 devices: a whole 8x8x8 slice. The times are simulated.
1024 devices in a mesh: dir: 32 (over z, x_hi, core), tile: 32 (over x_lo, y).
Axes of the slice: x: 8 (x_hi: 2, x_lo: 4; x = x_hi * 4 + x_lo), y: 8, z: 8, core: 2. Of those that a mesh axis runs over, the one named last changes fastest.
Arguments:
- receiver_old: float32 [64, 1024, 8, 256], P('dir', 'tile'), may hold values from -6 to 6
- receiver_now: float32 [64, 1024, 8, 256], P('dir', 'tile'), may hold values from -6 to 6
- courant: bfloat16 [64, 1024, 8, 256], P('dir', 'tile'), may hold values from 0.019897461 to 0.1796875
- source_snaps: bfloat16 [4, 64, 1024, 8, 256], P(None, 'dir', 'tile'), may hold values from -6 to 6
- recorded: bfloat16 [4, 64, 1024, 256], P(None, 'dir', 'tile'), may hold values from -6 to 6
- row_owner: int32 [64, 1024, 1], P(None, 'tile'), may hold values from 0 to 31; in each aligned block of 32 rows (0 to 31, 32 to 63, ..., all dimensions but the last counted through in order) at most 2 rows name the same one
- band_start: int32 [64, 1024], P(None, 'tile'), may hold values from 0 to 28
- band_weight: bfloat16 [64, 1024, 4], P(None, 'tile'), may hold values from 0.019897461 to 0.119628906
Outputs:
- wavefield: float32 [64, 1024, 8, 256], P('dir', 'tile')
- stack: float32 [1024, 2048], P('tile', 'dir')
Inputs may be any that keep to these rules, and one draw needn't show every extreme that they name: `row_owner`: in the 32 rows of one direction held by one index of tile, no tile is named by more than 2 rows, a bound that some block reaches.
All inputs are finite; a program needn't handle non-finite values.
Results may differ from a plain program's by a relative error of at most 0.0029.
Values may be sent and summed in bfloat16 or wider, within the bound.
No kernel may reach another device: no remote copies, remote signals or barrier semaphores. Data moves between devices by JAX's collectives and lax.ppermute only.
A program may use at most 32 MiB of HBM per device.

v0:
```python
import jax
import jax.numpy as jnp
from jax import lax
from jax.sharding import PartitionSpec as P

STEPS = 4
BAND = 4


stencil_coef = (-205.0 / 72.0, 8.0 / 5.0, -1.0 / 5.0, 8.0 / 315.0, -1.0 / 560.0)


def with_halo(value, sides, width):
    for axis, dim in sides:
        count, length = (lax.axis_size(axis), value.shape[dim])
        up = [(i, (i + 1) % count) for i in range(count - 1)]
        down = [(j, i) for i, j in up]
        last = lax.slice_in_dim(value, length - width, length, axis=dim)
        leading = lax.slice_in_dim(value, 0, width, axis=dim)
        before = lax.ppermute(last, axis, up)
        after = lax.ppermute(leading, axis, down)
        value = jnp.concatenate([before, value, after], axis=dim)
    return value


def laplace(padded_all, rows_here, depth, across):
    middle = padded_all[..., 4 : 4 + rows_here, 4 : 4 + depth, 4 : 4 + across]
    result = 3.0 * stencil_coef[0] * middle
    for reach in range(1, 5):
        plus_x = padded_all[..., 4 + reach : 4 + reach + rows_here, 4 : 4 + depth, 4 : 4 + across]
        minus_x = padded_all[..., 4 - reach : 4 - reach + rows_here, 4 : 4 + depth, 4 : 4 + across]
        plus_z = padded_all[..., 4 : 4 + rows_here, 4 + reach : 4 + reach + depth, 4 : 4 + across]
        minus_z = padded_all[..., 4 : 4 + rows_here, 4 - reach : 4 - reach + depth, 4 : 4 + across]
        plus_y = padded_all[..., 4 : 4 + rows_here, 4 : 4 + depth, 4 + reach : 4 + reach + across]
        minus_y = padded_all[..., 4 : 4 + rows_here, 4 : 4 + depth, 4 - reach : 4 - reach + across]
        result = result + stencil_coef[reach] * (
            plus_x + minus_x + plus_z + minus_z + plus_y + minus_y
        )
    return result


def build_slots(owner_col, start_col, weight_col, n_tiles, capacity, rows_here):
    hits = (owner_col[:, :, None] == jnp.arange(n_tiles, dtype=jnp.int32)[None, None, :]).astype(
        jnp.int32
    )
    before = jnp.cumsum(hits, axis=1) - hits
    rank_row = jnp.sum(before * hits, axis=2)
    slot_row = owner_col * capacity + rank_row
    selector = (
        slot_row[:, None, :] == jnp.arange(n_tiles * capacity, dtype=jnp.int32)[None, :, None]
    ).astype(jnp.bfloat16)
    positions = start_col[:, :, None] + jnp.arange(BAND, dtype=jnp.int32)[None, None, :]
    placed = (positions[..., None] == jnp.arange(rows_here, dtype=jnp.int32)).astype(jnp.float32)
    band_rows = jnp.sum(weight_col.astype(jnp.float32)[..., None] * placed, axis=2).astype(
        jnp.bfloat16
    )
    band_cols = jnp.einsum(
        "ksr,krc->ksc", selector, band_rows, preferred_element_type=jnp.float32
    ).astype(jnp.bfloat16)
    return (selector, band_cols)


def apply_band(got_rows, got_cols, rows_here):
    flat_rows = got_rows.reshape(-1, got_rows.shape[-1])
    flat_cols = got_cols.reshape(-1, rows_here)
    return lax.dot_general(
        flat_cols, flat_rows, (((0,), (0,)), ((), ())), preferred_element_type=jnp.float32
    )


def per_device(
    receiver_old, receiver_now, courant, source_snaps, recorded, row_owner, band_start, band_weight
):
    local_dirs, rows_here, depth, across = receiver_now.shape
    speed_wide = courant.astype(jnp.float32)
    field_old = receiver_old
    field_now = receiver_now
    image_sum = jnp.zeros(field_now.shape, jnp.float32)
    for step in range(STEPS):
        padded_x = with_halo(field_now, (("tile", 1),), 4)
        padded_all = jnp.pad(padded_x, ((0, 0), (0, 0), (4, 4), (4, 4)))
        curvature = laplace(padded_all, rows_here, depth, across)
        curvature = curvature.at[:, :, 0, :].add(recorded[step].astype(jnp.float32))
        field_new = 2.0 * field_now - field_old + speed_wide * curvature
        image_sum = image_sum + source_snaps[step].astype(jnp.float32) * field_new
        field_old, field_now = (field_now, field_new)
    image_flat = image_sum.astype(jnp.bfloat16).reshape(local_dirs, rows_here, depth * across)
    n_tiles = lax.axis_size("tile")
    capacity = max(2, 2 * rows_here // n_tiles)
    owner_all = row_owner[:, :, 0]
    first_dir = lax.axis_index("dir") * local_dirs
    owner_here = lax.dynamic_slice_in_dim(owner_all, first_dir, local_dirs, 0)
    start_here = lax.dynamic_slice_in_dim(band_start, first_dir, local_dirs, 0)
    weight_here = lax.dynamic_slice_in_dim(band_weight, first_dir, local_dirs, 0)
    selector, band_cols = build_slots(
        owner_here, start_here, weight_here, n_tiles, capacity, rows_here
    )
    send_rows = jnp.einsum(
        "ksr,krp->ksp", selector, image_flat, preferred_element_type=jnp.float32
    ).astype(jnp.bfloat16)
    send_rows = send_rows.reshape(local_dirs, n_tiles, capacity, depth * across)
    band_cols = band_cols.reshape(local_dirs, n_tiles, capacity, rows_here)
    got_rows, got_cols = (
        lax.all_to_all(send_rows, "tile", split_axis=1, concat_axis=1, tiled=True),
        lax.all_to_all(band_cols, "tile", split_axis=1, concat_axis=1, tiled=True),
    )
    partial_img = apply_band(got_rows, got_cols, rows_here)
    stack = lax.psum_scatter(partial_img, "dir", scatter_dimension=1, tiled=True)
    return (field_now, stack)


def solution(mesh):
    return jax.shard_map(
        per_device,
        mesh=mesh,
        in_specs=(
            P("dir", "tile", None, None),
            P("dir", "tile", None, None),
            P("dir", "tile", None, None),
            P(None, "dir", "tile", None, None),
            P(None, "dir", "tile", None),
            P(None, "tile", None),
            P(None, "tile"),
            P(None, "tile", None),
        ),
        out_specs=(P("dir", "tile", None, None), P("tile", "dir")),
        check_vma=False,
    )
```

profile of v0, /device:TPU:16, one launch (start us, length us, event | category | flops | bytes accessed | tf_op | source)
XLA Modules:
  0.0 259.4 jit_solution(236128430146016536)
XLA Ops:
  7.2 0.9 fusion.123
  8.1 3.6 %collective-permute-start.1 = (f32[2,4,8,256]{3,2,1,0:T(8,128)S(1)}, f32[2,4,8,256]{3,2,1,0:T(8,128)S(1)}, u32[]{:S(2)}, u32[]{:S(2)}) collective-permute-start(f32[2,4,8,256]{3,2,1,0:T(8,128)S(1)} %get-tuple-element.60), channel_id=1, source_target_pairs={{0,1},{1,2},{2,3},{3,4},{4,5},{5,6},{6,7},{7,8},{8,9},{9,10},{10,1... | collective-permute-start | bytes 196616 | tf_op jit(solution)/shard_map/ppermute | solution.py:20
  11.7 12.6 %collective-permute-start = (f32[2,4,8,256]{3,2,1,0:T(8,128)S(1)}, f32[2,4,8,256]{3,2,1,0:T(8,128)S(1)}, u32[]{:S(2)}, u32[]{:S(2)}) collective-permute-start(f32[2,4,8,256]{3,2,1,0:T(8,128)S(1)} %get-tuple-element.61), channel_id=1, source_target_pairs={{1,0},{2,1},{3,2},{4,3},{5,4},{6,5},{7,6},{8,7},{9,8},{10,9},{11,1... | collective-permute-start | bytes 196616 | tf_op jit(solution)/shard_map/ppermute | solution.py:21
  24.3 0.8 fusion.124
  25.2 0.8 constant_dynamic-slice_fusion.2
  27.3 1.1 constant_dynamic-update-slice_fusion.1
  28.4 0.8 copy-done.2
  29.9 4.7 %fusion.98 = f32[2,32,8,256]{3,2,1,0:T(8,128)} fusion(f32[2,40,16,264]{3,2,1,0:T(8,128)S(1)} %select_maximum_fusion.6, f32[2,36,8,256]{3,2,1,0:T(8,128)} %copy-done.2, f32[2,36,8,256]{3,2,1,0:T(8,128)S(1)} %constant_dynamic-update-slice_fusion, f32[2,32,8,256]{3,2,1,0:T(8,128)S(1)} %copy-done.1), kind=kLoop, calls=%fused_computation.172 | loop fusion | flops 3801088 | bytes 13631488 | tf_op jit(solution)/shard_map/add | solution.py:36
  34.6 1.1 slice_add_fusion.35
  35.7 2.3 scatter-add.14
  38.1 1.3 fusion.87
  39.4 1.9 collective-permute-start.2
  41.3 3.9 %collective-permute-start.3 = (f32[2,4,8,256]{3,2,1,0:T(8,128)S(1)}, f32[2,4,8,256]{3,2,1,0:T(8,128)S(1)}, u32[]{:S(2)}, u32[]{:S(2)}) collective-permute-start(f32[2,4,8,256]{3,2,1,0:T(8,128)S(1)} %get-tuple-element.57), channel_id=1, source_target_pairs={{0,1},{1,2},{2,3},{3,4},{4,5},{5,6},{6,7},{7,8},{8,9},{9,10},{10,1... | collective-permute-start | bytes 196616 | tf_op jit(solution)/shard_map/ppermute | solution.py:20
  45.8 1.7 collective-permute-done.3
  48.1 2.2 fusion.67
  50.5 0.8 scatter-add.15
  51.4 1.9 collective-permute-start.4
  53.4 3.9 %collective-permute-start.5 = (f32[2,4,8,256]{3,2,1,0:T(8,128)S(1)}, f32[2,4,8,256]{3,2,1,0:T(8,128)S(1)}, u32[]{:S(2)}, u32[]{:S(2)}) collective-permute-start(f32[2,4,8,256]{3,2,1,0:T(8,128)S(1)} %get-tuple-element.55), channel_id=1, source_target_pairs={{0,1},{1,2},{2,3},{3,4},{4,5},{5,6},{6,7},{7,8},{8,9},{9,10},{10,1... | collective-permute-start | bytes 196616 | tf_op jit(solution)/shard_map/ppermute | solution.py:20
  57.6 1.9 collective-permute-done.5
  60.1 2.2 fusion.39
  62.5 0.8 scatter-add.16
  63.4 1.9 collective-permute-start.6
  65.4 3.9 %collective-permute-start.7 = (f32[2,4,8,256]{3,2,1,0:T(8,128)S(1)}, f32[2,4,8,256]{3,2,1,0:T(8,128)S(1)}, u32[]{:S(2)}, u32[]{:S(2)}) collective-permute-start(f32[2,4,8,256]{3,2,1,0:T(8,128)S(1)} %get-tuple-element.53), channel_id=1, source_target_pairs={{0,1},{1,2},{2,3},{3,4},{4,5},{5,6},{6,7},{7,8},{8,9},{9,10},{10,1... | collective-permute-start | bytes 196616 | tf_op jit(solution)/shard_map/ppermute | solution.py:20
  70.3 8.2 %all-to-all-start = ((bf16[2,32,2,32]{3,2,0,1:T(2,128)(2,1)}), bf16[2,32,2,32]{3,2,0,1:T(2,128)(2,1)S(1)}, u32[]{:S(2)}, u32[]{:S(2)}) async-start(bf16[2,32,2,32]{3,2,0,1:T(2,128)(2,1)} %copy.63), calls=%async_computation | async-start | bytes 65536 | tf_op jit(solution)/shard_map/all_to_all | solution.py:105
  79.4 2.2 fusion.11
  81.7 0.8 scatter-add.19
  82.5 2.3 fusion.106
  86.3 1.3 all-to-all-done
  87.6 21.5 %all_to_all.10 = bf16[2,32,2,2048]{3,2,0,1:T(2,128)(2,1)S(1)} all-to-all(bf16[2,32,2,2048]{3,2,0,1:T(2,128)(2,1)S(1)} %copy.64), channel_id=1, replica_groups=mesh['dir'=32,'tile'=32] {'tile'}, dimensions={1} | all-to-all | bytes 1048576 | tf_op jit(solution)/shard_map/all_to_all | solution.py:104
  109.1 1.5 convolution_bitcast_fusion
  110.6 140.5 %reduce-scatter.4.cloned.1.call-done = f32[64,32]{1,0:T(8,128)} async-done(((f32[2048,32]{1,0:T(8,128)}), f32[64,32]{1,0:T(8,128)}) %reduce-scatter.4.cloned.1.call-update) | async-done | bytes 8208
  251.1 1.4 copy.70
  (48 shorter events, 7.8 us)
Async XLA Ops:
  7.2 38.1 %copy-start = (bf16[64,32,4]{0,2,1:T(4,128)(2,1)S(1)}, bf16[64,32,4]{0,2,1:T(4,128)(2,1)}, u32[]{:S(2)}) copy-start(bf16[64,32,4]{0,2,1:T(4,128)(2,1)} %param.23) | copy-start | bytes 49156
  7.2 22.1 %copy-start.1 = (f32[2,32,8,256]{3,2,1,0:T(8,128)S(1)}, f32[2,32,8,256]{3,2,1,0:T(8,128)}, u32[]{:S(2)}) copy-start(f32[2,32,8,256]{3,2,1,0:T(8,128)} %param.17) | copy-start | bytes 1572868
  8.1 19.2 %collective-permute-start.1 = (f32[2,4,8,256]{3,2,1,0:T(8,128)S(1)}, f32[2,4,8,256]{3,2,1,0:T(8,128)S(1)}, u32[]{:S(2)}, u32[]{:S(2)}) collective-permute-start(f32[2,4,8,256]{3,2,1,0:T(8,128)S(1)} %get-tuple-element.60), channel_id=1, source_target_pairs={{0,1},{1,2},{2,3},{3,4},{4,5},{5,6},{6,7},{7,8},{8,9},{9,10},{10,1... | collective-permute-start | bytes 196616 | tf_op jit(solution)/shard_map/ppermute | solution.py:20
  11.7 17.5 %collective-permute-start = (f32[2,4,8,256]{3,2,1,0:T(8,128)S(1)}, f32[2,4,8,256]{3,2,1,0:T(8,128)S(1)}, u32[]{:S(2)}, u32[]{:S(2)}) collective-permute-start(f32[2,4,8,256]{3,2,1,0:T(8,128)S(1)} %get-tuple-element.61), channel_id=1, source_target_pairs={{1,0},{2,1},{3,2},{4,3},{5,4},{6,5},{7,6},{8,7},{9,8},{10,9},{11,1... | collective-permute-start | bytes 196616 | tf_op jit(solution)/shard_map/ppermute | solution.py:21
  28.4 0.8 copy-start.2
  29.9 8.2 %copy-start.3 = (bf16[2,32,8,256]{3,2,1,0:T(8,128)(2,1)S(1)}, bf16[2,32,8,256]{3,2,1,0:T(8,128)(2,1)}, u32[]{:S(2)}) copy-start(bf16[2,32,8,256]{3,2,1,0:T(8,128)(2,1)} %param.18) | copy-start | bytes 786436
  39.4 6.4 %collective-permute-start.2 = (f32[2,4,8,256]{3,2,1,0:T(8,128)S(1)}, f32[2,4,8,256]{3,2,1,0:T(8,128)S(1)}, u32[]{:S(2)}, u32[]{:S(2)}) collective-permute-start(f32[2,4,8,256]{3,2,1,0:T(8,128)S(1)} %get-tuple-element.56), channel_id=1, source_target_pairs={{1,0},{2,1},{3,2},{4,3},{5,4},{6,5},{7,6},{8,7},{9,8},{10,9},{11,1... | collective-permute-start | bytes 196616 | tf_op jit(solution)/shard_map/ppermute | solution.py:21
  41.3 6.2 %collective-permute-start.3 = (f32[2,4,8,256]{3,2,1,0:T(8,128)S(1)}, f32[2,4,8,256]{3,2,1,0:T(8,128)S(1)}, u32[]{:S(2)}, u32[]{:S(2)}) collective-permute-start(f32[2,4,8,256]{3,2,1,0:T(8,128)S(1)} %get-tuple-element.57), channel_id=1, source_target_pairs={{0,1},{1,2},{2,3},{3,4},{4,5},{5,6},{6,7},{7,8},{8,9},{9,10},{10,1... | collective-permute-start | bytes 196616 | tf_op jit(solution)/shard_map/ppermute | solution.py:20
  51.4 6.2 %collective-permute-start.4 = (f32[2,4,8,256]{3,2,1,0:T(8,128)S(1)}, f32[2,4,8,256]{3,2,1,0:T(8,128)S(1)}, u32[]{:S(2)}, u32[]{:S(2)}) collective-permute-start(f32[2,4,8,256]{3,2,1,0:T(8,128)S(1)} %get-tuple-element.54), channel_id=1, source_target_pairs={{1,0},{2,1},{3,2},{4,3},{5,4},{6,5},{7,6},{8,7},{9,8},{10,9},{11,1... | collective-permute-start | bytes 196616 | tf_op jit(solution)/shard_map/ppermute | solution.py:21
  53.4 6.2 %collective-permute-start.5 = (f32[2,4,8,256]{3,2,1,0:T(8,128)S(1)}, f32[2,4,8,256]{3,2,1,0:T(8,128)S(1)}, u32[]{:S(2)}, u32[]{:S(2)}) collective-permute-start(f32[2,4,8,256]{3,2,1,0:T(8,128)S(1)} %get-tuple-element.55), channel_id=1, source_target_pairs={{0,1},{1,2},{2,3},{3,4},{4,5},{5,6},{6,7},{7,8},{8,9},{9,10},{10,1... | collective-permute-start | bytes 196616 | tf_op jit(solution)/shard_map/ppermute | solution.py:20
  63.4 15.3 %collective-permute-start.6 = (f32[2,4,8,256]{3,2,1,0:T(8,128)S(1)}, f32[2,4,8,256]{3,2,1,0:T(8,128)S(1)}, u32[]{:S(2)}, u32[]{:S(2)}) collective-permute-start(f32[2,4,8,256]{3,2,1,0:T(8,128)S(1)} %get-tuple-element.52), channel_id=1, source_target_pairs={{1,0},{2,1},{3,2},{4,3},{5,4},{6,5},{7,6},{8,7},{9,8},{10,9},{11,1... | collective-permute-start | bytes 196616 | tf_op jit(solution)/shard_map/ppermute | solution.py:21
  65.4 13.4 %collective-permute-start.7 = (f32[2,4,8,256]{3,2,1,0:T(8,128)S(1)}, f32[2,4,8,256]{3,2,1,0:T(8,128)S(1)}, u32[]{:S(2)}, u32[]{:S(2)}) collective-permute-start(f32[2,4,8,256]{3,2,1,0:T(8,128)S(1)} %get-tuple-element.53), channel_id=1, source_target_pairs={{0,1},{1,2},{2,3},{3,4},{4,5},{5,6},{6,7},{7,8},{8,9},{9,10},{10,1... | collective-permute-start | bytes 196616 | tf_op jit(solution)/shard_map/ppermute | solution.py:20
  70.3 17.3 %all-to-all-start = ((bf16[2,32,2,32]{3,2,0,1:T(2,128)(2,1)}), bf16[2,32,2,32]{3,2,0,1:T(2,128)(2,1)S(1)}, u32[]{:S(2)}, u32[]{:S(2)}) async-start(bf16[2,32,2,32]{3,2,0,1:T(2,128)(2,1)} %copy.63), calls=%async_computation | async-start | bytes 65536 | tf_op jit(solution)/shard_map/all_to_all | solution.py:105
  78.5 172.6 %reduce-scatter.4.cloned.1.call-start = ((), (), s32[]{:S(2)}) async-start(), calls=%async_computation.3 | async-start | bytes 1081344
Sparse Core Ops, SparseCore 0:
  110.7 140.3 reduce-scatter.3
where the time goes:
time: 260 us; the launch traced here: 259 us
  waiting for transfers between devices  146 us (56%)
  starting transfers between devices  42.2 us (16%)
  blocking collectives  21.5 us (8%)
  other arithmetic  19.6 us (8%)
  between operations  14.4 us (6%)
  local copies, waits for them, and re-layouts  13.7 us (5%)
    unnamed x2, waiting for transfers between devices  141 us
    all_to_all x1, blocking collectives, per_device(): lax.all_to_all(send_rows, 'tile', split_axis=1, concat_axis=1, tiled=True)  21.5 us
    ppermute x4, starting transfers between devices, with_halo(): after = lax.ppermute(leading, axis, down)  18.3 us
    ppermute x4, starting transfers between devices, with_halo(): before = lax.ppermute(last, axis, up)  15.4 us
    add x4, other arithmetic, laplace(): result + stencil_coef[reach] * (plus_x + minus_x + plus_z + minus_z + plu...  11.5 us
    all_to_all x1, starting transfers between devices, per_device(): lax.all_to_all(band_cols, 'tile', split_axis=1, concat_axis=1, tiled=True)  8.23 us
  transfers between devices with their start and end apart: 10, of which 6 were waited for; matrix products, arithmetic and copies ran while one was open for 5% of the time, Pallas kernels for 0%

commit v1 on v0

--- a/solution.py
+++ b/solution.py
@@ -39,33 +39,16 @@
     return result
 
 
-def build_slots(owner_col, start_col, weight_col, n_tiles, capacity, rows_here):
-    hits = (owner_col[:, :, None] == jnp.arange(n_tiles, dtype=jnp.int32)[None, None, :]).astype(
-        jnp.int32
-    )
-    before = jnp.cumsum(hits, axis=1) - hits
-    rank_row = jnp.sum(before * hits, axis=2)
-    slot_row = owner_col * capacity + rank_row
-    selector = (
-        slot_row[:, None, :] == jnp.arange(n_tiles * capacity, dtype=jnp.int32)[None, :, None]
-    ).astype(jnp.bfloat16)
-    positions = start_col[:, :, None] + jnp.arange(BAND, dtype=jnp.int32)[None, None, :]
-    placed = (positions[..., None] == jnp.arange(rows_here, dtype=jnp.int32)).astype(jnp.float32)
-    band_rows = jnp.sum(weight_col.astype(jnp.float32)[..., None] * placed, axis=2).astype(
-        jnp.bfloat16
-    )
-    band_cols = jnp.einsum(
-        "ksr,krc->ksc", selector, band_rows, preferred_element_type=jnp.float32
-    ).astype(jnp.bfloat16)
-    return (selector, band_cols)
-
-
-def apply_band(got_rows, got_cols, rows_here):
-    flat_rows = got_rows.reshape(-1, got_rows.shape[-1])
-    flat_cols = got_cols.reshape(-1, rows_here)
-    return lax.dot_general(
-        flat_cols, flat_rows, (((0,), (0,)), ((), ())), preferred_element_type=jnp.float32
-    )
+def band_matrix(owner, start, weight, n_tiles, n_rows):
+    first = owner * n_rows + start
+    place = jnp.arange(n_tiles * n_rows, dtype=jnp.int32)
+    diff = place[None, None, :] - first[:, :, None]
+    wide = weight.astype(jnp.bfloat16)
+    zero = jnp.zeros((), jnp.bfloat16)
+    out = jnp.where(diff == 0, wide[:, :, 0:1], zero)
+    for k in range(1, BAND):
+        out = jnp.where(diff == k, wide[:, :, k : k + 1], out)
+    return out
 
 
 def per_device(
@@ -85,27 +68,22 @@
         image_sum = image_sum + source_snaps[step].astype(jnp.float32) * field_new
         field_old, field_now = (field_now, field_new)
     image_flat = image_sum.astype(jnp.bfloat16).reshape(local_dirs, rows_here, depth * across)
+    n_dir = lax.axis_size("dir")
     n_tiles = lax.axis_size("tile")
-    capacity = max(2, 2 * rows_here // n_tiles)
-    owner_all = row_owner[:, :, 0]
-    first_dir = lax.axis_index("dir") * local_dirs
-    owner_here = lax.dynamic_slice_in_dim(owner_all, first_dir, local_dirs, 0)
-    start_here = lax.dynamic_slice_in_dim(band_start, first_dir, local_dirs, 0)
-    weight_here = lax.dynamic_slice_in_dim(band_weight, first_dir, local_dirs, 0)
-    selector, band_cols = build_slots(
-        owner_here, start_here, weight_here, n_tiles, capacity, rows_here
+    cols = depth * across // n_dir
+    blocks = image_flat.reshape(local_dirs, rows_here, n_dir, cols)
+    got = lax.all_to_all(blocks, "dir", split_axis=2, concat_axis=0, tiled=True)
+    all_dirs = got.shape[0]
+    got = got.reshape(all_dirs * rows_here, cols)
+    owner = row_owner[:, :, 0]
+    mt = band_matrix(owner, band_start, band_weight, n_tiles, rows_here)
+    mt = mt.reshape(all_dirs * rows_here, n_tiles * rows_here)
+    partial = lax.dot_general(
+        mt, got, (((0,), (0,)), ((), ())), preferred_element_type=jnp.float32
     )
-    send_rows = jnp.einsum(
-        "ksr,krp->ksp", selector, image_flat, preferred_element_type=jnp.float32
-    ).astype(jnp.bfloat16)
-    send_rows = send_rows.reshape(local_dirs, n_tiles, capacity, depth * across)
-    band_cols = band_cols.reshape(local_dirs, n_tiles, capacity, rows_here)
-    got_rows, got_cols = (
-        lax.all_to_all(send_rows, "tile", split_axis=1, concat_axis=1, tiled=True),
-        lax.all_to_all(band_cols, "tile", split_axis=1, concat_axis=1, tiled=True),
-    )
-    partial_img = apply_band(got_rows, got_cols, rows_here)
-    stack = lax.psum_scatter(partial_img, "dir", scatter_dimension=1, tiled=True)
+    partial = partial.reshape(n_tiles, rows_here, cols)
+    sent = lax.all_to_all(partial, "tile", split_axis=0, concat_axis=0, tiled=True)
+    stack = jnp.sum(sent, axis=0)
     return (field_now, stack)
 
 

time: 260 us -> 133 us (0.51)
  waiting for transfers between devices: 146 us -> 20.2 us
  between operations: 14.4 us -> 1 us
  blocking collectives: 21.5 us -> 27.1 us
  starting transfers between devices: 42.2 us -> 47.2 us
    unnamed x2 -> x0, waiting for transfers between devices: 141 us -> none
    all_to_all x1, waiting for transfers between devices: 1.31 us -> 12.8 us  [per_device(): got = lax.all_to_all(blocks, 'dir', split_axis=2, concat_axis=0, tiled=True)]
    all_to_all x1, blocking collectives: 21.5 us -> 27.1 us  [per_device(): lax.all_to_all(partial, 'tile', split_axis=0, concat_axis=0, tiled=True)]
    all_to_all x1, starting transfers between devices: 8.23 us -> 13.3 us  [per_device(): got = lax.all_to_all(blocks, 'dir', split_axis=2, concat_axis=0, tiled=True)]
    ppermute x4, waiting for transfers between devices: 3.58 us -> 6.26 us  [with_halo(): before = lax.ppermute(last, axis, up)]
  transfers between devices with their start and end apart: 10 -> 9, of which waited for: 6 -> 7; matrix products, arithmetic and copies ran while one was open for 5% -> 3% of each run, Pallas kernels for 0% -> 0%
where the time goes in v1:
time: 133 us; the launch traced here: 132 us
  starting transfers between devices  47.2 us (35%)
  blocking collectives  27.1 us (20%)
  other arithmetic  20.9 us (16%)
  waiting for transfers between devices  20.2 us (15%)
  local copies, waits for them, and re-layouts  13.1 us (10%)
  matrix products  2.76 us (2%)
    all_to_all x1, blocking collectives, per_device(): lax.all_to_all(partial, 'tile', split_axis=0, concat_axis=0, tiled=True)  27.1 us
    ppermute x4, starting transfers between devices, with_halo(): after = lax.ppermute(leading, axis, down)  19.2 us
    ppermute x4, starting transfers between devices, with_halo(): before = lax.ppermute(last, axis, up)  14.7 us
    all_to_all x1, starting transfers between devices, per_device(): got = lax.all_to_all(blocks, 'dir', split_axis=2, concat_axis=0, tiled=True)  13.3 us
    all_to_all x1, waiting for transfers between devices, per_device(): got = lax.all_to_all(blocks, 'dir', split_axis=2, concat_axis=0, tiled=True)  12.8 us
    add x4, other arithmetic, laplace(): result + stencil_coef[reach] * (plus_x + minus_x + plus_z + minus_z + plu...  11.4 us
    ppermute x4, waiting for transfers between devices, with_halo(): before = lax.ppermute(last, axis, up)  6.26 us
    scatter-add x4, local copies, waits for them, and re-layouts, per_device(): curvature = curvature.at[:, :, 0, :].add(recorded[step].astype(jnp.float32))  4.78 us
  transfers between devices with their start and end apart: 9, of which 7 were waited for; matrix products, arithmetic and copies ran while one was open for 3% of the time, Pallas kernels for 0%

profile of v1, /device:TPU:16, one launch (start us, length us, event | category | flops | bytes accessed | tf_op | source)
XLA Modules:
  0.0 132.2 jit_solution(1136376545859582370)
XLA Ops:
  0.6 0.9 fusion.133
  1.6 3.6 %collective-permute-start.1 = (f32[2,4,8,256]{3,2,1,0:T(8,128)S(1)}, f32[2,4,8,256]{3,2,1,0:T(8,128)S(1)}, u32[]{:S(2)}, u32[]{:S(2)}) collective-permute-start(f32[2,4,8,256]{3,2,1,0:T(8,128)S(1)} %get-tuple-element.60), channel_id=1, source_target_pairs={{0,1},{1,2},{2,3},{3,4},{4,5},{5,6},{6,7},{7,8},{8,9},{9,10},{10,1... | collective-permute-start | bytes 196616 | tf_op jit(solution)/shard_map/ppermute | solution.py:20
  5.2 12.6 %collective-permute-start = (f32[2,4,8,256]{3,2,1,0:T(8,128)S(1)}, f32[2,4,8,256]{3,2,1,0:T(8,128)S(1)}, u32[]{:S(2)}, u32[]{:S(2)}) collective-permute-start(f32[2,4,8,256]{3,2,1,0:T(8,128)S(1)} %get-tuple-element.61), channel_id=1, source_target_pairs={{1,0},{2,1},{3,2},{4,3},{5,4},{6,5},{7,6},{8,7},{9,8},{10,9},{11,1... | collective-permute-start | bytes 196616 | tf_op jit(solution)/shard_map/ppermute | solution.py:21
  17.8 0.8 fusion.134
  19.2 1.9 %constant_dynamic-update-slice_fusion.1 = (f32[2,36,8,256]{3,2,1,0:T(8,128)S(1)}, f32[2,36,8,256]{3,2,1,0:T(8,128)}) fusion(f32[2,32,8,256]{3,2,1,0:T(8,128)} %param.17, f32[2,36,8,256]{3,2,1,0:T(8,128)} %constant_dynamic-update-slice_fusion.3), kind=kLoop, calls=%fused_computation.232 | loop fusion | bytes 1572864
  21.8 4.6 %fusion.109 = f32[2,32,8,256]{3,2,1,0:T(8,128)} fusion(f32[2,40,16,264]{3,2,1,0:T(8,128)S(1)} %select_maximum_fusion.6, f32[2,36,8,256]{3,2,1,0:T(8,128)} %get-tuple-element.59, f32[2,36,8,256]{3,2,1,0:T(8,128)S(1)} %constant_dynamic-update-slice_fusion, f32[2,32,8,256]{3,2,1,0:T(8,128)S(1)} %copy-done), kind=kLoop, calls=%fused_computation.183 | loop fusion | flops 3801088 | bytes 13631488 | tf_op jit(solution)/shard_map/add | solution.py:36
  26.5 1.1 slice_add_fusion.35
  27.6 2.3 %scatter-add.14 = f32[2,32,8,256]{3,2,1,0:T(8,128)} dynamic-update-slice(f32[2,32,8,256]{3,2,1,0:T(8,128)} %fusion.109, f32[2,32,1,256]{3,2,1,0:T(1,128)S(1)} %slice_add_fusion.35, s32[]{:T(128)} %constant.109.clone.1, s32[]{:T(128)} %constant.109.clone.1, s32[]{:T(128)} %constant.109.clone.1, s32[]{:T(128)} %constant.109.clone.1) | dynamic-update-slice | bytes 131076 | tf_op jit(solution)/shard_map/scatter-add | solution.py:66
  29.9 1.3 fusion.98
  31.2 2.8 %collective-permute-start.2 = (f32[2,4,8,256]{3,2,1,0:T(8,128)S(1)}, f32[2,4,8,256]{3,2,1,0:T(8,128)S(1)}, u32[]{:S(2)}, u32[]{:S(2)}) collective-permute-start(f32[2,4,8,256]{3,2,1,0:T(8,128)S(1)} %get-tuple-element.56), channel_id=1, source_target_pairs={{1,0},{2,1},{3,2},{4,3},{5,4},{6,5},{7,6},{8,7},{9,8},{10,9},{11,1... | collective-permute-start | bytes 196616 | tf_op jit(solution)/shard_map/ppermute | solution.py:21
  34.0 3.1 %collective-permute-start.3 = (f32[2,4,8,256]{3,2,1,0:T(8,128)S(1)}, f32[2,4,8,256]{3,2,1,0:T(8,128)S(1)}, u32[]{:S(2)}, u32[]{:S(2)}) collective-permute-start(f32[2,4,8,256]{3,2,1,0:T(8,128)S(1)} %get-tuple-element.57), channel_id=1, source_target_pairs={{0,1},{1,2},{2,3},{3,4},{4,5},{5,6},{6,7},{7,8},{8,9},{9,10},{10,1... | collective-permute-start | bytes 196616 | tf_op jit(solution)/shard_map/ppermute | solution.py:20
  37.7 2.5 %collective-permute-done.3 = f32[2,4,8,256]{3,2,1,0:T(8,128)S(1)} collective-permute-done((f32[2,4,8,256]{3,2,1,0:T(8,128)S(1)}, f32[2,4,8,256]{3,2,1,0:T(8,128)S(1)}, u32[]{:S(2)}, u32[]{:S(2)}) %collective-permute-start.3) | collective-permute-done | bytes 65568 | tf_op jit(solution)/shard_map/ppermute | solution.py:20
  40.8 2.2 %fusion.78 = f32[2,32,8,256]{3,2,1,0:T(8,128)S(1)} fusion(f32[2,32,8,256]{3,2,1,0:T(8,128)S(1)} %fusion.98, f32[2,4,8,256]{3,2,1,0:T(8,128)S(1)} %collective-permute-done.3, f32[2,4,8,256]{3,2,1,0:T(8,128)S(1)} %collective-permute-done.2, f32[2,40,16,264]{3,2,1,0:T(8,128)S(1)} %select_maximum_fusion.4), kind=kLoop, calls=%fused_computation.133 | loop fusion | flops 4849664 | bytes 9568256 | tf_op jit(solution)/shard_map/add | solution.py:36
  43.1 0.8 scatter-add.15
  44.1 1.9 %collective-permute-start.4 = (f32[2,4,8,256]{3,2,1,0:T(8,128)S(1)}, f32[2,4,8,256]{3,2,1,0:T(8,128)S(1)}, u32[]{:S(2)}, u32[]{:S(2)}) collective-permute-start(f32[2,4,8,256]{3,2,1,0:T(8,128)S(1)} %get-tuple-element.54), channel_id=1, source_target_pairs={{1,0},{2,1},{3,2},{4,3},{5,4},{6,5},{7,6},{8,7},{9,8},{10,9},{11,1... | collective-permute-start | bytes 196616 | tf_op jit(solution)/shard_map/ppermute | solution.py:21
  46.0 3.9 %collective-permute-start.5 = (f32[2,4,8,256]{3,2,1,0:T(8,128)S(1)}, f32[2,4,8,256]{3,2,1,0:T(8,128)S(1)}, u32[]{:S(2)}, u32[]{:S(2)}) collective-permute-start(f32[2,4,8,256]{3,2,1,0:T(8,128)S(1)} %get-tuple-element.55), channel_id=1, source_target_pairs={{0,1},{1,2},{2,3},{3,4},{4,5},{5,6},{6,7},{7,8},{8,9},{9,10},{10,1... | collective-permute-start | bytes 196616 | tf_op jit(solution)/shard_map/ppermute | solution.py:20
  50.3 1.9 %collective-permute-done.5 = f32[2,4,8,256]{3,2,1,0:T(8,128)S(1)} collective-permute-done((f32[2,4,8,256]{3,2,1,0:T(8,128)S(1)}, f32[2,4,8,256]{3,2,1,0:T(8,128)S(1)}, u32[]{:S(2)}, u32[]{:S(2)}) %collective-permute-start.5) | collective-permute-done | bytes 65568 | tf_op jit(solution)/shard_map/ppermute | solution.py:20
  52.8 2.2 %fusion.50 = f32[2,32,8,256]{3,2,1,0:T(8,128)S(1)} fusion(f32[2,32,8,256]{3,2,1,0:T(8,128)S(1)} %fusion.99, f32[2,4,8,256]{3,2,1,0:T(8,128)S(1)} %collective-permute-done.5, f32[2,4,8,256]{3,2,1,0:T(8,128)S(1)} %collective-permute-done.4, f32[2,40,16,264]{3,2,1,0:T(8,128)S(1)} %select_maximum_fusion.2), kind=kLoop, calls=%fused_computation.105 | loop fusion | flops 4849664 | bytes 9568256 | tf_op jit(solution)/shard_map/add | solution.py:36
  55.1 0.8 scatter-add.16
  56.1 1.9 %collective-permute-start.6 = (f32[2,4,8,256]{3,2,1,0:T(8,128)S(1)}, f32[2,4,8,256]{3,2,1,0:T(8,128)S(1)}, u32[]{:S(2)}, u32[]{:S(2)}) collective-permute-start(f32[2,4,8,256]{3,2,1,0:T(8,128)S(1)} %get-tuple-element.52), channel_id=1, source_target_pairs={{1,0},{2,1},{3,2},{4,3},{5,4},{6,5},{7,6},{8,7},{9,8},{10,9},{11,1... | collective-permute-start | bytes 196616 | tf_op jit(solution)/shard_map/ppermute | solution.py:21
  58.0 4.1 %collective-permute-start.7 = (f32[2,4,8,256]{3,2,1,0:T(8,128)S(1)}, f32[2,4,8,256]{3,2,1,0:T(8,128)S(1)}, u32[]{:S(2)}, u32[]{:S(2)}) collective-permute-start(f32[2,4,8,256]{3,2,1,0:T(8,128)S(1)} %get-tuple-element.53), channel_id=1, source_target_pairs={{0,1},{1,2},{2,3},{3,4},{4,5},{5,6},{6,7},{7,8},{8,9},{9,10},{10,1... | collective-permute-start | bytes 196616 | tf_op jit(solution)/shard_map/ppermute | solution.py:20
  62.3 1.9 %collective-permute-done.7 = f32[2,4,8,256]{3,2,1,0:T(8,128)S(1)} collective-permute-done((f32[2,4,8,256]{3,2,1,0:T(8,128)S(1)}, f32[2,4,8,256]{3,2,1,0:T(8,128)S(1)}, u32[]{:S(2)}, u32[]{:S(2)}) %collective-permute-start.7) | collective-permute-done | bytes 65568 | tf_op jit(solution)/shard_map/ppermute | solution.py:20
  64.8 2.2 %fusion.22 = f32[2,32,8,256]{3,2,1,0:T(8,128)S(1)} fusion(f32[2,32,8,256]{3,2,1,0:T(8,128)S(1)} %fusion.100, f32[2,4,8,256]{3,2,1,0:T(8,128)S(1)} %collective-permute-done.7, f32[2,4,8,256]{3,2,1,0:T(8,128)S(1)} %collective-permute-done.6, f32[2,40,16,264]{3,2,1,0:T(8,128)S(1)} %select_maximum_fusion), kind=kLoop, calls=%fused_computation.77 | loop fusion | flops 4849664 | bytes 9568256 | tf_op jit(solution)/shard_map/add | solution.py:36
  67.1 0.8 scatter-add.19
  68.0 2.3 %fusion.117 = (bf16[2,32,8,256]{3,2,1,0:T(8,128)(2,1)S(1)}, f32[2,32,8,256]{3,2,1,0:T(8,128)}) fusion(f32[2,32,8,256]{3,2,1,0:T(8,128)S(1)} %fusion.100, f32[2,32,8,256]{3,2,1,0:T(8,128)S(1)} %fusion.99, f32[2,32,8,256]{3,2,1,0:T(8,128)S(1)} %fusion.98, bf16[4,2,32,8,256]{4,3,2,1,0:T(8,128)(2,1)} %param.19, f32[2,32,8,256]{3,2,1,0:T(8,128)S(1)} %scatter-add.19, ...), kind=kLoop, calls=%fused_computation.211 | loop fusion | flops 2228224 | bytes 4194304 | tf_op jit(solution)/shard_map/convert_element_type | solution.py:70
  70.7 1.1 reshape.255
  71.8 13.3 %all-to-all-start = ((bf16[32,2,2048]{2,1,0:T(2,128)(2,1)}), bf16[32,2,2048]{2,1,0:T(2,128)(2,1)S(1)}, u32[]{:S(2)}, u32[]{:S(2)}) async-start(bf16[32,2,2048]{2,1,0:T(2,128)(2,1)} %reshape.255), calls=%async_computation | async-start | bytes 524288 | tf_op jit(solution)/shard_map/all_to_all | solution.py:75
  86.1 12.8 %all-to-all-done = bf16[32,2,2048]{2,1,0:T(2,128)(2,1)S(1)} async-done(((bf16[32,2,2048]{2,1,0:T(2,128)(2,1)}), bf16[32,2,2048]{2,1,0:T(2,128)(2,1)S(1)}, u32[]{:S(2)}, u32[]{:S(2)}) %all-to-all-start) | async-done | bytes 262176 | tf_op jit(solution)/shard_map/all_to_all | solution.py:75
  99.3 2.8 %fusion.4 = f32[32,32,64]{2,1,0:T(8,128)S(1)} fusion(bf16[2048,64,1]{1,0,2:T(8,128)(2,1)S(1)} %bitcast.66, s32[2048]{0:T(1024)S(1)} %sub.54, s32[32,32]{1,0:T(8,128)S(1)} %multiply_add_fusion, bf16[2048]{0:T(1024)(128)(2,1)S(1)} %broadcast_in_dim.46, bf16[2048]{0:T(1024)(128)(2,1)S(1)} %broadcast_in_dim.44, bf16[2048]{0:T(1024)(128)(2,1)S(1)} %broadcast_in_dim.42, ...), kind=kOutput, calls=%fused_computation.8 | convolution fusion | flops 287309824 | bytes 552960 | tf_op jit(solution)/shard_map/dot_general | solution.py:81
  102.4 27.1 %all_to_all.20 = f32[32,1,2048]{2,1,0:T(1,128)S(1)} all-to-all(f32[32,1,2048]{2,1,0:T(1,128)S(1)} %reshape.257), channel_id=1, replica_groups=mesh['dir'=32,'tile'=32] {'tile'}, dimensions={0} | all-to-all | bytes 524288 | tf_op jit(solution)/shard_map/all_to_all | solution.py:85
  130.0 1.3 reduce.8
  131.5 0.7 reduce_sum.9
  (48 shorter events, 7.5 us)
Async XLA Ops:
  0.6 20.6 %copy-start = (f32[2,32,8,256]{3,2,1,0:T(8,128)S(1)}, f32[2,32,8,256]{3,2,1,0:T(8,128)}, u32[]{:S(2)}) copy-start(f32[2,32,8,256]{3,2,1,0:T(8,128)} %param.17) | copy-start | bytes 1572868
  1.6 17.0 %collective-permute-start.1 = (f32[2,4,8,256]{3,2,1,0:T(8,128)S(1)}, f32[2,4,8,256]{3,2,1,0:T(8,128)S(1)}, u32[]{:S(2)}, u32[]{:S(2)}) collective-permute-start(f32[2,4,8,256]{3,2,1,0:T(8,128)S(1)} %get-tuple-element.60), channel_id=1, source_target_pairs={{0,1},{1,2},{2,3},{3,4},{4,5},{5,6},{6,7},{7,8},{8,9},{9,10},{10,1... | collective-permute-start | bytes 196616 | tf_op jit(solution)/shard_map/ppermute | solution.py:20
  5.2 16.0 %collective-permute-start = (f32[2,4,8,256]{3,2,1,0:T(8,128)S(1)}, f32[2,4,8,256]{3,2,1,0:T(8,128)S(1)}, u32[]{:S(2)}, u32[]{:S(2)}) collective-permute-start(f32[2,4,8,256]{3,2,1,0:T(8,128)S(1)} %get-tuple-element.61), channel_id=1, source_target_pairs={{1,0},{2,1},{3,2},{4,3},{5,4},{6,5},{7,6},{8,7},{9,8},{10,9},{11,1... | collective-permute-start | bytes 196616 | tf_op jit(solution)/shard_map/ppermute | solution.py:21
  21.8 8.1 %copy-start.1 = (bf16[2,32,8,256]{3,2,1,0:T(8,128)(2,1)S(1)}, bf16[2,32,8,256]{3,2,1,0:T(8,128)(2,1)}, u32[]{:S(2)}) copy-start(bf16[2,32,8,256]{3,2,1,0:T(8,128)(2,1)} %param.18) | copy-start | bytes 786436
  31.2 6.5 %collective-permute-start.2 = (f32[2,4,8,256]{3,2,1,0:T(8,128)S(1)}, f32[2,4,8,256]{3,2,1,0:T(8,128)S(1)}, u32[]{:S(2)}, u32[]{:S(2)}) collective-permute-start(f32[2,4,8,256]{3,2,1,0:T(8,128)S(1)} %get-tuple-element.56), channel_id=1, source_target_pairs={{1,0},{2,1},{3,2},{4,3},{5,4},{6,5},{7,6},{8,7},{9,8},{10,9},{11,1... | collective-permute-start | bytes 196616 | tf_op jit(solution)/shard_map/ppermute | solution.py:21
  34.0 6.2 %collective-permute-start.3 = (f32[2,4,8,256]{3,2,1,0:T(8,128)S(1)}, f32[2,4,8,256]{3,2,1,0:T(8,128)S(1)}, u32[]{:S(2)}, u32[]{:S(2)}) collective-permute-start(f32[2,4,8,256]{3,2,1,0:T(8,128)S(1)} %get-tuple-element.57), channel_id=1, source_target_pairs={{0,1},{1,2},{2,3},{3,4},{4,5},{5,6},{6,7},{7,8},{8,9},{9,10},{10,1... | collective-permute-start | bytes 196616 | tf_op jit(solution)/shard_map/ppermute | solution.py:20
  44.1 6.2 %collective-permute-start.4 = (f32[2,4,8,256]{3,2,1,0:T(8,128)S(1)}, f32[2,4,8,256]{3,2,1,0:T(8,128)S(1)}, u32[]{:S(2)}, u32[]{:S(2)}) collective-permute-start(f32[2,4,8,256]{3,2,1,0:T(8,128)S(1)} %get-tuple-element.54), channel_id=1, source_target_pairs={{1,0},{2,1},{3,2},{4,3},{5,4},{6,5},{7,6},{8,7},{9,8},{10,9},{11,1... | collective-permute-start | bytes 196616 | tf_op jit(solution)/shard_map/ppermute | solution.py:21
  46.0 6.2 %collective-permute-start.5 = (f32[2,4,8,256]{3,2,1,0:T(8,128)S(1)}, f32[2,4,8,256]{3,2,1,0:T(8,128)S(1)}, u32[]{:S(2)}, u32[]{:S(2)}) collective-permute-start(f32[2,4,8,256]{3,2,1,0:T(8,128)S(1)} %get-tuple-element.55), channel_id=1, source_target_pairs={{0,1},{1,2},{2,3},{3,4},{4,5},{5,6},{6,7},{7,8},{8,9},{9,10},{10,1... | collective-permute-start | bytes 196616 | tf_op jit(solution)/shard_map/ppermute | solution.py:20
  56.1 6.2 %collective-permute-start.6 = (f32[2,4,8,256]{3,2,1,0:T(8,128)S(1)}, f32[2,4,8,256]{3,2,1,0:T(8,128)S(1)}, u32[]{:S(2)}, u32[]{:S(2)}) collective-permute-start(f32[2,4,8,256]{3,2,1,0:T(8,128)S(1)} %get-tuple-element.52), channel_id=1, source_target_pairs={{1,0},{2,1},{3,2},{4,3},{5,4},{6,5},{7,6},{8,7},{9,8},{10,9},{11,1... | collective-permute-start | bytes 196616 | tf_op jit(solution)/shard_map/ppermute | solution.py:21
  58.0 6.2 %collective-permute-start.7 = (f32[2,4,8,256]{3,2,1,0:T(8,128)S(1)}, f32[2,4,8,256]{3,2,1,0:T(8,128)S(1)}, u32[]{:S(2)}, u32[]{:S(2)}) collective-permute-start(f32[2,4,8,256]{3,2,1,0:T(8,128)S(1)} %get-tuple-element.53), channel_id=1, source_target_pairs={{0,1},{1,2},{2,3},{3,4},{4,5},{5,6},{6,7},{7,8},{8,9},{9,10},{10,1... | collective-permute-start | bytes 196616 | tf_op jit(solution)/shard_map/ppermute | solution.py:20
  70.2 14.8 %copy-start.2 = (bf16[64,32,4]{0,2,1:T(4,128)(2,1)S(1)}, bf16[64,32,4]{0,2,1:T(4,128)(2,1)}, u32[]{:S(2)}) copy-start(bf16[64,32,4]{0,2,1:T(4,128)(2,1)} %param.23) | copy-start | bytes 49156
  70.2 15.7 %copy-start.3 = (s32[64,32]{0,1:T(8,128)S(1)}, s32[64,32]{0,1:T(8,128)}, u32[]{:S(2)}) copy-start(s32[64,32]{0,1:T(8,128)} %param.22) | copy-start | bytes 24580
  70.2 15.7 %copy-start.4 = (s32[64,32,1]{0,2,1:T(1,128)S(1)}, s32[64,32,1]{0,2,1:T(1,128)}, u32[]{:S(2)}) copy-start(s32[64,32,1]{0,2,1:T(1,128)} %param.21) | copy-start | bytes 24580
  71.8 27.1 %all-to-all-start = ((bf16[32,2,2048]{2,1,0:T(2,128)(2,1)}), bf16[32,2,2048]{2,1,0:T(2,128)(2,1)S(1)}, u32[]{:S(2)}, u32[]{:S(2)}) async-start(bf16[32,2,2048]{2,1,0:T(2,128)(2,1)} %reshape.255), calls=%async_computation | async-start | bytes 524288 | tf_op jit(solution)/shard_map/all_to_all | solution.py:75

commit v2 on v1

--- a/solution.py
+++ b/solution.py
@@ -8,19 +8,6 @@
 
 
 stencil_coef = (-205.0 / 72.0, 8.0 / 5.0, -1.0 / 5.0, 8.0 / 315.0, -1.0 / 560.0)
-
-
-def with_halo(value, sides, width):
-    for axis, dim in sides:
-        count, length = (lax.axis_size(axis), value.shape[dim])
-        up = [(i, (i + 1) % count) for i in range(count - 1)]
-        down = [(j, i) for i, j in up]
-        last = lax.slice_in_dim(value, length - width, length, axis=dim)
-        leading = lax.slice_in_dim(value, 0, width, axis=dim)
-        before = lax.ppermute(last, axis, up)
-        after = lax.ppermute(leading, axis, down)
-        value = jnp.concatenate([before, value, after], axis=dim)
-    return value
 
 
 def laplace(padded_all, rows_here, depth, across):
@@ -51,21 +38,68 @@
     return out
 
 
+def exchange_halo(parts):
+    count = lax.axis_size("tile")
+    up = [(i, i + 1) for i in range(count - 1)]
+    down = [(j, i) for i, j in up]
+    tails = jnp.concatenate([lax.slice_in_dim(p, p.shape[d] - w, p.shape[d], axis=d).reshape(-1) for p, d, w in parts])
+    heads = jnp.concatenate([lax.slice_in_dim(p, 0, w, axis=d).reshape(-1) for p, d, w in parts])
+    before = lax.ppermute(tails, "tile", up)
+    after = lax.ppermute(heads, "tile", down)
+    return before, after
+
+
+def unpack(flat, parts):
+    out = []
+    offset = 0
+    for p, d, w in parts:
+        shape = list(p.shape)
+        shape[d] = w
+        size = 1
+        for n in shape:
+            size *= n
+        out.append(flat[offset : offset + size].reshape(shape))
+        offset += size
+    return out
+
+
 def per_device(
     receiver_old, receiver_now, courant, source_snaps, recorded, row_owner, band_start, band_weight
 ):
     local_dirs, rows_here, depth, across = receiver_now.shape
-    speed_wide = courant.astype(jnp.float32)
-    field_old = receiver_old
-    field_now = receiver_now
-    image_sum = jnp.zeros(field_now.shape, jnp.float32)
+    reach = 4
+    halo = reach * STEPS
+    wide_parts = [(receiver_now, 1, halo), (receiver_old, 1, halo - reach)]
+    narrow_parts = [(courant, 1, halo - reach), (recorded, 2, halo - reach)]
+    wide_before, wide_after = exchange_halo(wide_parts)
+    narrow_before, narrow_after = exchange_halo(narrow_parts)
+    now_b, old_b = unpack(wide_before, wide_parts)
+    now_a, old_a = unpack(wide_after, wide_parts)
+    c_b, rec_b = unpack(narrow_before, narrow_parts)
+    c_a, rec_a = unpack(narrow_after, narrow_parts)
+    field_now = jnp.concatenate([now_b, receiver_now, now_a], axis=1)
+    field_old = jnp.concatenate([old_b, receiver_old, old_a], axis=1)
+    speed_wide = jnp.concatenate([c_b, courant, c_a], axis=1).astype(jnp.float32)
+    rec_wide = jnp.concatenate([rec_b, recorded, rec_a], axis=2).astype(jnp.float32)
+    plane = lax.broadcasted_iota(jnp.int32, (1, 1, depth, 1), 2)
+    image_sum = jnp.zeros(receiver_now.shape, jnp.float32)
     for step in range(STEPS):
-        padded_x = with_halo(field_now, (("tile", 1),), 4)
-        padded_all = jnp.pad(padded_x, ((0, 0), (0, 0), (4, 4), (4, 4)))
-        curvature = laplace(padded_all, rows_here, depth, across)
-        curvature = curvature.at[:, :, 0, :].add(recorded[step].astype(jnp.float32))
-        field_new = 2.0 * field_now - field_old + speed_wide * curvature
-        image_sum = image_sum + source_snaps[step].astype(jnp.float32) * field_new
+        ext_in = halo - reach * step
+        ext_out = ext_in - reach
+        rows_out = rows_here + 2 * ext_out
+        lo = (halo - reach) - ext_out
+        padded_all = jnp.pad(field_now, ((0, 0), (0, 0), (4, 4), (4, 4)))
+        curvature = laplace(padded_all, rows_out, depth, across)
+        inject = rec_wide[step][:, lo : lo + rows_out, None, :]
+        curvature = curvature + jnp.where(plane == 0, inject, 0.0)
+        now_mid = field_now[:, reach : reach + rows_out]
+        old_off = field_old.shape[1] // 2 - rows_out // 2
+        old_mid = field_old[:, old_off : old_off + rows_out]
+        speed_mid = speed_wide[:, lo : lo + rows_out]
+        field_new = 2.0 * now_mid - old_mid + speed_mid * curvature
+        image_sum = image_sum + source_snaps[step].astype(jnp.float32) * field_new[
+            :, ext_out : ext_out + rows_here
+        ]
         field_old, field_now = (field_now, field_new)
     image_flat = image_sum.astype(jnp.bfloat16).reshape(local_dirs, rows_here, depth * across)
     n_dir = lax.axis_size("dir")

time: 133 us -> 109 us (0.82)
  other arithmetic: 20.9 us -> 11.9 us
  starting transfers between devices: 47.2 us -> 39.4 us
  blocking collectives: 27.1 us -> 22.6 us
  waiting for transfers between devices: 20.2 us -> 15.7 us
  local copies, waits for them, and re-layouts: 13.1 us -> 14.8 us
    ppermute x8 -> x4, starting transfers between devices: 33.9 us -> 22 us  [the longest x2 16.5 us: exchange_halo(): after = lax.ppermute(heads, 'tile', down)]
    add x11 -> x3, other arithmetic: 14.2 us -> 6.85 us  [per_device(): field_new = 2.0 * now_mid - old_mid + speed_mid * curvature]
    slice x5 -> x19, local copies, waits for them, and re-layouts: 1.8 us -> 6.96 us  [the longest x12 3.05 us: unpack(): out.append(flat[offset:offset + size].reshape(shape))]
    scatter-add x4 -> x0, local copies, waits for them, and re-layouts: 4.78 us -> none  [per_device(): curvature = curvature.at[:, :, 0, :].add(recorded[step].astype(jnp.float32))]
    ppermute x8 -> x4, waiting for transfers between devices: 7.35 us -> 2.73 us  [the longest x2 2.35 us: exchange_halo(): after = lax.ppermute(heads, 'tile', down)]
    all_to_all x1, blocking collectives: 27.1 us -> 22.6 us  [per_device(): lax.all_to_all(partial, 'tile', split_axis=0, concat_axis=0, tiled=True)]
    all_to_all x1, starting transfers between devices: 13.3 us -> 17.4 us  [per_device(): got = lax.all_to_all(blocks, 'dir', split_axis=2, concat_axis=0, tiled=True)]
    reshape x0 -> x6, local copies, waits for them, and re-layouts: none -> 1.67 us  [the longest x4 1.62 us: unpack(): out.append(flat[offset:offset + size].reshape(shape))]
  transfers between devices with their start and end apart: 9 -> 5, of which waited for: 7 -> 3; matrix products, arithmetic and copies ran while one was open for 3% -> 5% of each run, Pallas kernels for 0% -> 0%
where the time goes in v2:
time: 109 us
  starting transfers between devices  39.4 us (36%)
  blocking collectives  22.6 us (21%)
  waiting for transfers between devices  15.7 us (14%)
  local copies, waits for them, and re-layouts  14.8 us (14%)
  other arithmetic  11.9 us (11%)
  matrix products  2.76 us (3%)
  between operations  1.25 us (1%)
    all_to_all x1, blocking collectives, per_device(): lax.all_to_all(partial, 'tile', split_axis=0, concat_axis=0, tiled=True)  22.6 us
    all_to_all x1, starting transfers between devices, per_device(): got = lax.all_to_all(blocks, 'dir', split_axis=2, concat_axis=0, tiled=True)  17.4 us
    ppermute x2, starting transfers between devices, exchange_halo(): after = lax.ppermute(heads, 'tile', down)  16.5 us
    all_to_all x1, waiting for transfers between devices, per_device(): got = lax.all_to_all(blocks, 'dir', split_axis=2, concat_axis=0, tiled=True)  13 us
    add x3, other arithmetic, per_device(): field_new = 2.0 * now_mid - old_mid + speed_mid * curvature  6.85 us
    ppermute x2, starting transfers between devices, exchange_halo(): before = lax.ppermute(tails, 'tile', up)  5.52 us
    unnamed x44, local copies, waits for them, and re-layouts  3.54 us
    slice x12, local copies, waits for them, and re-layouts, unpack(): out.append(flat[offset:offset + size].reshape(shape))  3.05 us
  transfers between devices with their start and end apart: 5, of which 3 were waited for; matrix products, arithmetic and copies ran while one was open for 5% of the time, Pallas kernels for 0%

profile of v2, /device:TPU:16, one launch (start us, length us, event | category | flops | bytes accessed | tf_op | source)
XLA Modules:
  0.0 108.5 jit_solution(12578176327820807753)
XLA Ops:
  0.6 1.0 fusion.131
  1.7 0.9 fusion.132
  2.7 3.6 %collective-permute-start.2 = (bf16[73728]{0:T(1024)(128)(2,1)S(1)}, bf16[73728]{0:T(1024)(128)(2,1)S(1)}, u32[]{:S(2)}, u32[]{:S(2)}) collective-permute-start(bf16[73728]{0:T(1024)(128)(2,1)S(1)} %pad_maximum_fusion.2), channel_id=1, source_target_pairs={{0,1},{1,2},{2,3},{3,4},{4,5},{5,6},{6,7},{7,8},{8,9},{9,10},{10,1... | collective-permute-start | bytes 442376 | tf_op jit(solution)/shard_map/ppermute | solution.py:47
  6.5 12.6 %collective-permute-start.3 = (bf16[73728]{0:T(1024)(128)(2,1)S(1)}, bf16[73728]{0:T(1024)(128)(2,1)S(1)}, u32[]{:S(2)}, u32[]{:S(2)}) collective-permute-start(bf16[73728]{0:T(1024)(128)(2,1)S(1)} %pad_maximum_fusion.3), channel_id=1, source_target_pairs={{1,0},{2,1},{3,2},{4,3},{5,4},{6,5},{7,6},{8,7},{9,8},{10,9},{11,1... | collective-permute-start | bytes 442376 | tf_op jit(solution)/shard_map/ppermute | solution.py:48
  19.4 1.9 %collective-permute-start = (f32[114688]{0:T(1024)S(1)}, f32[114688]{0:T(1024)S(1)}, u32[]{:S(2)}, u32[]{:S(2)}) collective-permute-start(f32[114688]{0:T(1024)S(1)} %pad_maximum_fusion), channel_id=1, source_target_pairs={{0,1},{1,2},{2,3},{3,4},{4,5},{5,6},{6,7},{7,8},{8,9},{9,10},{10,1... | collective-permute-start | bytes 1376264 | tf_op jit(solution)/shard_map/ppermute | solution.py:47
  21.6 0.8 pad_maximum_fusion.1
  22.4 3.9 %collective-permute-start.1 = (f32[114688]{0:T(1024)}, f32[114688]{0:T(1024)}, u32[]{:S(2)}, u32[]{:S(2)}) collective-permute-start(f32[114688]{0:T(1024)} %pad_maximum_fusion.1), channel_id=1, source_target_pairs={{1,0},{2,1},{3,2},{4,3},{5,4},{6,5},{7,6},{8,7},{9,8},{10,9},{11,1... | collective-permute-start | bytes 1376264 | tf_op jit(solution)/shard_map/ppermute | solution.py:48
  26.6 0.7 slice_bitcast_fusion
  27.4 0.7 slice.668
  28.1 0.6 slice.681
  28.7 0.6 slice.694
  29.4 0.4 collective-permute-done
  29.8 0.8 copy-done.9
  30.8 2.3 %collective-permute-done.1 = f32[114688]{0:T(1024)} collective-permute-done((f32[114688]{0:T(1024)}, f32[114688]{0:T(1024)}, u32[]{:S(2)}, u32[]{:S(2)}) %collective-permute-start.1) | collective-permute-done | bytes 458784 | tf_op jit(solution)/shard_map/ppermute | solution.py:48
  33.1 1.0 slice.639
  34.2 1.0 slice.641
  35.2 0.7 reshape.164
  35.9 0.9 slice.642
  36.9 0.7 reshape.165
  37.6 3.2 %fusion.22 = f32[2,56,8,256]{3,2,1,0:T(8,128)S(1)} fusion(f32[2,64,8,256]{3,2,1,0:T(8,128)S(1)} %constant_dynamic-update-slice_fusion, f32[2,12,8,256]{3,2,1,0:T(8,128)} %reshape.165, f32[2,32,8,256]{3,2,1,0:T(8,128)S(1)} %copy-done.2, f32[2,12,8,256]{3,2,1,0:T(8,128)} %reshape.164, f32[2,56,256]{2,1,0:T(8,128)} %get-tuple-element.11, ...), kind=kLoop, calls=%fused_computation.89 | loop fusion | flops 9175040 | bytes 11715072 | tf_op jit(solution)/shard_map/add | solution.py:99
  40.9 2.0 %fusion.49 = f32[2,48,8,256]{3,2,1,0:T(8,128)S(1)} fusion(f32[2,56,8,256]{3,2,1,0:T(8,128)S(1)} %fusion.22, f32[2,56,8,256]{3,2,1,0:T(8,128)S(1)} %maximum_convert_fusion, f32[2,64,8,256]{3,2,1,0:T(8,128)S(1)} %constant_dynamic-update-slice_fusion, f32[2,48,256]{2,1,0:T(8,128)S(1)} %copy-done.10, pred[8]{0:T(512)(128)(4,1)S(1)} %iota_compare_fusion), kind=kLoop, calls=%fused_computation.121 | loop fusion | flops 6881280 | bytes 10453504 | tf_op jit(solution)/shard_map/add | solution.py:99
  42.9 1.6 %fusion.76 = f32[2,40,8,256]{3,2,1,0:T(8,128)S(1)} fusion(f32[2,48,8,256]{3,2,1,0:T(8,128)S(1)} %fusion.49, f32[2,56,8,256]{3,2,1,0:T(8,128)S(1)} %maximum_convert_fusion, f32[2,56,8,256]{3,2,1,0:T(8,128)S(1)} %fusion.22, f32[2,40,256]{2,1,0:T(8,128)S(1)} %copy-done.11, pred[8]{0:T(512)(128)(4,1)S(1)} %iota_compare_fusion), kind=kLoop, calls=%fused_computation.153 | loop fusion | flops 5734400 | bytes 8733184 | tf_op jit(solution)/shard_map/add | solution.py:99
  44.6 2.1 %fusion.122 = (bf16[2,32,8,256]{3,2,1,0:T(8,128)(2,1)S(1)}, f32[2,32,8,256]{3,2,1,0:T(8,128)}) fusion(f32[2,56,8,256]{3,2,1,0:T(8,128)S(1)} %fusion.22, f32[2,48,8,256]{3,2,1,0:T(8,128)S(1)} %fusion.49, f32[2,40,8,256]{3,2,1,0:T(8,128)S(1)} %fusion.76, bf16[4,2,32,8,256]{4,3,2,1,0:T(8,128)(2,1)S(1)} %copy-done.3, f32[2,32,256]{2,1,0:T(8,128)S(1)} %copy-done.12, ...), kind=kLoop, calls=%fused_computation.205 | loop fusion | flops 6160384 | bytes 8847872 | tf_op jit(solution)/shard_map/convert_element_type | solution.py:104
  47.2 1.1 %reshape.176 = bf16[32,2,2048]{2,1,0:T(2,128)(2,1)} reshape(bf16[32,2,32,64]{3,2,1,0:T(8,128)(2,1)S(1)} %bitcast.57) | data formatting | bytes 524288
  48.3 17.4 %all-to-all-start = ((bf16[32,2,2048]{2,1,0:T(2,128)(2,1)}), bf16[32,2,2048]{2,1,0:T(2,128)(2,1)S(1)}, u32[]{:S(2)}, u32[]{:S(2)}) async-start(bf16[32,2,2048]{2,1,0:T(2,128)(2,1)} %reshape.176), calls=%async_computation | async-start | bytes 524288 | tf_op jit(solution)/shard_map/all_to_all | solution.py:109
  66.8 13.0 %all-to-all-done = bf16[32,2,2048]{2,1,0:T(2,128)(2,1)S(1)} async-done(((bf16[32,2,2048]{2,1,0:T(2,128)(2,1)}), bf16[32,2,2048]{2,1,0:T(2,128)(2,1)S(1)}, u32[]{:S(2)}, u32[]{:S(2)}) %all-to-all-start) | async-done | bytes 262176 | tf_op jit(solution)/shard_map/all_to_all | solution.py:109
  79.8 0.4 reshape.177
  80.1 2.8 %fusion.4 = f32[32,32,64]{2,1,0:T(8,128)S(1)} fusion(bf16[2048,64,1]{1,0,2:T(8,128)(2,1)S(1)} %bitcast.66, s32[2048]{0:T(1024)S(1)} %sub.54, s32[32,32]{1,0:T(8,128)S(1)} %multiply_add_fusion, bf16[2048]{0:T(1024)(128)(2,1)S(1)} %broadcast_in_dim.144, bf16[2048]{0:T(1024)(128)(2,1)S(1)} %broadcast_in_dim.142, bf16[2048]{0:T(1024)(128)(2,1)S(1)} %broadcast_in_dim.140, ...), kind=kOutput, calls=%fused_computation.72 | convolution fusion | flops 287309824 | bytes 552960 | tf_op jit(solution)/shard_map/dot_general | solution.py:115
  83.2 22.6 %all_to_all.20 = f32[32,1,2048]{2,1,0:T(1,128)S(1)} all-to-all(f32[32,1,2048]{2,1,0:T(1,128)S(1)} %reshape.178), channel_id=1, replica_groups=mesh['dir'=32,'tile'=32] {'tile'}, dimensions={0} | all-to-all | bytes 524288 | tf_op jit(solution)/shard_map/all_to_all | solution.py:119
  105.9 0.5 broadcast.120
  106.4 1.3 %reduce = f32[32,2048]{1,0:T(8,128)S(1)} reduce(f32[32,1,2048]{2,1,0:T(1,128)S(1)} %all_to_all.20, f32[]{:T(128)} %broadcast.120), dimensions={1}, to_apply=%all_to_all.17.reduce_sub_computation | reduce | bytes 524292 | tf_op jit(solution)/shard_map/all_to_all | solution.py:119
  107.9 0.7 reduce_sum.9
  (80 shorter events, 3.4 us)
Async XLA Ops:
  0.6 18.4 %copy-start = (f32[2,32,8,256]{3,2,1,0:T(8,128)S(1)}, f32[2,32,8,256]{3,2,1,0:T(8,128)}, u32[]{:S(2)}) copy-start(f32[2,32,8,256]{3,2,1,0:T(8,128)} %param.9) | copy-start | bytes 1572868
  2.7 23.7 %collective-permute-start.2 = (bf16[73728]{0:T(1024)(128)(2,1)S(1)}, bf16[73728]{0:T(1024)(128)(2,1)S(1)}, u32[]{:S(2)}, u32[]{:S(2)}) collective-permute-start(bf16[73728]{0:T(1024)(128)(2,1)S(1)} %pad_maximum_fusion.2), channel_id=1, source_target_pairs={{0,1},{1,2},{2,3},{3,4},{4,5},{5,6},{6,7},{7,8},{8,9},{9,10},{10,1... | collective-permute-start | bytes 442376 | tf_op jit(solution)/shard_map/ppermute | solution.py:47
  6.3 13.0 %copy-start.2 = (f32[2,32,8,256]{3,2,1,0:T(8,128)S(1)}, f32[2,32,8,256]{3,2,1,0:T(8,128)}, u32[]{:S(2)}) copy-start(f32[2,32,8,256]{3,2,1,0:T(8,128)} %param.8) | copy-start | bytes 1572868
  6.5 20.0 %collective-permute-start.3 = (bf16[73728]{0:T(1024)(128)(2,1)S(1)}, bf16[73728]{0:T(1024)(128)(2,1)S(1)}, u32[]{:S(2)}, u32[]{:S(2)}) collective-permute-start(bf16[73728]{0:T(1024)(128)(2,1)S(1)} %pad_maximum_fusion.3), channel_id=1, source_target_pairs={{1,0},{2,1},{3,2},{4,3},{5,4},{6,5},{7,6},{8,7},{9,8},{10,9},{11,1... | collective-permute-start | bytes 442376 | tf_op jit(solution)/shard_map/ppermute | solution.py:48
  19.4 10.4 %collective-permute-start = (f32[114688]{0:T(1024)S(1)}, f32[114688]{0:T(1024)S(1)}, u32[]{:S(2)}, u32[]{:S(2)}) collective-permute-start(f32[114688]{0:T(1024)S(1)} %pad_maximum_fusion), channel_id=1, source_target_pairs={{0,1},{1,2},{2,3},{3,4},{4,5},{5,6},{6,7},{7,8},{8,9},{9,10},{10,1... | collective-permute-start | bytes 1376264 | tf_op jit(solution)/shard_map/ppermute | solution.py:47
  21.4 5.1 %copy-start.8 = (bf16[4,2,32,256]{3,2,1,0:T(8,128)(2,1)S(1)}, bf16[4,2,32,256]{3,2,1,0:T(8,128)(2,1)}, u32[]{:S(2)}) copy-start(bf16[4,2,32,256]{3,2,1,0:T(8,128)(2,1)} %param.12) | copy-start | bytes 393220
  22.4 10.7 %collective-permute-start.1 = (f32[114688]{0:T(1024)}, f32[114688]{0:T(1024)}, u32[]{:S(2)}, u32[]{:S(2)}) collective-permute-start(f32[114688]{0:T(1024)} %pad_maximum_fusion.1), channel_id=1, source_target_pairs={{1,0},{2,1},{3,2},{4,3},{5,4},{6,5},{7,6},{8,7},{9,8},{10,9},{11,1... | collective-permute-start | bytes 1376264 | tf_op jit(solution)/shard_map/ppermute | solution.py:48
  26.6 2.8 %copy-start.1 = (bf16[2,32,8,256]{3,2,1,0:T(8,128)(2,1)S(1)}, bf16[2,32,8,256]{3,2,1,0:T(8,128)(2,1)}, u32[]{:S(2)}) copy-start(bf16[2,32,8,256]{3,2,1,0:T(8,128)(2,1)} %param.10) | copy-start | bytes 786436
  27.3 2.1 %copy-start.4 = (bf16[2,12,8,256]{3,2,1,0:T(8,128)(2,1)}, bf16[2,12,8,256]{3,2,1,0:T(8,128)(2,1)S(1)}, u32[]{:S(2)}) copy-start(bf16[2,12,8,256]{3,2,1,0:T(8,128)(2,1)S(1)} %slice.508) | copy-start | bytes 294916
  27.4 2.0 %copy-start.6 = (bf16[2,12,8,256]{3,2,1,0:T(8,128)(2,1)}, bf16[2,12,8,256]{3,2,1,0:T(8,128)(2,1)S(1)}, u32[]{:S(2)}) copy-start(bf16[2,12,8,256]{3,2,1,0:T(8,128)(2,1)S(1)} %slice.512) | copy-start | bytes 294916
  29.8 0.8 copy-start.9
  34.2 3.4 %copy-start.5 = (bf16[2,12,8,256]{3,2,1,0:T(8,128)(2,1)S(1)}, bf16[2,12,8,256]{3,2,1,0:T(8,128)(2,1)}, u32[]{:S(2)}) copy-start(bf16[2,12,8,256]{3,2,1,0:T(8,128)(2,1)} %copy-done.4) | copy-start | bytes 294916
  34.2 3.4 %copy-start.7 = (bf16[2,12,8,256]{3,2,1,0:T(8,128)(2,1)S(1)}, bf16[2,12,8,256]{3,2,1,0:T(8,128)(2,1)}, u32[]{:S(2)}) copy-start(bf16[2,12,8,256]{3,2,1,0:T(8,128)(2,1)} %copy-done.6) | copy-start | bytes 294916
  37.6 3.3 %copy-start.10 = (f32[2,48,256]{2,1,0:T(8,128)S(1)}, f32[2,48,256]{2,1,0:T(8,128)}, u32[]{:S(2)}) copy-start(f32[2,48,256]{2,1,0:T(8,128)} %slice.668) | copy-start | bytes 294916
  40.9 2.0 %copy-start.11 = (f32[2,40,256]{2,1,0:T(8,128)S(1)}, f32[2,40,256]{2,1,0:T(8,128)}, u32[]{:S(2)}) copy-start(f32[2,40,256]{2,1,0:T(8,128)} %slice.681) | copy-start | bytes 245764
  42.9 1.7 %copy-start.3 = (bf16[4,2,32,8,256]{4,3,2,1,0:T(8,128)(2,1)S(1)}, bf16[4,2,32,8,256]{4,3,2,1,0:T(8,128)(2,1)}, u32[]{:S(2)}) copy-start(bf16[4,2,32,8,256]{4,3,2,1,0:T(8,128)(2,1)} %param.11) | copy-start | bytes 3145732
  42.9 1.7 %copy-start.12 = (f32[2,32,256]{2,1,0:T(8,128)S(1)}, f32[2,32,256]{2,1,0:T(8,128)}, u32[]{:S(2)}) copy-start(f32[2,32,256]{2,1,0:T(8,128)} %slice.694) | copy-start | bytes 196612
  47.0 18.7 %copy-start.13 = (bf16[64,32,4]{0,2,1:T(4,128)(2,1)S(1)}, bf16[64,32,4]{0,2,1:T(4,128)(2,1)}, u32[]{:S(2)}) copy-start(bf16[64,32,4]{0,2,1:T(4,128)(2,1)} %param.15) | copy-start | bytes 49156
  47.2 19.4 %copy-start.14 = (s32[64,32]{0,1:T(8,128)S(1)}, s32[64,32]{0,1:T(8,128)}, u32[]{:S(2)}) copy-start(s32[64,32]{0,1:T(8,128)} %param.14) | copy-start | bytes 24580
  47.2 19.4 %copy-start.15 = (s32[64,32,1]{0,2,1:T(1,128)S(1)}, s32[64,32,1]{0,2,1:T(1,128)}, u32[]{:S(2)}) copy-start(s32[64,32,1]{0,2,1:T(1,128)} %param.13) | copy-start | bytes 24580
  48.3 31.4 %all-to-all-start = ((bf16[32,2,2048]{2,1,0:T(2,128)(2,1)}), bf16[32,2,2048]{2,1,0:T(2,128)(2,1)S(1)}, u32[]{:S(2)}, u32[]{:S(2)}) async-start(bf16[32,2,2048]{2,1,0:T(2,128)(2,1)} %reshape.176), calls=%async_computation | async-start | bytes 524288 | tf_op jit(solution)/shard_map/all_to_all | solution.py:109

commit v3 on v2

--- a/solution.py
+++ b/solution.py
@@ -38,29 +38,11 @@
     return out
 
 
-def exchange_halo(parts):
+def exchange_halo(tails, heads):
     count = lax.axis_size("tile")
     up = [(i, i + 1) for i in range(count - 1)]
     down = [(j, i) for i, j in up]
-    tails = jnp.concatenate([lax.slice_in_dim(p, p.shape[d] - w, p.shape[d], axis=d).reshape(-1) for p, d, w in parts])
-    heads = jnp.concatenate([lax.slice_in_dim(p, 0, w, axis=d).reshape(-1) for p, d, w in parts])
-    before = lax.ppermute(tails, "tile", up)
-    after = lax.ppermute(heads, "tile", down)
-    return before, after
-
-
-def unpack(flat, parts):
-    out = []
-    offset = 0
-    for p, d, w in parts:
-        shape = list(p.shape)
-        shape[d] = w
-        size = 1
-        for n in shape:
-            size *= n
-        out.append(flat[offset : offset + size].reshape(shape))
-        offset += size
-    return out
+    return lax.ppermute(tails, "tile", up), lax.ppermute(heads, "tile", down)
 
 
 def per_device(
@@ -69,14 +51,20 @@
     local_dirs, rows_here, depth, across = receiver_now.shape
     reach = 4
     halo = reach * STEPS
-    wide_parts = [(receiver_now, 1, halo), (receiver_old, 1, halo - reach)]
-    narrow_parts = [(courant, 1, halo - reach), (recorded, 2, halo - reach)]
-    wide_before, wide_after = exchange_halo(wide_parts)
-    narrow_before, narrow_after = exchange_halo(narrow_parts)
-    now_b, old_b = unpack(wide_before, wide_parts)
-    now_a, old_a = unpack(wide_after, wide_parts)
-    c_b, rec_b = unpack(narrow_before, narrow_parts)
-    c_a, rec_a = unpack(narrow_after, narrow_parts)
+    old_halo = halo - reach
+    wide_before, wide_after = exchange_halo(
+        jnp.concatenate([receiver_now[:, -halo:], receiver_old[:, -old_halo:]], axis=1),
+        jnp.concatenate([receiver_now[:, :halo], receiver_old[:, :old_halo]], axis=1),
+    )
+    traces = jnp.moveaxis(recorded, 0, 2)
+    narrow_before, narrow_after = exchange_halo(
+        jnp.concatenate([courant[:, -old_halo:], traces[:, -old_halo:]], axis=2),
+        jnp.concatenate([courant[:, :old_halo], traces[:, :old_halo]], axis=2),
+    )
+    now_b, old_b = wide_before[:, :halo], wide_before[:, halo:]
+    now_a, old_a = wide_after[:, :halo], wide_after[:, halo:]
+    c_b, rec_b = narrow_before[:, :, :depth], jnp.moveaxis(narrow_before[:, :, depth:], 2, 0)
+    c_a, rec_a = narrow_after[:, :, :depth], jnp.moveaxis(narrow_after[:, :, depth:], 2, 0)
     field_now = jnp.concatenate([now_b, receiver_now, now_a], axis=1)
     field_old = jnp.concatenate([old_b, receiver_old, old_a], axis=1)
     speed_wide = jnp.concatenate([c_b, courant, c_a], axis=1).astype(jnp.float32)

time: 109 us -> 102 us (0.936)
  local copies, waits for them, and re-layouts: 14.8 us -> 7.17 us
  waiting for transfers between devices: 15.7 us -> 18.2 us
  other arithmetic: 11.9 us -> 10.3 us
    slice x16 -> x10, local copies, waits for them, and re-layouts: 5.03 us -> 1.2 us  [the longest x1 1.02 us: per_device(): courant[:, -old_halo:]]
    ppermute x4, waiting for transfers between devices: 2.73 us -> 5.18 us  [exchange_halo(): return (lax.ppermute(tails, 'tile', up), lax.ppermute(heads, 'tile', down))]
    slice x3, local copies, waits for them, and re-layouts: 1.93 us -> 0.03 us  [per_device(): inject = rec_wide[step][:, lo:lo + rows_out, None, :]]
    reshape x6 -> x0, local copies, waits for them, and re-layouts: 1.67 us -> none  [the longest x4 1.62 us: unpack(): out.append(flat[offset:offset + size].reshape(shape))]
    unnamed x44 -> x21, local copies, waits for them, and re-layouts: 3.54 us -> 3.93 us
  transfers between devices with their start and end apart: 5 -> 5, of which waited for: 3 -> 3; matrix products, arithmetic and copies ran while one was open for 5% -> 1% of each run, Pallas kernels for 0% -> 0%
where the time goes in v3:
time: 102 us
  starting transfers between devices  39.6 us (39%)
  blocking collectives  22.6 us (22%)
  waiting for transfers between devices  18.2 us (18%)
  other arithmetic  10.3 us (10%)
  local copies, waits for them, and re-layouts  7.17 us (7%)
  matrix products  2.76 us (3%)
  between operations  1.1 us (1%)
    all_to_all x1, blocking collectives, per_device(): lax.all_to_all(partial, 'tile', split_axis=0, concat_axis=0, tiled=True)  22.6 us
    ppermute x4, starting transfers between devices, exchange_halo(): return (lax.ppermute(tails, 'tile', up), lax.ppermute(heads, 'tile', down))  22.2 us
    all_to_all x1, starting transfers between devices, per_device(): got = lax.all_to_all(blocks, 'dir', split_axis=2, concat_axis=0, tiled=True)  17.4 us
    all_to_all x1, waiting for transfers between devices, per_device(): got = lax.all_to_all(blocks, 'dir', split_axis=2, concat_axis=0, tiled=True)  13 us
    add x3, other arithmetic, per_device(): field_new = 2.0 * now_mid - old_mid + speed_mid * curvature  5.85 us
    ppermute x4, waiting for transfers between devices, exchange_halo(): return (lax.ppermute(tails, 'tile', up), lax.ppermute(heads, 'tile', down))  5.18 us
    unnamed x21, local copies, waits for them, and re-layouts  3.93 us
    dot_general x1, matrix products, per_device(): lax.dot_general(mt, got, (((0,), (0,)), ((), ())), preferred_element_type...  2.76 us
  transfers between devices with their start and end apart: 5, of which 3 were waited for; matrix products, arithmetic and copies ran while one was open for 1% of the time, Pallas kernels for 0%

profile of v3, /device:TPU:16, one launch (start us, length us, event | category | flops | bytes accessed | tf_op | source)
XLA Modules:
  0.0 101.7 jit_solution(16540147311965239633)
XLA Ops:
  0.6 1.1 %copy.30 = bf16[4,2,32,256]{3,0,2,1:T(4,128)(2,1)S(1)} copy(bf16[4,2,32,256]{3,2,1,0:T(8,128)(2,1)} %param.12) | data formatting | bytes 262144 | tf_op args[4]
  1.8 1.0 %fusion.131 = (bf16[2,12,8,256]{3,2,1,0:T(8,128)(2,1)S(1)}, bf16[2,12,8,256]{3,2,1,0:T(8,128)(2,1)S(1)}) fusion(bf16[2,32,8,256]{3,2,1,0:T(8,128)(2,1)} %param.10), kind=kLoop, calls=%fused_computation.237 | loop fusion | bytes 393216 | tf_op jit(solution)/shard_map/slice | solution.py:61
  2.8 3.6 %collective-permute-start.2 = (bf16[2,12,12,256]{3,2,1,0:T(8,128)(2,1)S(1)}, bf16[2,12,12,256]{3,2,1,0:T(8,128)(2,1)S(1)}, u32[]{:S(2)}, u32[]{:S(2)}) collective-permute-start(bf16[2,12,12,256]{3,2,1,0:T(8,128)(2,1)S(1)} %pad_maximum_fusion.3), channel_id=1, source_target_pairs={{0,1},{1,2},{2,3},{3,4},{4,5},{5,6},{6,7},{7,8},{8,9},{9,10},{10,1... | collective-permute-start | bytes 442376 | tf_op jit(solution)/shard_map/ppermute | solution.py:45
  6.5 12.6 %collective-permute-start.3 = (bf16[2,12,12,256]{3,2,1,0:T(8,128)(2,1)S(1)}, bf16[2,12,12,256]{3,2,1,0:T(8,128)(2,1)S(1)}, u32[]{:S(2)}, u32[]{:S(2)}) collective-permute-start(bf16[2,12,12,256]{3,2,1,0:T(8,128)(2,1)S(1)} %pad_maximum_fusion.4), channel_id=1, source_target_pairs={{1,0},{2,1},{3,2},{4,3},{5,4},{6,5},{7,6},{8,7},{9,8},{10,9},{11,1... | collective-permute-start | bytes 442376 | tf_op jit(solution)/shard_map/ppermute | solution.py:45
  19.2 2.1 %collective-permute-start = (f32[2,28,8,256]{3,2,1,0:T(8,128)S(1)}, f32[2,28,8,256]{3,2,1,0:T(8,128)S(1)}, u32[]{:S(2)}, u32[]{:S(2)}) collective-permute-start(f32[2,28,8,256]{3,2,1,0:T(8,128)S(1)} %pad_maximum_fusion.1), channel_id=1, source_target_pairs={{0,1},{1,2},{2,3},{3,4},{4,5},{5,6},{6,7},{7,8},{8,9},{9,10},{10,1... | collective-permute-start | bytes 1376264 | tf_op jit(solution)/shard_map/ppermute | solution.py:45
  21.3 3.9 %collective-permute-start.1 = (f32[2,28,8,256]{3,2,1,0:T(8,128)S(1)}, f32[2,28,8,256]{3,2,1,0:T(8,128)S(1)}, u32[]{:S(2)}, u32[]{:S(2)}) collective-permute-start(f32[2,28,8,256]{3,2,1,0:T(8,128)S(1)} %pad_maximum_fusion.2), channel_id=1, source_target_pairs={{1,0},{2,1},{3,2},{4,3},{5,4},{6,5},{7,6},{8,7},{9,8},{10,9},{11,1... | collective-permute-start | bytes 1376264 | tf_op jit(solution)/shard_map/ppermute | solution.py:45
  25.6 0.8 copy-done.1
  26.5 3.2 %collective-permute-done = f32[2,28,8,256]{3,2,1,0:T(8,128)S(1)} collective-permute-done((f32[2,28,8,256]{3,2,1,0:T(8,128)S(1)}, f32[2,28,8,256]{3,2,1,0:T(8,128)S(1)}, u32[]{:S(2)}, u32[]{:S(2)}) %collective-permute-start) | collective-permute-done | bytes 458784 | tf_op jit(solution)/shard_map/ppermute | solution.py:45
  29.7 1.9 %collective-permute-done.1 = f32[2,28,8,256]{3,2,1,0:T(8,128)S(1)} collective-permute-done((f32[2,28,8,256]{3,2,1,0:T(8,128)S(1)}, f32[2,28,8,256]{3,2,1,0:T(8,128)S(1)}, u32[]{:S(2)}, u32[]{:S(2)}) %collective-permute-start.1) | collective-permute-done | bytes 458784 | tf_op jit(solution)/shard_map/ppermute | solution.py:45
  31.8 2.3 %fusion.22 = f32[2,56,8,256]{3,2,1,0:T(8,128)S(1)} fusion(f32[2,64,8,256]{3,2,1,0:T(8,128)S(1)} %pad_maximum_fusion, f32[2,12,8,256]{3,2,1,0:T(8,128)S(1)} %slice.598, f32[2,32,8,256]{3,2,1,0:T(8,128)S(1)} %copy-done.2, f32[2,12,8,256]{3,2,1,0:T(8,128)S(1)} %slice.597, f32[2,56,256]{2,1,0:T(8,128)S(1)} %get-tuple-element.11, ...), kind=kLoop, calls=%fused_computation.90 | loop fusion | flops 9175040 | bytes 11715072 | tf_op jit(solution)/shard_map/add | solution.py:87
  34.1 1.9 %fusion.49 = f32[2,48,8,256]{3,2,1,0:T(8,128)S(1)} fusion(f32[2,56,8,256]{3,2,1,0:T(8,128)S(1)} %fusion.22, f32[2,56,8,256]{3,2,1,0:T(8,128)S(1)} %maximum_convert_fusion, f32[2,64,8,256]{3,2,1,0:T(8,128)S(1)} %pad_maximum_fusion, f32[2,48,256]{2,1,0:T(8,128)S(1)} %slice.626, pred[8]{0:T(512)(128)(4,1)S(1)} %iota_compare_fusion), kind=kLoop, calls=%fused_computation.122 | loop fusion | flops 6881280 | bytes 10453504 | tf_op jit(solution)/shard_map/add | solution.py:87
  36.1 1.6 %fusion.76 = f32[2,40,8,256]{3,2,1,0:T(8,128)S(1)} fusion(f32[2,48,8,256]{3,2,1,0:T(8,128)S(1)} %fusion.49, f32[2,56,8,256]{3,2,1,0:T(8,128)S(1)} %maximum_convert_fusion, f32[2,56,8,256]{3,2,1,0:T(8,128)S(1)} %fusion.22, f32[2,40,256]{2,1,0:T(8,128)S(1)} %slice.639, pred[8]{0:T(512)(128)(4,1)S(1)} %iota_compare_fusion), kind=kLoop, calls=%fused_computation.154 | loop fusion | flops 5734400 | bytes 8733184 | tf_op jit(solution)/shard_map/add | solution.py:87
  37.7 2.2 %fusion.122 = (bf16[2,32,8,256]{3,2,1,0:T(8,128)(2,1)S(1)}, f32[2,32,8,256]{3,2,1,0:T(8,128)}) fusion(f32[2,56,8,256]{3,2,1,0:T(8,128)S(1)} %fusion.22, f32[2,48,8,256]{3,2,1,0:T(8,128)S(1)} %fusion.49, f32[2,40,8,256]{3,2,1,0:T(8,128)S(1)} %fusion.76, bf16[4,2,32,8,256]{4,3,2,1,0:T(8,128)(2,1)S(1)} %copy-done.3, f32[2,32,256]{2,1,0:T(8,128)S(1)} %slice.652, ...), kind=kLoop, calls=%fused_computation.206 | loop fusion | flops 6160384 | bytes 8847872 | tf_op jit(solution)/shard_map/convert_element_type | solution.py:92
  39.9 0.2 reshape_reshape.3
  40.2 0.2 copy.31
  40.4 1.1 %reshape.92 = bf16[32,2,2048]{2,1,0:T(2,128)(2,1)} reshape(bf16[32,2,32,64]{3,2,1,0:T(8,128)(2,1)S(1)} %bitcast.52) | data formatting | bytes 524288
  41.5 17.4 %all-to-all-start = ((bf16[32,2,2048]{2,1,0:T(2,128)(2,1)}), bf16[32,2,2048]{2,1,0:T(2,128)(2,1)S(1)}, u32[]{:S(2)}, u32[]{:S(2)}) async-start(bf16[32,2,2048]{2,1,0:T(2,128)(2,1)} %reshape.92), calls=%async_computation | async-start | bytes 524288 | tf_op jit(solution)/shard_map/all_to_all | solution.py:97
  59.0 0.1 copy.20
  59.1 0.1 copy.21
  59.2 0.1 broadcast_in_dim.140
  59.3 0.1 copy.22
  59.4 0.1 broadcast_in_dim.142
  59.5 0.1 copy.23
  59.9 13.0 %all-to-all-done = bf16[32,2,2048]{2,1,0:T(2,128)(2,1)S(1)} async-done(((bf16[32,2,2048]{2,1,0:T(2,128)(2,1)}), bf16[32,2,2048]{2,1,0:T(2,128)(2,1)S(1)}, u32[]{:S(2)}, u32[]{:S(2)}) %all-to-all-start) | async-done | bytes 262176 | tf_op jit(solution)/shard_map/all_to_all | solution.py:97
  72.9 0.4 reshape.93
  73.3 2.8 %fusion.4 = f32[32,32,64]{2,1,0:T(8,128)S(1)} fusion(bf16[2048,64,1]{1,0,2:T(8,128)(2,1)S(1)} %bitcast.53, s32[2048]{0:T(1024)S(1)} %sub.54, s32[32,32]{1,0:T(8,128)S(1)} %multiply_add_fusion, bf16[2048]{0:T(1024)(128)(2,1)S(1)} %broadcast_in_dim.144, bf16[2048]{0:T(1024)(128)(2,1)S(1)} %broadcast_in_dim.142, bf16[2048]{0:T(1024)(128)(2,1)S(1)} %broadcast_in_dim.140, ...), kind=kOutput, calls=%fused_computation.72 | convolution fusion | flops 287309824 | bytes 552960 | tf_op jit(solution)/shard_map/dot_general | solution.py:103
  76.1 0.3 reshape.94
  76.4 22.6 %all_to_all.20 = f32[32,1,2048]{2,1,0:T(1,128)S(1)} all-to-all(f32[32,1,2048]{2,1,0:T(1,128)S(1)} %reshape.94), channel_id=1, replica_groups=mesh['dir'=32,'tile'=32] {'tile'}, dimensions={0} | all-to-all | bytes 524288 | tf_op jit(solution)/shard_map/all_to_all | solution.py:107
  99.0 0.5 broadcast.120
  99.6 1.3 %reduce = f32[32,2048]{1,0:T(8,128)S(1)} reduce(f32[32,1,2048]{2,1,0:T(1,128)S(1)} %all_to_all.20, f32[]{:T(128)} %broadcast.120), dimensions={1}, to_apply=%all_to_all.17.reduce_sub_computation | reduce | bytes 524292 | tf_op jit(solution)/shard_map/all_to_all | solution.py:107
  100.8 0.2 reshape.95
  101.0 0.7 reduce_sum.9
  (49 shorter events, 1.1 us)
Async XLA Ops:
  0.6 18.4 %copy-start = (f32[2,32,8,256]{3,2,1,0:T(8,128)S(1)}, f32[2,32,8,256]{3,2,1,0:T(8,128)}, u32[]{:S(2)}) copy-start(f32[2,32,8,256]{3,2,1,0:T(8,128)} %param.9) | copy-start | bytes 1572868
  1.8 17.4 %copy-start.2 = (f32[2,32,8,256]{3,2,1,0:T(8,128)S(1)}, f32[2,32,8,256]{3,2,1,0:T(8,128)}, u32[]{:S(2)}) copy-start(f32[2,32,8,256]{3,2,1,0:T(8,128)} %param.8) | copy-start | bytes 1572868
  2.8 22.5 %collective-permute-start.2 = (bf16[2,12,12,256]{3,2,1,0:T(8,128)(2,1)S(1)}, bf16[2,12,12,256]{3,2,1,0:T(8,128)(2,1)S(1)}, u32[]{:S(2)}, u32[]{:S(2)}) collective-permute-start(bf16[2,12,12,256]{3,2,1,0:T(8,128)(2,1)S(1)} %pad_maximum_fusion.3), channel_id=1, source_target_pairs={{0,1},{1,2},{2,3},{3,4},{4,5},{5,6},{6,7},{7,8},{8,9},{9,10},{10,1... | collective-permute-start | bytes 442376 | tf_op jit(solution)/shard_map/ppermute | solution.py:45
  6.5 18.9 %collective-permute-start.3 = (bf16[2,12,12,256]{3,2,1,0:T(8,128)(2,1)S(1)}, bf16[2,12,12,256]{3,2,1,0:T(8,128)(2,1)S(1)}, u32[]{:S(2)}, u32[]{:S(2)}) collective-permute-start(bf16[2,12,12,256]{3,2,1,0:T(8,128)(2,1)S(1)} %pad_maximum_fusion.4), channel_id=1, source_target_pairs={{1,0},{2,1},{3,2},{4,3},{5,4},{6,5},{7,6},{8,7},{9,8},{10,9},{11,1... | collective-permute-start | bytes 442376 | tf_op jit(solution)/shard_map/ppermute | solution.py:45
  19.2 6.2 %copy-start.4 = (bf16[4,2,32,256]{3,2,1,0:T(8,128)(2,1)S(1)}, bf16[4,2,32,256]{3,2,1,0:T(8,128)(2,1)}, u32[]{:S(2)}) copy-start(bf16[4,2,32,256]{3,2,1,0:T(8,128)(2,1)} %param.12) | copy-start | bytes 393220
  19.2 10.5 %collective-permute-start = (f32[2,28,8,256]{3,2,1,0:T(8,128)S(1)}, f32[2,28,8,256]{3,2,1,0:T(8,128)S(1)}, u32[]{:S(2)}, u32[]{:S(2)}) collective-permute-start(f32[2,28,8,256]{3,2,1,0:T(8,128)S(1)} %pad_maximum_fusion.1), channel_id=1, source_target_pairs={{0,1},{1,2},{2,3},{3,4},{4,5},{5,6},{6,7},{7,8},{8,9},{9,10},{10,1... | collective-permute-start | bytes 1376264 | tf_op jit(solution)/shard_map/ppermute | solution.py:45
  21.3 10.4 %collective-permute-start.1 = (f32[2,28,8,256]{3,2,1,0:T(8,128)S(1)}, f32[2,28,8,256]{3,2,1,0:T(8,128)S(1)}, u32[]{:S(2)}, u32[]{:S(2)}) collective-permute-start(f32[2,28,8,256]{3,2,1,0:T(8,128)S(1)} %pad_maximum_fusion.2), channel_id=1, source_target_pairs={{1,0},{2,1},{3,2},{4,3},{5,4},{6,5},{7,6},{8,7},{9,8},{10,9},{11,1... | collective-permute-start | bytes 1376264 | tf_op jit(solution)/shard_map/ppermute | solution.py:45
  25.5 1.0 copy-start.1
  36.1 1.7 %copy-start.3 = (bf16[4,2,32,8,256]{4,3,2,1,0:T(8,128)(2,1)S(1)}, bf16[4,2,32,8,256]{4,3,2,1,0:T(8,128)(2,1)}, u32[]{:S(2)}) copy-start(bf16[4,2,32,8,256]{4,3,2,1,0:T(8,128)(2,1)} %param.11) | copy-start | bytes 3145732
  40.1 18.7 %copy-start.5 = (bf16[64,32,4]{0,2,1:T(4,128)(2,1)S(1)}, bf16[64,32,4]{0,2,1:T(4,128)(2,1)}, u32[]{:S(2)}) copy-start(bf16[64,32,4]{0,2,1:T(4,128)(2,1)} %param.15) | copy-start | bytes 49156
  40.4 19.4 %copy-start.6 = (s32[64,32]{0,1:T(8,128)S(1)}, s32[64,32]{0,1:T(8,128)}, u32[]{:S(2)}) copy-start(s32[64,32]{0,1:T(8,128)} %param.14) | copy-start | bytes 24580
  40.4 19.4 %copy-start.7 = (s32[64,32,1]{0,2,1:T(1,128)S(1)}, s32[64,32,1]{0,2,1:T(1,128)}, u32[]{:S(2)}) copy-start(s32[64,32,1]{0,2,1:T(1,128)} %param.13) | copy-start | bytes 24580
  41.5 31.4 %all-to-all-start = ((bf16[32,2,2048]{2,1,0:T(2,128)(2,1)}), bf16[32,2,2048]{2,1,0:T(2,128)(2,1)S(1)}, u32[]{:S(2)}, u32[]{:S(2)}) async-start(bf16[32,2,2048]{2,1,0:T(2,128)(2,1)} %reshape.92), calls=%async_computation | async-start | bytes 524288 | tf_op jit(solution)/shard_map/all_to_all | solution.py:97

commit v4 on v3

--- a/solution.py
+++ b/solution.py
@@ -99,13 +99,13 @@
     got = got.reshape(all_dirs * rows_here, cols)
     owner = row_owner[:, :, 0]
     mt = band_matrix(owner, band_start, band_weight, n_tiles, rows_here)
-    mt = mt.reshape(all_dirs * rows_here, n_tiles * rows_here)
+    mt = lax.optimization_barrier(mt.reshape(all_dirs * rows_here, n_tiles * rows_here))
     partial = lax.dot_general(
         mt, got, (((0,), (0,)), ((), ())), preferred_element_type=jnp.float32
     )
-    partial = partial.reshape(n_tiles, rows_here, cols)
+    partial = partial.reshape(n_tiles, rows_here * cols)
     sent = lax.all_to_all(partial, "tile", split_axis=0, concat_axis=0, tiled=True)
-    stack = jnp.sum(sent, axis=0)
+    stack = jnp.sum(sent.reshape(n_tiles, rows_here, cols), axis=0)
     return (field_now, stack)
 
 

time: 102 us -> 104 us (1.020)
  waiting for transfers between devices: 18.2 us -> 12.4 us
  local copies, waits for them, and re-layouts: 7.17 us -> 11.9 us
  starting transfers between devices: 39.6 us -> 35.6 us
  other arithmetic: 10.3 us -> 14.1 us
  blocking collectives: 22.6 us -> 25 us
    all_to_all x1, starting transfers between devices: 17.4 us -> 12.3 us  [per_device(): got = lax.all_to_all(blocks, 'dir', split_axis=2, concat_axis=0, tiled=True)]
    select_n x0 -> x1, other arithmetic: none -> 4.93 us  [band_matrix(): out = jnp.where(diff == k, wide[:, :, k:k + 1], out)]
    all_to_all x1, waiting for transfers between devices: 13 us -> 8.93 us  [per_device(): got = lax.all_to_all(blocks, 'dir', split_axis=2, concat_axis=0, tiled=True)]
    all_to_all x1, blocking collectives: 22.6 us -> 25 us  [per_device(): lax.all_to_all(partial, 'tile', split_axis=0, concat_axis=0, tiled=True)]
    ppermute x4, waiting for transfers between devices: 5.18 us -> 3.43 us  [exchange_halo(): return (lax.ppermute(tails, 'tile', up), lax.ppermute(heads, 'tile', down))]
    unnamed x21 -> x19, local copies, waits for them, and re-layouts: 3.93 us -> 2.55 us
    all_to_all x1 -> x0, other arithmetic: 1.26 us -> none  [per_device(): lax.all_to_all(partial, 'tile', split_axis=0, concat_axis=0, tiled=True)]
    ppermute x4, starting transfers between devices: 22.2 us -> 23.3 us  [exchange_halo(): return (lax.ppermute(tails, 'tile', up), lax.ppermute(heads, 'tile', down))]
  transfers between devices with their start and end apart: 5 -> 5, of which waited for: 3 -> 2; matrix products, arithmetic and copies ran while one was open for 1% -> 12% of each run, Pallas kernels for 0% -> 0%
where the time goes in v4:
time: 104 us
  starting transfers between devices  35.6 us (34%)
  blocking collectives  25 us (24%)
  other arithmetic  14.1 us (14%)
  waiting for transfers between devices  12.4 us (12%)
  local copies, waits for them, and re-layouts  11.9 us (11%)
  matrix products  3.47 us (3%)
  between operations  1.05 us (1%)
    all_to_all x1, blocking collectives, per_device(): lax.all_to_all(partial, 'tile', split_axis=0, concat_axis=0, tiled=True)  25 us
    ppermute x4, starting transfers between devices, exchange_halo(): return (lax.ppermute(tails, 'tile', up), lax.ppermute(heads, 'tile', down))  23.3 us
    all_to_all x1, starting transfers between devices, per_device(): got = lax.all_to_all(blocks, 'dir', split_axis=2, concat_axis=0, tiled=True)  12.3 us
    all_to_all x1, waiting for transfers between devices, per_device(): got = lax.all_to_all(blocks, 'dir', split_axis=2, concat_axis=0, tiled=True)  8.93 us
    add x3, other arithmetic, per_device(): field_new = 2.0 * now_mid - old_mid + speed_mid * curvature  5.86 us
    select_n x1, other arithmetic, band_matrix(): out = jnp.where(diff == k, wide[:, :, k:k + 1], out)  4.93 us
    dot_general x1, matrix products, per_device(): lax.dot_general(mt, got, (((0,), (0,)), ((), ())), preferred_element_type...  3.47 us
    ppermute x4, waiting for transfers between devices, exchange_halo(): return (lax.ppermute(tails, 'tile', up), lax.ppermute(heads, 'tile', down))  3.43 us
  transfers between devices with their start and end apart: 5, of which 2 were waited for; matrix products, arithmetic and copies ran while one was open for 12% of the time, Pallas kernels for 0%

profile of v4, /device:TPU:16, one launch (start us, length us, event | category | flops | bytes accessed | tf_op | source)
XLA Modules:
  0.0 103.5 jit_solution(3835257659397061446)
XLA Ops:
  0.7 1.1 %copy.40 = bf16[4,2,32,256]{3,0,2,1:T(4,128)(2,1)S(1)} copy(bf16[4,2,32,256]{3,2,1,0:T(8,128)(2,1)} %param.12) | data formatting | bytes 262144 | tf_op args[4]
  1.8 1.0 fusion.123
  2.8 14.9 %collective-permute-start.3 = (bf16[2,12,12,256]{3,2,1,0:T(8,128)(2,1)S(1)}, bf16[2,12,12,256]{3,2,1,0:T(8,128)(2,1)}, u32[]{:S(2)}, u32[]{:S(2)}) collective-permute-start(bf16[2,12,12,256]{3,2,1,0:T(8,128)(2,1)S(1)} %pad_maximum_fusion.4), channel_id=1, source_target_pairs={{1,0},{2,1},{3,2},{4,3},{5,4},{6,5},{7,6},{8,7},{9,8},{10,9},{11,1... | collective-permute-start | bytes 442376 | tf_op jit(solution)/shard_map/ppermute | solution.py:45
  17.7 0.7 pad_maximum_fusion.3
  18.4 1.9 %collective-permute-start.2 = (bf16[2,12,12,256]{3,2,1,0:T(8,128)(2,1)}, bf16[2,12,12,256]{3,2,1,0:T(8,128)(2,1)}, u32[]{:S(2)}, u32[]{:S(2)}) collective-permute-start(bf16[2,12,12,256]{3,2,1,0:T(8,128)(2,1)} %pad_maximum_fusion.3), channel_id=1, source_target_pairs={{0,1},{1,2},{2,3},{3,4},{4,5},{5,6},{6,7},{7,8},{8,9},{9,10},{10,1... | collective-permute-start | bytes 442376 | tf_op jit(solution)/shard_map/ppermute | solution.py:45
  20.3 1.1 %fusion.122 = (f32[2,12,8,256]{3,2,1,0:T(8,128)S(1)}, f32[2,12,8,256]{3,2,1,0:T(8,128)S(1)}) fusion(f32[2,32,8,256]{3,2,1,0:T(8,128)} %param.8), kind=kLoop, calls=%fused_computation.225 | loop fusion | bytes 786432 | tf_op jit(solution)/shard_map/slice | solution.py:56
  21.4 1.1 %fusion.121 = (f32[2,16,8,256]{3,2,1,0:T(8,128)S(1)}, f32[2,16,8,256]{3,2,1,0:T(8,128)S(1)}) fusion(f32[2,32,8,256]{3,2,1,0:T(8,128)} %param.9), kind=kLoop, calls=%fused_computation.224 | loop fusion | bytes 1048576 | tf_op jit(solution)/shard_map/slice | solution.py:56
  22.6 4.6 %collective-permute-start.1 = (f32[2,28,8,256]{3,2,1,0:T(8,128)S(1)}, f32[2,28,8,256]{3,2,1,0:T(8,128)S(1)}, u32[]{:S(2)}, u32[]{:S(2)}) collective-permute-start(f32[2,28,8,256]{3,2,1,0:T(8,128)S(1)} %pad_maximum_fusion.2), channel_id=1, source_target_pairs={{1,0},{2,1},{3,2},{4,3},{5,4},{6,5},{7,6},{8,7},{9,8},{10,9},{11,1... | collective-permute-start | bytes 1376264 | tf_op jit(solution)/shard_map/ppermute | solution.py:45
  27.2 1.9 %collective-permute-start = (f32[2,28,8,256]{3,2,1,0:T(8,128)S(1)}, f32[2,28,8,256]{3,2,1,0:T(8,128)S(1)}, u32[]{:S(2)}, u32[]{:S(2)}) collective-permute-start(f32[2,28,8,256]{3,2,1,0:T(8,128)S(1)} %pad_maximum_fusion.1), channel_id=1, source_target_pairs={{0,1},{1,2},{2,3},{3,4},{4,5},{5,6},{6,7},{7,8},{8,9},{9,10},{10,1... | collective-permute-start | bytes 1376264 | tf_op jit(solution)/shard_map/ppermute | solution.py:45
  29.6 0.1 copy.31
  30.0 0.1 copy.32
  30.2 0.9 slice_bitcast_fusion.4
  31.1 0.9 slice_bitcast_fusion.5
  32.2 0.9 slice.602
  33.1 0.9 slice.600
  34.2 3.4 %collective-permute-done = f32[2,28,8,256]{3,2,1,0:T(8,128)S(1)} collective-permute-done((f32[2,28,8,256]{3,2,1,0:T(8,128)S(1)}, f32[2,28,8,256]{3,2,1,0:T(8,128)S(1)}, u32[]{:S(2)}, u32[]{:S(2)}) %collective-permute-start) | collective-permute-done | bytes 458784 | tf_op jit(solution)/shard_map/ppermute | solution.py:45
  37.8 2.3 %fusion.19 = f32[2,56,8,256]{3,2,1,0:T(8,128)S(1)} fusion(f32[2,64,8,256]{3,2,1,0:T(8,128)S(1)} %pad_maximum_fusion, f32[2,12,8,256]{3,2,1,0:T(8,128)S(1)} %slice.598, f32[2,32,8,256]{3,2,1,0:T(8,128)S(1)} %copy-done.2, f32[2,12,8,256]{3,2,1,0:T(8,128)S(1)} %slice.597, f32[2,56,256]{2,1,0:T(8,128)S(1)} %get-tuple-element.11, ...), kind=kLoop, calls=%fused_computation.85 | loop fusion | flops 9175040 | bytes 11715072 | tf_op jit(solution)/shard_map/add | solution.py:87
  40.0 1.9 %fusion.46 = f32[2,48,8,256]{3,2,1,0:T(8,128)S(1)} fusion(f32[2,56,8,256]{3,2,1,0:T(8,128)S(1)} %fusion.19, f32[2,56,8,256]{3,2,1,0:T(8,128)S(1)} %maximum_convert_fusion, f32[2,64,8,256]{3,2,1,0:T(8,128)S(1)} %pad_maximum_fusion, f32[2,48,256]{2,1,0:T(8,128)S(1)} %slice.626, pred[8]{0:T(512)(128)(4,1)S(1)} %iota_compare_fusion), kind=kLoop, calls=%fused_computation.117 | loop fusion | flops 6881280 | bytes 10453504 | tf_op jit(solution)/shard_map/add | solution.py:87
  42.0 1.6 %fusion.73 = f32[2,40,8,256]{3,2,1,0:T(8,128)S(1)} fusion(f32[2,48,8,256]{3,2,1,0:T(8,128)S(1)} %fusion.46, f32[2,56,8,256]{3,2,1,0:T(8,128)S(1)} %maximum_convert_fusion, f32[2,56,8,256]{3,2,1,0:T(8,128)S(1)} %fusion.19, f32[2,40,256]{2,1,0:T(8,128)S(1)} %slice.639, pred[8]{0:T(512)(128)(4,1)S(1)} %iota_compare_fusion), kind=kLoop, calls=%fused_computation.149 | loop fusion | flops 5734400 | bytes 8733184 | tf_op jit(solution)/shard_map/add | solution.py:87
  43.7 2.2 %fusion.119 = (bf16[2,32,8,256]{3,2,1,0:T(8,128)(2,1)S(1)}, f32[2,32,8,256]{3,2,1,0:T(8,128)}) fusion(f32[2,56,8,256]{3,2,1,0:T(8,128)S(1)} %fusion.19, f32[2,48,8,256]{3,2,1,0:T(8,128)S(1)} %fusion.46, f32[2,40,8,256]{3,2,1,0:T(8,128)S(1)} %fusion.73, bf16[4,2,32,8,256]{4,3,2,1,0:T(8,128)(2,1)S(1)} %copy-done.3, f32[2,32,256]{2,1,0:T(8,128)S(1)} %slice.652, ...), kind=kLoop, calls=%fused_computation.201 | loop fusion | flops 6160384 | bytes 8847872 | tf_op jit(solution)/shard_map/convert_element_type | solution.py:92
  45.8 0.2 reshape_reshape.3
  46.1 0.2 copy.41
  46.3 1.1 %reshape.50 = bf16[32,2,2048]{2,1,0:T(2,128)(2,1)} reshape(bf16[32,2,32,64]{3,2,1,0:T(8,128)(2,1)S(1)} %bitcast.52) | data formatting | bytes 524288
  47.4 12.3 %all-to-all-start = ((bf16[32,2,2048]{2,1,0:T(2,128)(2,1)}), bf16[32,2,2048]{2,1,0:T(2,128)(2,1)S(1)}, u32[]{:S(2)}, u32[]{:S(2)}) async-start(bf16[32,2,2048]{2,1,0:T(2,128)(2,1)} %reshape.50), calls=%async_computation | async-start | bytes 524288 | tf_op jit(solution)/shard_map/all_to_all | solution.py:97
  59.7 4.9 %fusion.4 = bf16[2048,1024]{1,0:T(8,128)(2,1)} fusion(s32[2048]{0:T(1024)S(1)} %sub.33, bf16[2048]{0:T(1024)(128)(2,1)S(1)} %broadcast_in_dim.144, bf16[2048]{0:T(1024)(128)(2,1)S(1)} %broadcast_in_dim.142, bf16[2048]{0:T(1024)(128)(2,1)S(1)} %broadcast_in_dim.140, bf16[2048]{0:T(1024)(128)(2,1)S(1)} %broadcast_in_dim.138), kind=kLoop, calls=%fused_computation.69 | loop fusion | flops 18874368 | bytes 4218880 | tf_op jit(solution)/shard_map/jit(_where)/select_n | solution.py:37
  64.6 8.9 %all-to-all-done = bf16[32,2,2048]{2,1,0:T(2,128)(2,1)S(1)} async-done(((bf16[32,2,2048]{2,1,0:T(2,128)(2,1)}), bf16[32,2,2048]{2,1,0:T(2,128)(2,1)S(1)}, u32[]{:S(2)}, u32[]{:S(2)}) %all-to-all-start) | async-done | bytes 262176 | tf_op jit(solution)/shard_map/all_to_all | solution.py:97
  73.6 0.4 reshape.51
  73.9 3.5 %fusion.126 = f32[1024,64]{1,0:T(8,128)S(1)} fusion(bf16[2048,1024]{1,0:T(8,128)(2,1)} %fusion.4, bf16[2048,64]{1,0:T(8,128)(2,1)S(1)} %bitcast.51), kind=kOutput, calls=%fused_computation.230 | convolution fusion | flops 268435456 | bytes 4718592 | tf_op jit(solution)/shard_map/dot_general | solution.py:103
  77.4 0.3 all_to_all.22
  77.7 25.0 %all_to_all.25 = f32[32,1,2048]{2,1,0:T(1,128)S(1)} all-to-all(f32[32,1,2048]{2,1,0:T(1,128)S(1)} %all_to_all.22), channel_id=1, replica_groups=mesh['dir'=32,'tile'=32] {'tile'}, dimensions={0} | all-to-all | bytes 524288 | tf_op jit(solution)/shard_map/all_to_all | solution.py:107
  102.7 0.2 reduce_sum.11
  102.8 0.7 reduce_sum.12
  (47 shorter events, 1.3 us)
Async XLA Ops:
  0.6 31.4 %copy-start.4 = (bf16[4,2,32,256]{3,2,1,0:T(8,128)(2,1)S(1)}, bf16[4,2,32,256]{3,2,1,0:T(8,128)(2,1)}, u32[]{:S(2)}) copy-start(bf16[4,2,32,256]{3,2,1,0:T(8,128)(2,1)} %param.12) | copy-start | bytes 393220
  0.6 28.5 %copy-start.5 = (bf16[64,32,4]{0,2,1:T(4,128)(2,1)S(1)}, bf16[64,32,4]{0,2,1:T(4,128)(2,1)}, u32[]{:S(2)}) copy-start(bf16[64,32,4]{0,2,1:T(4,128)(2,1)} %param.15) | copy-start | bytes 49156
  0.7 28.6 %copy-start.6 = (s32[64,32]{0,1:T(8,128)S(1)}, s32[64,32]{0,1:T(8,128)}, u32[]{:S(2)}) copy-start(s32[64,32]{0,1:T(8,128)} %param.14) | copy-start | bytes 24580
  0.7 28.6 %copy-start.7 = (s32[64,32,1]{0,2,1:T(1,128)S(1)}, s32[64,32,1]{0,2,1:T(1,128)}, u32[]{:S(2)}) copy-start(s32[64,32,1]{0,2,1:T(1,128)} %param.13) | copy-start | bytes 24580
  1.7 32.3 %copy-start.1 = (bf16[2,32,8,256]{3,2,1,0:T(8,128)(2,1)S(1)}, bf16[2,32,8,256]{3,2,1,0:T(8,128)(2,1)}, u32[]{:S(2)}) copy-start(bf16[2,32,8,256]{3,2,1,0:T(8,128)(2,1)} %param.10) | copy-start | bytes 786436
  2.8 27.4 %collective-permute-start.3 = (bf16[2,12,12,256]{3,2,1,0:T(8,128)(2,1)S(1)}, bf16[2,12,12,256]{3,2,1,0:T(8,128)(2,1)}, u32[]{:S(2)}, u32[]{:S(2)}) collective-permute-start(bf16[2,12,12,256]{3,2,1,0:T(8,128)(2,1)S(1)} %pad_maximum_fusion.4), channel_id=1, source_target_pairs={{1,0},{2,1},{3,2},{4,3},{5,4},{6,5},{7,6},{8,7},{9,8},{10,9},{11,1... | collective-permute-start | bytes 442376 | tf_op jit(solution)/shard_map/ppermute | solution.py:45
  18.4 12.7 %collective-permute-start.2 = (bf16[2,12,12,256]{3,2,1,0:T(8,128)(2,1)}, bf16[2,12,12,256]{3,2,1,0:T(8,128)(2,1)}, u32[]{:S(2)}, u32[]{:S(2)}) collective-permute-start(bf16[2,12,12,256]{3,2,1,0:T(8,128)(2,1)} %pad_maximum_fusion.3), channel_id=1, source_target_pairs={{0,1},{1,2},{2,3},{3,4},{4,5},{5,6},{6,7},{7,8},{8,9},{9,10},{10,1... | collective-permute-start | bytes 442376 | tf_op jit(solution)/shard_map/ppermute | solution.py:45
  21.4 16.2 %copy-start = (f32[2,32,8,256]{3,2,1,0:T(8,128)S(1)}, f32[2,32,8,256]{3,2,1,0:T(8,128)}, u32[]{:S(2)}) copy-start(f32[2,32,8,256]{3,2,1,0:T(8,128)} %param.9) | copy-start | bytes 1572868
  22.6 11.6 %collective-permute-start.1 = (f32[2,28,8,256]{3,2,1,0:T(8,128)S(1)}, f32[2,28,8,256]{3,2,1,0:T(8,128)S(1)}, u32[]{:S(2)}, u32[]{:S(2)}) collective-permute-start(f32[2,28,8,256]{3,2,1,0:T(8,128)S(1)} %pad_maximum_fusion.2), channel_id=1, source_target_pairs={{1,0},{2,1},{3,2},{4,3},{5,4},{6,5},{7,6},{8,7},{9,8},{10,9},{11,1... | collective-permute-start | bytes 1376264 | tf_op jit(solution)/shard_map/ppermute | solution.py:45
  27.2 10.4 %collective-permute-start = (f32[2,28,8,256]{3,2,1,0:T(8,128)S(1)}, f32[2,28,8,256]{3,2,1,0:T(8,128)S(1)}, u32[]{:S(2)}, u32[]{:S(2)}) collective-permute-start(f32[2,28,8,256]{3,2,1,0:T(8,128)S(1)} %pad_maximum_fusion.1), channel_id=1, source_target_pairs={{0,1},{1,2},{2,3},{3,4},{4,5},{5,6},{6,7},{7,8},{8,9},{9,10},{10,1... | collective-permute-start | bytes 1376264 | tf_op jit(solution)/shard_map/ppermute | solution.py:45
  29.7 8.0 %copy-start.2 = (f32[2,32,8,256]{3,2,1,0:T(8,128)S(1)}, f32[2,32,8,256]{3,2,1,0:T(8,128)}, u32[]{:S(2)}) copy-start(f32[2,32,8,256]{3,2,1,0:T(8,128)} %param.8) | copy-start | bytes 1572868
  42.0 1.7 %copy-start.3 = (bf16[4,2,32,8,256]{4,3,2,1,0:T(8,128)(2,1)S(1)}, bf16[4,2,32,8,256]{4,3,2,1,0:T(8,128)(2,1)}, u32[]{:S(2)}) copy-start(bf16[4,2,32,8,256]{4,3,2,1,0:T(8,128)(2,1)} %param.11) | copy-start | bytes 3145732
  47.4 26.1 %all-to-all-start = ((bf16[32,2,2048]{2,1,0:T(2,128)(2,1)}), bf16[32,2,2048]{2,1,0:T(2,128)(2,1)S(1)}, u32[]{:S(2)}, u32[]{:S(2)}) async-start(bf16[32,2,2048]{2,1,0:T(2,128)(2,1)} %reshape.50), calls=%async_computation | async-start | bytes 524288 | tf_op jit(solution)/shard_map/all_to_all | solution.py:97

commit v5 on v4

--- a/solution.py
+++ b/solution.py
@@ -99,7 +99,7 @@
     got = got.reshape(all_dirs * rows_here, cols)
     owner = row_owner[:, :, 0]
     mt = band_matrix(owner, band_start, band_weight, n_tiles, rows_here)
-    mt = lax.optimization_barrier(mt.reshape(all_dirs * rows_here, n_tiles * rows_here))
+    mt = mt.reshape(all_dirs * rows_here, n_tiles * rows_here)
     partial = lax.dot_general(
         mt, got, (((0,), (0,)), ((), ())), preferred_element_type=jnp.float32
     )

time: 104 us -> 101 us (0.971)
  waiting for transfers between devices: 12.4 us -> 18.2 us
  other arithmetic: 14.1 us -> 8.51 us
  local copies, waits for them, and re-layouts: 11.9 us -> 7.13 us
  starting transfers between devices: 35.6 us -> 39.6 us
  blocking collectives: 25 us -> 22.6 us
    all_to_all x1, starting transfers between devices: 12.3 us -> 17.4 us  [per_device(): got = lax.all_to_all(blocks, 'dir', split_axis=2, concat_axis=0, tiled=True)]
    select_n x1 -> x0, other arithmetic: 4.93 us -> none  [band_matrix(): out = jnp.where(diff == k, wide[:, :, k:k + 1], out)]
    all_to_all x1, waiting for transfers between devices: 8.93 us -> 13 us  [per_device(): got = lax.all_to_all(blocks, 'dir', split_axis=2, concat_axis=0, tiled=True)]
    all_to_all x1, blocking collectives: 25 us -> 22.6 us  [per_device(): lax.all_to_all(partial, 'tile', split_axis=0, concat_axis=0, tiled=True)]
    ppermute x4, waiting for transfers between devices: 3.43 us -> 5.18 us  [exchange_halo(): return (lax.ppermute(tails, 'tile', up), lax.ppermute(heads, 'tile', down))]
    ppermute x4, starting transfers between devices: 23.3 us -> 22.2 us  [exchange_halo(): return (lax.ppermute(tails, 'tile', up), lax.ppermute(heads, 'tile', down))]
    slice x1, local copies, waits for them, and re-layouts: 1.13 us -> 0.04 us  [per_device(): receiver_now[:, -halo:]]
  transfers between devices with their start and end apart: 5 -> 5, of which waited for: 2 -> 3; matrix products, arithmetic and copies ran while one was open for 12% -> 1% of each run, Pallas kernels for 0% -> 0%
where the time goes in v5:
time: 101 us; the launch traced here: 100 us
  starting transfers between devices  39.6 us (39%)
  blocking collectives  22.6 us (22%)
  waiting for transfers between devices  18.2 us (18%)
  other arithmetic  8.51 us (8%)
  local copies, waits for them, and re-layouts  7.13 us (7%)
  matrix products  3.29 us (3%)
  between operations  1.08 us (1%)
    all_to_all x1, blocking collectives, per_device(): lax.all_to_all(partial, 'tile', split_axis=0, concat_axis=0, tiled=True)  22.6 us
    ppermute x4, starting transfers between devices, exchange_halo(): return (lax.ppermute(tails, 'tile', up), lax.ppermute(heads, 'tile', down))  22.2 us
    all_to_all x1, starting transfers between devices, per_device(): got = lax.all_to_all(blocks, 'dir', split_axis=2, concat_axis=0, tiled=True)  17.4 us
    all_to_all x1, waiting for transfers between devices, per_device(): got = lax.all_to_all(blocks, 'dir', split_axis=2, concat_axis=0, tiled=True)  13 us
    add x3, other arithmetic, per_device(): field_new = 2.0 * now_mid - old_mid + speed_mid * curvature  5.85 us
    ppermute x4, waiting for transfers between devices, exchange_halo(): return (lax.ppermute(tails, 'tile', up), lax.ppermute(heads, 'tile', down))  5.18 us
    unnamed x19, local copies, waits for them, and re-layouts  3.39 us
    dot_general x1, matrix products, per_device(): lax.dot_general(mt, got, (((0,), (0,)), ((), ())), preferred_element_type...  3.29 us
  transfers between devices with their start and end apart: 5, of which 3 were waited for; matrix products, arithmetic and copies ran while one was open for 1% of the time, Pallas kernels for 0%

profile of v5, /device:TPU:16, one launch (start us, length us, event | category | flops | bytes accessed | tf_op | source)
XLA Modules:
  0.0 100.4 jit_solution(846864274885833870)
XLA Ops:
  0.6 1.1 %copy.40 = bf16[4,2,32,256]{3,0,2,1:T(4,128)(2,1)S(1)} copy(bf16[4,2,32,256]{3,2,1,0:T(8,128)(2,1)} %param.12) | data formatting | bytes 262144 | tf_op args[4]
  1.8 1.0 %fusion.135 = (bf16[2,12,8,256]{3,2,1,0:T(8,128)(2,1)S(1)}, bf16[2,12,8,256]{3,2,1,0:T(8,128)(2,1)S(1)}) fusion(bf16[2,32,8,256]{3,2,1,0:T(8,128)(2,1)} %param.10), kind=kLoop, calls=%fused_computation.237 | loop fusion | bytes 393216 | tf_op jit(solution)/shard_map/slice | solution.py:61
  2.8 3.6 %collective-permute-start.2 = (bf16[2,12,12,256]{3,2,1,0:T(8,128)(2,1)S(1)}, bf16[2,12,12,256]{3,2,1,0:T(8,128)(2,1)S(1)}, u32[]{:S(2)}, u32[]{:S(2)}) collective-permute-start(bf16[2,12,12,256]{3,2,1,0:T(8,128)(2,1)S(1)} %pad_maximum_fusion.3), channel_id=1, source_target_pairs={{0,1},{1,2},{2,3},{3,4},{4,5},{5,6},{6,7},{7,8},{8,9},{9,10},{10,1... | collective-permute-start | bytes 442376 | tf_op jit(solution)/shard_map/ppermute | solution.py:45
  6.5 12.6 %collective-permute-start.3 = (bf16[2,12,12,256]{3,2,1,0:T(8,128)(2,1)S(1)}, bf16[2,12,12,256]{3,2,1,0:T(8,128)(2,1)S(1)}, u32[]{:S(2)}, u32[]{:S(2)}) collective-permute-start(bf16[2,12,12,256]{3,2,1,0:T(8,128)(2,1)S(1)} %pad_maximum_fusion.4), channel_id=1, source_target_pairs={{1,0},{2,1},{3,2},{4,3},{5,4},{6,5},{7,6},{8,7},{9,8},{10,9},{11,1... | collective-permute-start | bytes 442376 | tf_op jit(solution)/shard_map/ppermute | solution.py:45
  19.2 2.1 %collective-permute-start = (f32[2,28,8,256]{3,2,1,0:T(8,128)S(1)}, f32[2,28,8,256]{3,2,1,0:T(8,128)S(1)}, u32[]{:S(2)}, u32[]{:S(2)}) collective-permute-start(f32[2,28,8,256]{3,2,1,0:T(8,128)S(1)} %pad_maximum_fusion.1), channel_id=1, source_target_pairs={{0,1},{1,2},{2,3},{3,4},{4,5},{5,6},{6,7},{7,8},{8,9},{9,10},{10,1... | collective-permute-start | bytes 1376264 | tf_op jit(solution)/shard_map/ppermute | solution.py:45
  21.3 3.9 %collective-permute-start.1 = (f32[2,28,8,256]{3,2,1,0:T(8,128)S(1)}, f32[2,28,8,256]{3,2,1,0:T(8,128)S(1)}, u32[]{:S(2)}, u32[]{:S(2)}) collective-permute-start(f32[2,28,8,256]{3,2,1,0:T(8,128)S(1)} %pad_maximum_fusion.2), channel_id=1, source_target_pairs={{1,0},{2,1},{3,2},{4,3},{5,4},{6,5},{7,6},{8,7},{9,8},{10,9},{11,1... | collective-permute-start | bytes 1376264 | tf_op jit(solution)/shard_map/ppermute | solution.py:45
  25.6 0.8 copy-done.1
  26.5 3.2 %collective-permute-done = f32[2,28,8,256]{3,2,1,0:T(8,128)S(1)} collective-permute-done((f32[2,28,8,256]{3,2,1,0:T(8,128)S(1)}, f32[2,28,8,256]{3,2,1,0:T(8,128)S(1)}, u32[]{:S(2)}, u32[]{:S(2)}) %collective-permute-start) | collective-permute-done | bytes 458784 | tf_op jit(solution)/shard_map/ppermute | solution.py:45
  29.7 1.9 %collective-permute-done.1 = f32[2,28,8,256]{3,2,1,0:T(8,128)S(1)} collective-permute-done((f32[2,28,8,256]{3,2,1,0:T(8,128)S(1)}, f32[2,28,8,256]{3,2,1,0:T(8,128)S(1)}, u32[]{:S(2)}, u32[]{:S(2)}) %collective-permute-start.1) | collective-permute-done | bytes 458784 | tf_op jit(solution)/shard_map/ppermute | solution.py:45
  31.8 2.3 %fusion.26 = f32[2,56,8,256]{3,2,1,0:T(8,128)S(1)} fusion(f32[2,64,8,256]{3,2,1,0:T(8,128)S(1)} %pad_maximum_fusion, f32[2,12,8,256]{3,2,1,0:T(8,128)S(1)} %slice.598, f32[2,32,8,256]{3,2,1,0:T(8,128)S(1)} %copy-done.2, f32[2,12,8,256]{3,2,1,0:T(8,128)S(1)} %slice.597, f32[2,56,256]{2,1,0:T(8,128)S(1)} %get-tuple-element.11, ...), kind=kLoop, calls=%fused_computation.91 | loop fusion | flops 9175040 | bytes 11715072 | tf_op jit(solution)/shard_map/add | solution.py:87
  34.1 1.9 %fusion.53 = f32[2,48,8,256]{3,2,1,0:T(8,128)S(1)} fusion(f32[2,56,8,256]{3,2,1,0:T(8,128)S(1)} %fusion.26, f32[2,56,8,256]{3,2,1,0:T(8,128)S(1)} %maximum_convert_fusion, f32[2,64,8,256]{3,2,1,0:T(8,128)S(1)} %pad_maximum_fusion, f32[2,48,256]{2,1,0:T(8,128)S(1)} %slice.626, pred[8]{0:T(512)(128)(4,1)S(1)} %iota_compare_fusion), kind=kLoop, calls=%fused_computation.123 | loop fusion | flops 6881280 | bytes 10453504 | tf_op jit(solution)/shard_map/add | solution.py:87
  36.1 1.6 %fusion.80 = f32[2,40,8,256]{3,2,1,0:T(8,128)S(1)} fusion(f32[2,48,8,256]{3,2,1,0:T(8,128)S(1)} %fusion.53, f32[2,56,8,256]{3,2,1,0:T(8,128)S(1)} %maximum_convert_fusion, f32[2,56,8,256]{3,2,1,0:T(8,128)S(1)} %fusion.26, f32[2,40,256]{2,1,0:T(8,128)S(1)} %slice.639, pred[8]{0:T(512)(128)(4,1)S(1)} %iota_compare_fusion), kind=kLoop, calls=%fused_computation.155 | loop fusion | flops 5734400 | bytes 8733184 | tf_op jit(solution)/shard_map/add | solution.py:87
  37.7 2.2 %fusion.126 = (bf16[2,32,8,256]{3,2,1,0:T(8,128)(2,1)S(1)}, f32[2,32,8,256]{3,2,1,0:T(8,128)}) fusion(f32[2,56,8,256]{3,2,1,0:T(8,128)S(1)} %fusion.26, f32[2,48,8,256]{3,2,1,0:T(8,128)S(1)} %fusion.53, f32[2,40,8,256]{3,2,1,0:T(8,128)S(1)} %fusion.80, bf16[4,2,32,8,256]{4,3,2,1,0:T(8,128)(2,1)S(1)} %copy-done.3, f32[2,32,256]{2,1,0:T(8,128)S(1)} %slice.652, ...), kind=kLoop, calls=%fused_computation.207 | loop fusion | flops 6160384 | bytes 8847872 | tf_op jit(solution)/shard_map/convert_element_type | solution.py:92
  39.9 0.2 reshape_reshape.3
  40.2 0.2 copy.41
  40.4 1.1 %reshape.50 = bf16[32,2,2048]{2,1,0:T(2,128)(2,1)} reshape(bf16[32,2,32,64]{3,2,1,0:T(8,128)(2,1)S(1)} %bitcast.50) | data formatting | bytes 524288
  41.5 17.4 %all-to-all-start = ((bf16[32,2,2048]{2,1,0:T(2,128)(2,1)}), bf16[32,2,2048]{2,1,0:T(2,128)(2,1)S(1)}, u32[]{:S(2)}, u32[]{:S(2)}) async-start(bf16[32,2,2048]{2,1,0:T(2,128)(2,1)} %reshape.50), calls=%async_computation | async-start | bytes 524288 | tf_op jit(solution)/shard_map/all_to_all | solution.py:97
  59.0 0.1 copy.30
  59.1 0.1 broadcast_in_dim.138
  59.2 0.1 copy.31
  59.3 0.1 broadcast_in_dim.140
  59.3 0.1 copy.32
  59.4 0.1 broadcast_in_dim.142
  59.5 0.1 copy.33
  59.6 0.1 broadcast_in_dim.144
  59.9 13.0 %all-to-all-done = bf16[32,2,2048]{2,1,0:T(2,128)(2,1)S(1)} async-done(((bf16[32,2,2048]{2,1,0:T(2,128)(2,1)}), bf16[32,2,2048]{2,1,0:T(2,128)(2,1)S(1)}, u32[]{:S(2)}, u32[]{:S(2)}) %all-to-all-start) | async-done | bytes 262176 | tf_op jit(solution)/shard_map/all_to_all | solution.py:97
  72.9 0.4 reshape.51
  73.3 3.3 %fusion.8 = f32[1024,64]{1,0:T(8,128)S(1)} fusion(bf16[2048,64]{1,0:T(8,128)(2,1)S(1)} %bitcast.51, s32[2048]{0:T(1024)S(1)} %sub.33, bf16[2048]{0:T(1024)(128)(2,1)S(1)} %broadcast_in_dim.144, bf16[2048]{0:T(1024)(128)(2,1)S(1)} %broadcast_in_dim.142, bf16[2048]{0:T(1024)(128)(2,1)S(1)} %broadcast_in_dim.140, bf16[2048]{0:T(1024)(128)(2,1)S(1)} %broadcast_in_dim.138), kind=kOutput, calls=%fused_computation.73 | convolution fusion | flops 287309824 | bytes 548864 | tf_op jit(solution)/shard_map/dot_general | solution.py:103
  76.6 0.3 all_to_all.22
  76.9 22.6 %all_to_all.25 = f32[32,1,2048]{2,1,0:T(1,128)S(1)} all-to-all(f32[32,1,2048]{2,1,0:T(1,128)S(1)} %all_to_all.22), channel_id=1, replica_groups=mesh['dir'=32,'tile'=32] {'tile'}, dimensions={0} | all-to-all | bytes 524288 | tf_op jit(solution)/shard_map/all_to_all | solution.py:107
  99.6 0.2 reduce_sum.11
  99.7 0.7 reduce_sum.12
  (46 shorter events, 0.9 us)
Async XLA Ops:
  0.6 18.4 %copy-start = (f32[2,32,8,256]{3,2,1,0:T(8,128)S(1)}, f32[2,32,8,256]{3,2,1,0:T(8,128)}, u32[]{:S(2)}) copy-start(f32[2,32,8,256]{3,2,1,0:T(8,128)} %param.9) | copy-start | bytes 1572868
  1.8 17.4 %copy-start.2 = (f32[2,32,8,256]{3,2,1,0:T(8,128)S(1)}, f32[2,32,8,256]{3,2,1,0:T(8,128)}, u32[]{:S(2)}) copy-start(f32[2,32,8,256]{3,2,1,0:T(8,128)} %param.8) | copy-start | bytes 1572868
  2.8 22.5 %collective-permute-start.2 = (bf16[2,12,12,256]{3,2,1,0:T(8,128)(2,1)S(1)}, bf16[2,12,12,256]{3,2,1,0:T(8,128)(2,1)S(1)}, u32[]{:S(2)}, u32[]{:S(2)}) collective-permute-start(bf16[2,12,12,256]{3,2,1,0:T(8,128)(2,1)S(1)} %pad_maximum_fusion.3), channel_id=1, source_target_pairs={{0,1},{1,2},{2,3},{3,4},{4,5},{5,6},{6,7},{7,8},{8,9},{9,10},{10,1... | collective-permute-start | bytes 442376 | tf_op jit(solution)/shard_map/ppermute | solution.py:45
  6.5 18.9 %collective-permute-start.3 = (bf16[2,12,12,256]{3,2,1,0:T(8,128)(2,1)S(1)}, bf16[2,12,12,256]{3,2,1,0:T(8,128)(2,1)S(1)}, u32[]{:S(2)}, u32[]{:S(2)}) collective-permute-start(bf16[2,12,12,256]{3,2,1,0:T(8,128)(2,1)S(1)} %pad_maximum_fusion.4), channel_id=1, source_target_pairs={{1,0},{2,1},{3,2},{4,3},{5,4},{6,5},{7,6},{8,7},{9,8},{10,9},{11,1... | collective-permute-start | bytes 442376 | tf_op jit(solution)/shard_map/ppermute | solution.py:45
  19.2 6.2 %copy-start.4 = (bf16[4,2,32,256]{3,2,1,0:T(8,128)(2,1)S(1)}, bf16[4,2,32,256]{3,2,1,0:T(8,128)(2,1)}, u32[]{:S(2)}) copy-start(bf16[4,2,32,256]{3,2,1,0:T(8,128)(2,1)} %param.12) | copy-start | bytes 393220
  19.2 10.5 %collective-permute-start = (f32[2,28,8,256]{3,2,1,0:T(8,128)S(1)}, f32[2,28,8,256]{3,2,1,0:T(8,128)S(1)}, u32[]{:S(2)}, u32[]{:S(2)}) collective-permute-start(f32[2,28,8,256]{3,2,1,0:T(8,128)S(1)} %pad_maximum_fusion.1), channel_id=1, source_target_pairs={{0,1},{1,2},{2,3},{3,4},{4,5},{5,6},{6,7},{7,8},{8,9},{9,10},{10,1... | collective-permute-start | bytes 1376264 | tf_op jit(solution)/shard_map/ppermute | solution.py:45
  21.3 10.4 %collective-permute-start.1 = (f32[2,28,8,256]{3,2,1,0:T(8,128)S(1)}, f32[2,28,8,256]{3,2,1,0:T(8,128)S(1)}, u32[]{:S(2)}, u32[]{:S(2)}) collective-permute-start(f32[2,28,8,256]{3,2,1,0:T(8,128)S(1)} %pad_maximum_fusion.2), channel_id=1, source_target_pairs={{1,0},{2,1},{3,2},{4,3},{5,4},{6,5},{7,6},{8,7},{9,8},{10,9},{11,1... | collective-permute-start | bytes 1376264 | tf_op jit(solution)/shard_map/ppermute | solution.py:45
  25.5 1.0 copy-start.1
  36.1 1.7 %copy-start.3 = (bf16[4,2,32,8,256]{4,3,2,1,0:T(8,128)(2,1)S(1)}, bf16[4,2,32,8,256]{4,3,2,1,0:T(8,128)(2,1)}, u32[]{:S(2)}) copy-start(bf16[4,2,32,8,256]{4,3,2,1,0:T(8,128)(2,1)} %param.11) | copy-start | bytes 3145732
  40.1 18.8 %copy-start.5 = (bf16[64,32,4]{0,2,1:T(4,128)(2,1)S(1)}, bf16[64,32,4]{0,2,1:T(4,128)(2,1)}, u32[]{:S(2)}) copy-start(bf16[64,32,4]{0,2,1:T(4,128)(2,1)} %param.15) | copy-start | bytes 49156
  40.4 19.4 %copy-start.6 = (s32[64,32]{0,1:T(8,128)S(1)}, s32[64,32]{0,1:T(8,128)}, u32[]{:S(2)}) copy-start(s32[64,32]{0,1:T(8,128)} %param.14) | copy-start | bytes 24580
  40.4 19.4 %copy-start.7 = (s32[64,32,1]{0,2,1:T(1,128)S(1)}, s32[64,32,1]{0,2,1:T(1,128)}, u32[]{:S(2)}) copy-start(s32[64,32,1]{0,2,1:T(1,128)} %param.13) | copy-start | bytes 24580
  41.5 31.4 %all-to-all-start = ((bf16[32,2,2048]{2,1,0:T(2,128)(2,1)}), bf16[32,2,2048]{2,1,0:T(2,128)(2,1)S(1)}, u32[]{:S(2)}, u32[]{:S(2)}) async-start(bf16[32,2,2048]{2,1,0:T(2,128)(2,1)} %reshape.50), calls=%async_computation | async-start | bytes 524288 | tf_op jit(solution)/shard_map/all_to_all | solution.py:97

commit v6 on v5

--- a/solution.py
+++ b/solution.py
@@ -52,23 +52,25 @@
     reach = 4
     halo = reach * STEPS
     old_halo = halo - reach
-    wide_before, wide_after = exchange_halo(
-        jnp.concatenate([receiver_now[:, -halo:], receiver_old[:, -old_halo:]], axis=1),
-        jnp.concatenate([receiver_now[:, :halo], receiver_old[:, :old_halo]], axis=1),
+    traces = jnp.pad(jnp.moveaxis(recorded, 0, 2), ((0, 0), (0, 0), (0, depth - STEPS), (0, 0)))
+    last_static = jnp.concatenate([courant[:, -old_halo:], traces[:, -old_halo:]], axis=1)
+    first_static = jnp.concatenate([courant[:, :old_halo], traces[:, :old_halo]], axis=1)
+    before, after = exchange_halo(
+        jnp.concatenate(
+            [receiver_now[:, -halo:], receiver_old[:, -old_halo:], last_static.astype(jnp.float32)], axis=1
+        ),
+        jnp.concatenate(
+            [receiver_now[:, :halo], receiver_old[:, :old_halo], first_static.astype(jnp.float32)], axis=1
+        ),
     )
-    traces = jnp.moveaxis(recorded, 0, 2)
-    narrow_before, narrow_after = exchange_halo(
-        jnp.concatenate([courant[:, -old_halo:], traces[:, -old_halo:]], axis=2),
-        jnp.concatenate([courant[:, :old_halo], traces[:, :old_halo]], axis=2),
-    )
-    now_b, old_b = wide_before[:, :halo], wide_before[:, halo:]
-    now_a, old_a = wide_after[:, :halo], wide_after[:, halo:]
-    c_b, rec_b = narrow_before[:, :, :depth], jnp.moveaxis(narrow_before[:, :, depth:], 2, 0)
-    c_a, rec_a = narrow_after[:, :, :depth], jnp.moveaxis(narrow_after[:, :, depth:], 2, 0)
+    edges = (halo, halo + old_halo, halo + 2 * old_halo)
+    now_b, old_b, c_b, rec_b = jnp.split(before, edges, axis=1)
+    now_a, old_a, c_a, rec_a = jnp.split(after, edges, axis=1)
     field_now = jnp.concatenate([now_b, receiver_now, now_a], axis=1)
     field_old = jnp.concatenate([old_b, receiver_old, old_a], axis=1)
-    speed_wide = jnp.concatenate([c_b, courant, c_a], axis=1).astype(jnp.float32)
-    rec_wide = jnp.concatenate([rec_b, recorded, rec_a], axis=2).astype(jnp.float32)
+    speed_wide = jnp.concatenate([c_b, courant.astype(jnp.float32), c_a], axis=1)
+    rec_wide = jnp.concatenate([rec_b, traces.astype(jnp.float32), rec_a], axis=1)
+    rec_wide = jnp.moveaxis(rec_wide[:, :, :STEPS], 2, 0)
     plane = lax.broadcasted_iota(jnp.int32, (1, 1, depth, 1), 2)
     image_sum = jnp.zeros(receiver_now.shape, jnp.float32)
     for step in range(STEPS):

time: 101 us -> 104 us (1.030)
  waiting for transfers between devices: 18.2 us -> 25.3 us
  starting transfers between devices: 39.6 us -> 33.9 us
  blocking collectives: 22.6 us -> 23.9 us
    ppermute x4 -> x2, waiting for transfers between devices: 5.18 us -> 12.5 us  [exchange_halo(): return (lax.ppermute(tails, 'tile', up), lax.ppermute(heads, 'tile', down))]
    ppermute x4 -> x2, starting transfers between devices: 22.2 us -> 16.8 us  [exchange_halo(): return (lax.ppermute(tails, 'tile', up), lax.ppermute(heads, 'tile', down))]
    all_to_all x1, blocking collectives: 22.6 us -> 23.9 us  [per_device(): lax.all_to_all(partial, 'tile', split_axis=0, concat_axis=0, tiled=True)]
    slice x7 -> x0, local copies, waits for them, and re-layouts: 1.1 us -> none  [the longest x1 1.02 us: per_device(): courant[:, -old_halo:]]
    unnamed x19 -> x21, local copies, waits for them, and re-layouts: 3.39 us -> 3.57 us
  transfers between devices with their start and end apart: 5 -> 3, of which waited for: 3 -> 3; matrix products, arithmetic and copies ran while one was open for 1% -> 1% of each run, Pallas kernels for 0% -> 0%
where the time goes in v6:
time: 104 us
  starting transfers between devices  33.9 us (33%)
  waiting for transfers between devices  25.3 us (24%)
  blocking collectives  23.9 us (23%)
  other arithmetic  8.69 us (8%)
  local copies, waits for them, and re-layouts  7.61 us (7%)
  matrix products  3.29 us (3%)
  between operations  1.04 us (1%)
    all_to_all x1, blocking collectives, per_device(): lax.all_to_all(partial, 'tile', split_axis=0, concat_axis=0, tiled=True)  23.9 us
    all_to_all x1, starting transfers between devices, per_device(): got = lax.all_to_all(blocks, 'dir', split_axis=2, concat_axis=0, tiled=True)  17.1 us
    ppermute x2, starting transfers between devices, exchange_halo(): return (lax.ppermute(tails, 'tile', up), lax.ppermute(heads, 'tile', down))  16.8 us
    all_to_all x1, waiting for transfers between devices, per_device(): got = lax.all_to_all(blocks, 'dir', split_axis=2, concat_axis=0, tiled=True)  12.8 us
    ppermute x2, waiting for transfers between devices, exchange_halo(): return (lax.ppermute(tails, 'tile', up), lax.ppermute(heads, 'tile', down))  12.5 us
    add x3, other arithmetic, per_device(): field_new = 2.0 * now_mid - old_mid + speed_mid * curvature  5.86 us
    unnamed x21, local copies, waits for them, and re-layouts  3.57 us
    dot_general x1, matrix products, per_device(): lax.dot_general(mt, got, (((0,), (0,)), ((), ())), preferred_element_type...  3.29 us
  transfers between devices with their start and end apart: 3, of which 3 were waited for; matrix products, arithmetic and copies ran while one was open for 1% of the time, Pallas kernels for 0%

profile of v6, /device:TPU:16, one launch (start us, length us, event | category | flops | bytes accessed | tf_op | source)
XLA Modules:
  0.0 103.7 jit_solution(18044984834064213912)
XLA Ops:
  0.7 1.1 %copy.42 = bf16[4,2,32,256]{3,0,2,1:T(4,128)(2,1)S(1)} copy(bf16[4,2,32,256]{3,2,1,0:T(8,128)(2,1)} %param.12) | data formatting | bytes 262144 | tf_op args[4]
  1.7 1.1 %fusion.137 = (f32[2,12,8,256]{3,2,1,0:T(8,128)S(1)}, f32[2,12,8,256]{3,2,1,0:T(8,128)S(1)}) fusion(f32[2,32,8,256]{3,2,1,0:T(8,128)} %param.8), kind=kLoop, calls=%fused_computation.241 | loop fusion | bytes 786432 | tf_op jit(solution)/shard_map/slice | solution.py:60
  3.0 14.9 %collective-permute-start.1 = (f32[2,52,8,256]{3,2,1,0:T(8,128)S(1)}, f32[2,52,8,256]{3,2,1,0:T(8,128)S(1)}, u32[]{:S(2)}, u32[]{:S(2)}) collective-permute-start(f32[2,52,8,256]{3,2,1,0:T(8,128)S(1)} %pad_maximum_fusion.3), channel_id=1, source_target_pairs={{1,0},{2,1},{3,2},{4,3},{5,4},{6,5},{7,6},{8,7},{9,8},{10,9},{11,1... | collective-permute-start | bytes 2555912 | tf_op jit(solution)/shard_map/ppermute | solution.py:45
  18.0 1.9 %collective-permute-start = (f32[2,52,8,256]{3,2,1,0:T(8,128)S(1)}, f32[2,52,8,256]{3,2,1,0:T(8,128)S(1)}, u32[]{:S(2)}, u32[]{:S(2)}) collective-permute-start(f32[2,52,8,256]{3,2,1,0:T(8,128)S(1)} %pad_maximum_fusion.2), channel_id=1, source_target_pairs={{0,1},{1,2},{2,3},{3,4},{4,5},{5,6},{6,7},{7,8},{8,9},{9,10},{10,1... | collective-permute-start | bytes 2555912 | tf_op jit(solution)/shard_map/ppermute | solution.py:45
  20.1 8.0 %collective-permute-done.1 = f32[2,52,8,256]{3,2,1,0:T(8,128)S(1)} collective-permute-done((f32[2,52,8,256]{3,2,1,0:T(8,128)S(1)}, f32[2,52,8,256]{3,2,1,0:T(8,128)S(1)}, u32[]{:S(2)}, u32[]{:S(2)}) %collective-permute-start.1) | collective-permute-done | bytes 852000 | tf_op jit(solution)/shard_map/ppermute | solution.py:45
  28.2 4.4 %collective-permute-done = f32[2,52,8,256]{3,2,1,0:T(8,128)S(1)} collective-permute-done((f32[2,52,8,256]{3,2,1,0:T(8,128)S(1)}, f32[2,52,8,256]{3,2,1,0:T(8,128)S(1)}, u32[]{:S(2)}, u32[]{:S(2)}) %collective-permute-start) | collective-permute-done | bytes 852000 | tf_op jit(solution)/shard_map/ppermute | solution.py:45
  32.7 0.3 fusion.138
  33.4 1.0 copy-done.2
  34.4 2.3 %fusion.26 = f32[2,56,8,256]{3,2,1,0:T(8,128)S(1)} fusion(f32[2,64,8,256]{3,2,1,0:T(8,128)S(1)} %pad_maximum_fusion, f32[2,12,8,256]{3,2,1,0:T(8,128)S(1)} %get-tuple-element.9, f32[2,32,8,256]{3,2,1,0:T(8,128)S(1)} %copy-done.2, f32[2,12,8,256]{3,2,1,0:T(8,128)S(1)} %get-tuple-element.6, f32[2,56,256]{2,1,0:T(8,128)S(1)} %bitcast.56, ...), kind=kLoop, calls=%fused_computation.91 | loop fusion | flops 8945664 | bytes 12173824 | tf_op jit(solution)/shard_map/add | solution.py:89
  36.6 1.9 %fusion.53 = f32[2,48,8,256]{3,2,1,0:T(8,128)S(1)} fusion(f32[2,56,8,256]{3,2,1,0:T(8,128)S(1)} %fusion.26, f32[2,56,8,256]{3,2,1,0:T(8,128)S(1)} %pad_maximum_fusion.1, f32[2,64,8,256]{3,2,1,0:T(8,128)S(1)} %pad_maximum_fusion, f32[2,48,256]{2,1,0:T(8,128)S(1)} %slice.584, pred[8]{0:T(512)(128)(4,1)S(1)} %iota_compare_fusion), kind=kLoop, calls=%fused_computation.126 | loop fusion | flops 6881280 | bytes 10453504 | tf_op jit(solution)/shard_map/add | solution.py:89
  38.6 1.7 %fusion.80 = f32[2,40,8,256]{3,2,1,0:T(8,128)S(1)} fusion(f32[2,48,8,256]{3,2,1,0:T(8,128)S(1)} %fusion.53, f32[2,56,8,256]{3,2,1,0:T(8,128)S(1)} %pad_maximum_fusion.1, f32[2,56,8,256]{3,2,1,0:T(8,128)S(1)} %fusion.26, f32[2,40,256]{2,1,0:T(8,128)S(1)} %slice.597, pred[8]{0:T(512)(128)(4,1)S(1)} %iota_compare_fusion), kind=kLoop, calls=%fused_computation.158 | loop fusion | flops 5734400 | bytes 8733184 | tf_op jit(solution)/shard_map/add | solution.py:89
  40.3 2.2 %fusion.126 = (bf16[2,32,8,256]{3,2,1,0:T(8,128)(2,1)S(1)}, f32[2,32,8,256]{3,2,1,0:T(8,128)}) fusion(f32[2,56,8,256]{3,2,1,0:T(8,128)S(1)} %fusion.26, f32[2,48,8,256]{3,2,1,0:T(8,128)S(1)} %fusion.53, f32[2,40,8,256]{3,2,1,0:T(8,128)S(1)} %fusion.80, bf16[4,2,32,8,256]{4,3,2,1,0:T(8,128)(2,1)S(1)} %copy-done.3, f32[2,32,256]{2,1,0:T(8,128)S(1)} %slice.609, ...), kind=kLoop, calls=%fused_computation.210 | loop fusion | flops 6291456 | bytes 8585728 | tf_op jit(solution)/shard_map/convert_element_type | solution.py:94
  42.5 0.2 reshape_reshape.3
  42.8 0.2 copy.47
  43.0 1.1 %reshape.50 = bf16[32,2,2048]{2,1,0:T(2,128)(2,1)} reshape(bf16[32,2,32,64]{3,2,1,0:T(8,128)(2,1)S(1)} %bitcast.52) | data formatting | bytes 524288
  44.1 17.1 %all-to-all-start = ((bf16[32,2,2048]{2,1,0:T(2,128)(2,1)}), bf16[32,2,2048]{2,1,0:T(2,128)(2,1)S(1)}, u32[]{:S(2)}, u32[]{:S(2)}) async-start(bf16[32,2,2048]{2,1,0:T(2,128)(2,1)} %reshape.50), calls=%async_computation | async-start | bytes 524288 | tf_op jit(solution)/shard_map/all_to_all | solution.py:99
  61.2 0.1 copy.23
  61.4 0.1 copy.24
  61.5 0.1 broadcast_in_dim.138
  61.6 0.1 copy.25
  61.7 0.1 broadcast_in_dim.140
  61.8 0.1 copy.27
  61.9 0.1 broadcast_in_dim.144
  62.0 0.1 copy.26
  62.1 0.1 broadcast_in_dim.142
  62.2 12.8 %all-to-all-done = bf16[32,2,2048]{2,1,0:T(2,128)(2,1)S(1)} async-done(((bf16[32,2,2048]{2,1,0:T(2,128)(2,1)}), bf16[32,2,2048]{2,1,0:T(2,128)(2,1)S(1)}, u32[]{:S(2)}, u32[]{:S(2)}) %all-to-all-start) | async-done | bytes 262176 | tf_op jit(solution)/shard_map/all_to_all | solution.py:99
  75.0 0.4 reshape.51
  75.4 3.3 %fusion.8 = f32[1024,64]{1,0:T(8,128)S(1)} fusion(bf16[2048,64]{1,0:T(8,128)(2,1)S(1)} %bitcast.55, s32[2048]{0:T(1024)S(1)} %sub.33, bf16[2048]{0:T(1024)(128)(2,1)S(1)} %broadcast_in_dim.144, bf16[2048]{0:T(1024)(128)(2,1)S(1)} %broadcast_in_dim.142, bf16[2048]{0:T(1024)(128)(2,1)S(1)} %broadcast_in_dim.140, bf16[2048]{0:T(1024)(128)(2,1)S(1)} %broadcast_in_dim.138), kind=kOutput, calls=%fused_computation.73 | convolution fusion | flops 287309824 | bytes 548864 | tf_op jit(solution)/shard_map/dot_general | solution.py:105
  78.7 0.3 all_to_all.22
  79.0 23.9 %all_to_all.25 = f32[32,1,2048]{2,1,0:T(1,128)S(1)} all-to-all(f32[32,1,2048]{2,1,0:T(1,128)S(1)} %all_to_all.22), channel_id=1, replica_groups=mesh['dir'=32,'tile'=32] {'tile'}, dimensions={0} | all-to-all | bytes 524288 | tf_op jit(solution)/shard_map/all_to_all | solution.py:109
  102.9 0.2 reduce_sum.11
  103.0 0.7 reduce_sum.12
  (39 shorter events, 0.9 us)
Async XLA Ops:
  0.6 2.2 %copy-start = (f32[2,32,8,256]{3,2,1,0:T(8,128)S(1)}, f32[2,32,8,256]{3,2,1,0:T(8,128)}, u32[]{:S(2)}) copy-start(f32[2,32,8,256]{3,2,1,0:T(8,128)} %param.9) | copy-start | bytes 1572868
  0.6 2.2 %copy-start.1 = (bf16[2,32,8,256]{3,2,1,0:T(8,128)(2,1)S(1)}, bf16[2,32,8,256]{3,2,1,0:T(8,128)(2,1)}, u32[]{:S(2)}) copy-start(bf16[2,32,8,256]{3,2,1,0:T(8,128)(2,1)} %param.10) | copy-start | bytes 786436
  3.0 25.1 %collective-permute-start.1 = (f32[2,52,8,256]{3,2,1,0:T(8,128)S(1)}, f32[2,52,8,256]{3,2,1,0:T(8,128)S(1)}, u32[]{:S(2)}, u32[]{:S(2)}) collective-permute-start(f32[2,52,8,256]{3,2,1,0:T(8,128)S(1)} %pad_maximum_fusion.3), channel_id=1, source_target_pairs={{1,0},{2,1},{3,2},{4,3},{5,4},{6,5},{7,6},{8,7},{9,8},{10,9},{11,1... | collective-permute-start | bytes 2555912 | tf_op jit(solution)/shard_map/ppermute | solution.py:45
  18.0 14.6 %collective-permute-start = (f32[2,52,8,256]{3,2,1,0:T(8,128)S(1)}, f32[2,52,8,256]{3,2,1,0:T(8,128)S(1)}, u32[]{:S(2)}, u32[]{:S(2)}) collective-permute-start(f32[2,52,8,256]{3,2,1,0:T(8,128)S(1)} %pad_maximum_fusion.2), channel_id=1, source_target_pairs={{0,1},{1,2},{2,3},{3,4},{4,5},{5,6},{6,7},{7,8},{8,9},{9,10},{10,1... | collective-permute-start | bytes 2555912 | tf_op jit(solution)/shard_map/ppermute | solution.py:45
  33.3 1.0 %copy-start.2 = (f32[2,32,8,256]{3,2,1,0:T(8,128)S(1)}, f32[2,32,8,256]{3,2,1,0:T(8,128)}, u32[]{:S(2)}) copy-start(f32[2,32,8,256]{3,2,1,0:T(8,128)} %param.8) | copy-start | bytes 1572868
  38.6 1.7 %copy-start.3 = (bf16[4,2,32,8,256]{4,3,2,1,0:T(8,128)(2,1)S(1)}, bf16[4,2,32,8,256]{4,3,2,1,0:T(8,128)(2,1)}, u32[]{:S(2)}) copy-start(bf16[4,2,32,8,256]{4,3,2,1,0:T(8,128)(2,1)} %param.11) | copy-start | bytes 3145732
  42.7 18.4 %copy-start.5 = (s32[64,32]{0,1:T(8,128)S(1)}, s32[64,32]{0,1:T(8,128)}, u32[]{:S(2)}) copy-start(s32[64,32]{0,1:T(8,128)} %param.14) | copy-start | bytes 24580
  42.7 18.4 %copy-start.6 = (s32[64,32,1]{0,2,1:T(1,128)S(1)}, s32[64,32,1]{0,2,1:T(1,128)}, u32[]{:S(2)}) copy-start(s32[64,32,1]{0,2,1:T(1,128)} %param.13) | copy-start | bytes 24580
  42.7 18.6 %copy-start.4 = (bf16[64,32,4]{0,2,1:T(4,128)(2,1)S(1)}, bf16[64,32,4]{0,2,1:T(4,128)(2,1)}, u32[]{:S(2)}) copy-start(bf16[64,32,4]{0,2,1:T(4,128)(2,1)} %param.15) | copy-start | bytes 49156
  44.1 30.9 %all-to-all-start = ((bf16[32,2,2048]{2,1,0:T(2,128)(2,1)}), bf16[32,2,2048]{2,1,0:T(2,128)(2,1)S(1)}, u32[]{:S(2)}, u32[]{:S(2)}) async-start(bf16[32,2,2048]{2,1,0:T(2,128)(2,1)} %reshape.50), calls=%async_computation | async-start | bytes 524288 | tf_op jit(solution)/shard_map/all_to_all | solution.py:99

commit v7 on v5

--- a/solution.py
+++ b/solution.py
@@ -45,32 +45,12 @@
     return lax.ppermute(tails, "tile", up), lax.ppermute(heads, "tile", down)
 
 
-def per_device(
-    receiver_old, receiver_now, courant, source_snaps, recorded, row_owner, band_start, band_weight
-):
-    local_dirs, rows_here, depth, across = receiver_now.shape
+def run_steps(field_now, field_old, speed_wide, rec_wide, snaps, rows_here):
     reach = 4
     halo = reach * STEPS
-    old_halo = halo - reach
-    wide_before, wide_after = exchange_halo(
-        jnp.concatenate([receiver_now[:, -halo:], receiver_old[:, -old_halo:]], axis=1),
-        jnp.concatenate([receiver_now[:, :halo], receiver_old[:, :old_halo]], axis=1),
-    )
-    traces = jnp.moveaxis(recorded, 0, 2)
-    narrow_before, narrow_after = exchange_halo(
-        jnp.concatenate([courant[:, -old_halo:], traces[:, -old_halo:]], axis=2),
-        jnp.concatenate([courant[:, :old_halo], traces[:, :old_halo]], axis=2),
-    )
-    now_b, old_b = wide_before[:, :halo], wide_before[:, halo:]
-    now_a, old_a = wide_after[:, :halo], wide_after[:, halo:]
-    c_b, rec_b = narrow_before[:, :, :depth], jnp.moveaxis(narrow_before[:, :, depth:], 2, 0)
-    c_a, rec_a = narrow_after[:, :, :depth], jnp.moveaxis(narrow_after[:, :, depth:], 2, 0)
-    field_now = jnp.concatenate([now_b, receiver_now, now_a], axis=1)
-    field_old = jnp.concatenate([old_b, receiver_old, old_a], axis=1)
-    speed_wide = jnp.concatenate([c_b, courant, c_a], axis=1).astype(jnp.float32)
-    rec_wide = jnp.concatenate([rec_b, recorded, rec_a], axis=2).astype(jnp.float32)
+    _, _, depth, across = field_now.shape
     plane = lax.broadcasted_iota(jnp.int32, (1, 1, depth, 1), 2)
-    image_sum = jnp.zeros(receiver_now.shape, jnp.float32)
+    image_sum = jnp.zeros((field_now.shape[0], rows_here, depth, across), jnp.float32)
     for step in range(STEPS):
         ext_in = halo - reach * step
         ext_out = ext_in - reach
@@ -85,10 +65,56 @@
         old_mid = field_old[:, old_off : old_off + rows_out]
         speed_mid = speed_wide[:, lo : lo + rows_out]
         field_new = 2.0 * now_mid - old_mid + speed_mid * curvature
-        image_sum = image_sum + source_snaps[step].astype(jnp.float32) * field_new[
+        image_sum = image_sum + snaps[step].astype(jnp.float32) * field_new[
             :, ext_out : ext_out + rows_here
         ]
         field_old, field_now = (field_now, field_new)
+    return field_now, image_sum
+
+
+def per_device(
+    receiver_old, receiver_now, courant, source_snaps, recorded, row_owner, band_start, band_weight
+):
+    local_dirs, rows_here, depth, across = receiver_now.shape
+    reach = 4
+    halo = reach * STEPS
+    old_halo = halo - reach
+    traces = jnp.moveaxis(recorded, 0, 2)
+    narrow_before, narrow_after = exchange_halo(
+        jnp.concatenate([courant[:, -old_halo:], traces[:, -old_halo:]], axis=2),
+        jnp.concatenate([courant[:, :old_halo], traces[:, :old_halo]], axis=2),
+    )
+    c_b, rec_b = narrow_before[:, :, :depth], jnp.moveaxis(narrow_before[:, :, depth:], 2, 0)
+    c_a, rec_a = narrow_after[:, :, :depth], jnp.moveaxis(narrow_after[:, :, depth:], 2, 0)
+    speed_all = jnp.concatenate([c_b, courant, c_a], axis=1).astype(jnp.float32)
+    rec_all = jnp.concatenate([rec_b, recorded, rec_a], axis=2).astype(jnp.float32)
+    fields = []
+    images = []
+    for d in range(local_dirs):
+        now_d = receiver_now[d : d + 1]
+        old_d = receiver_old[d : d + 1]
+        wide_before, wide_after = exchange_halo(
+            jnp.concatenate([now_d[:, -halo:], old_d[:, -old_halo:]], axis=1),
+            jnp.concatenate([now_d[:, :halo], old_d[:, :old_halo]], axis=1),
+        )
+        if fields:
+            fields[-1], images[-1], wide_before, wide_after = lax.optimization_barrier(
+                (fields[-1], images[-1], wide_before, wide_after)
+            )
+        field_now = jnp.concatenate([wide_before[:, :halo], now_d, wide_after[:, :halo]], axis=1)
+        field_old = jnp.concatenate([wide_before[:, halo:], old_d, wide_after[:, halo:]], axis=1)
+        field_now, image_d = run_steps(
+            field_now,
+            field_old,
+            speed_all[d : d + 1],
+            rec_all[:, d : d + 1],
+            source_snaps[:, d : d + 1],
+            rows_here,
+        )
+        fields.append(field_now)
+        images.append(image_d)
+    field_now = jnp.concatenate(fields, axis=0)
+    image_sum = jnp.concatenate(images, axis=0)
     image_flat = image_sum.astype(jnp.bfloat16).reshape(local_dirs, rows_here, depth * across)
     n_dir = lax.axis_size("dir")
     n_tiles = lax.axis_size("tile")

time: 101 us -> 102 us (level)
  blocking collectives: 22.6 us -> 0 us
  starting transfers between devices: 39.6 us -> 53.4 us
  waiting for transfers between devices: 18.2 us -> 23.4 us
  local copies, waits for them, and re-layouts: 7.13 us -> 11.6 us
    all_to_all x1 -> x0, blocking collectives: 22.6 us -> none  [per_device(): lax.all_to_all(partial, 'tile', split_axis=0, concat_axis=0, tiled=True)]
    all_to_all x0 -> x1, starting transfers between devices: none -> 13.2 us  [per_device(): lax.all_to_all(partial, 'tile', split_axis=0, concat_axis=0, tiled=True)]
    all_to_all x0 -> x1, waiting for transfers between devices: none -> 10.7 us  [per_device(): lax.all_to_all(partial, 'tile', split_axis=0, concat_axis=0, tiled=True)]
    ppermute x4 -> x6, starting transfers between devices: 22.2 us -> 28.5 us  [exchange_halo(): return (lax.ppermute(tails, 'tile', up), lax.ppermute(heads, 'tile', down))]
    all_to_all x1, starting transfers between devices: 17.4 us -> 11.8 us  [per_device(): got = lax.all_to_all(blocks, 'dir', split_axis=2, concat_axis=0, tiled=True)]
    ppermute x4 -> x6, waiting for transfers between devices: 5.18 us -> 0.02 us  [exchange_halo(): return (lax.ppermute(tails, 'tile', up), lax.ppermute(heads, 'tile', down))]
    convert_element_type x2 -> x1, other arithmetic: 2.24 us -> 0.07 us  [per_device(): speed_all = jnp.concatenate([c_b, courant, c_a], axis=1).astype(jnp.float32)]
    broadcast_in_dim x0 -> x6, local copies, waits for them, and re-layouts: none -> 1.88 us  [run_steps(): curvature = curvature + jnp.where(plane == 0, inject, 0.0)]
  transfers between devices with their start and end apart: 5 -> 8, of which waited for: 3 -> 2; matrix products, arithmetic and copies ran while one was open for 1% -> 8% of each run, Pallas kernels for 0% -> 0%
where the time goes in v7:
time: 102 us; the launch traced here: 101 us
  starting transfers between devices  53.4 us (52%)
  waiting for transfers between devices  23.4 us (23%)
  local copies, waits for them, and re-layouts  11.6 us (11%)
  other arithmetic  8.18 us (8%)
  matrix products  3.29 us (3%)
  between operations  1.29 us (1%)
    ppermute x6, starting transfers between devices, exchange_halo(): return (lax.ppermute(tails, 'tile', up), lax.ppermute(heads, 'tile', down))  28.5 us
    all_to_all x1, starting transfers between devices, per_device(): lax.all_to_all(partial, 'tile', split_axis=0, concat_axis=0, tiled=True)  13.2 us
    all_to_all x1, waiting for transfers between devices, per_device(): got = lax.all_to_all(blocks, 'dir', split_axis=2, concat_axis=0, tiled=True)  12.7 us
    all_to_all x1, starting transfers between devices, per_device(): got = lax.all_to_all(blocks, 'dir', split_axis=2, concat_axis=0, tiled=True)  11.8 us
    all_to_all x1, waiting for transfers between devices, per_device(): lax.all_to_all(partial, 'tile', split_axis=0, concat_axis=0, tiled=True)  10.7 us
    add x6, other arithmetic, run_steps(): field_new = 2.0 * now_mid - old_mid + speed_mid * curvature  5.33 us
    unnamed x31, local copies, waits for them, and re-layouts  3.76 us
    dot_general x1, matrix products, per_device(): lax.dot_general(mt, got, (((0,), (0,)), ((), ())), preferred_element_type...  3.29 us
  transfers between devices with their start and end apart: 8, of which 2 were waited for; matrix products, arithmetic and copies ran while one was open for 8% of the time, Pallas kernels for 0%

profile of v7, /device:TPU:16, one launch (start us, length us, event | category | flops | bytes accessed | tf_op | source)
XLA Modules:
  0.0 101.1 jit_solution(8703449763292455557)
XLA Ops:
  0.6 1.1 %copy.41 = bf16[4,2,32,256]{3,0,2,1:T(4,128)(2,1)S(1)} copy(bf16[4,2,32,256]{3,2,1,0:T(8,128)(2,1)} %param.12) | data formatting | bytes 262144 | tf_op args[4]
  1.8 1.0 fusion.249
  2.8 14.9 %collective-permute-start.3 = (bf16[2,12,12,256]{3,2,1,0:T(8,128)(2,1)S(1)}, bf16[2,12,12,256]{3,2,1,0:T(8,128)(2,1)S(1)}, u32[]{:S(2)}, u32[]{:S(2)}) collective-permute-start(bf16[2,12,12,256]{3,2,1,0:T(8,128)(2,1)S(1)} %pad_maximum_fusion.9), channel_id=1, source_target_pairs={{1,0},{2,1},{3,2},{4,3},{5,4},{6,5},{7,6},{8,7},{9,8},{10,9},{11,1... | collective-permute-start | bytes 442376 | tf_op jit(solution)/shard_map/ppermute | solution.py:45
  17.7 1.9 %collective-permute-start.2 = (bf16[2,12,12,256]{3,2,1,0:T(8,128)(2,1)S(1)}, bf16[2,12,12,256]{3,2,1,0:T(8,128)(2,1)S(1)}, u32[]{:S(2)}, u32[]{:S(2)}) collective-permute-start(bf16[2,12,12,256]{3,2,1,0:T(8,128)(2,1)S(1)} %pad_maximum_fusion.8), channel_id=1, source_target_pairs={{0,1},{1,2},{2,3},{3,4},{4,5},{5,6},{6,7},{7,8},{8,9},{9,10},{10,1... | collective-permute-start | bytes 442376 | tf_op jit(solution)/shard_map/ppermute | solution.py:45
  19.8 1.9 %collective-permute-start = (f32[1,28,8,256]{3,2,1,0:T(8,128)S(1)}, f32[1,28,8,256]{3,2,1,0:T(8,128)S(1)}, u32[]{:S(2)}, u32[]{:S(2)}) collective-permute-start(f32[1,28,8,256]{3,2,1,0:T(8,128)S(1)} %pad_maximum_fusion.4), channel_id=1, source_target_pairs={{0,1},{1,2},{2,3},{3,4},{4,5},{5,6},{6,7},{7,8},{8,9},{9,10},{10,1... | collective-permute-start | bytes 688136 | tf_op jit(solution)/shard_map/ppermute | solution.py:45
  21.8 3.9 %collective-permute-start.1 = (f32[1,28,8,256]{3,2,1,0:T(8,128)S(1)}, f32[1,28,8,256]{3,2,1,0:T(8,128)S(1)}, u32[]{:S(2)}, u32[]{:S(2)}) collective-permute-start(f32[1,28,8,256]{3,2,1,0:T(8,128)S(1)} %pad_maximum_fusion.5), channel_id=1, source_target_pairs={{1,0},{2,1},{3,2},{4,3},{5,4},{6,5},{7,6},{8,7},{9,8},{10,9},{11,1... | collective-permute-start | bytes 688136 | tf_op jit(solution)/shard_map/ppermute | solution.py:45
  25.7 1.9 %collective-permute-start.4 = (f32[1,28,8,256]{3,2,1,0:T(8,128)S(1)}, f32[1,28,8,256]{3,2,1,0:T(8,128)S(1)}, u32[]{:S(2)}, u32[]{:S(2)}) collective-permute-start(f32[1,28,8,256]{3,2,1,0:T(8,128)S(1)} %pad_maximum_fusion.6), channel_id=1, source_target_pairs={{0,1},{1,2},{2,3},{3,4},{4,5},{5,6},{6,7},{7,8},{8,9},{9,10},{10,1... | collective-permute-start | bytes 688136 | tf_op jit(solution)/shard_map/ppermute | solution.py:45
  27.8 3.9 %collective-permute-start.5 = (f32[1,28,8,256]{3,2,1,0:T(8,128)S(1)}, f32[1,28,8,256]{3,2,1,0:T(8,128)S(1)}, u32[]{:S(2)}, u32[]{:S(2)}) collective-permute-start(f32[1,28,8,256]{3,2,1,0:T(8,128)S(1)} %pad_maximum_fusion.7), channel_id=1, source_target_pairs={{1,0},{2,1},{3,2},{4,3},{5,4},{6,5},{7,6},{8,7},{9,8},{10,9},{11,1... | collective-permute-start | bytes 688136 | tf_op jit(solution)/shard_map/ppermute | solution.py:45
  31.9 0.6 slice_bitcast_fusion
  32.6 0.6 slice_bitcast_fusion.14
  33.2 0.6 slice_bitcast_fusion.12
  33.8 0.6 slice_bitcast_fusion.8
  34.7 1.0 %fusion.26 = f32[1,56,8,256]{3,2,1,0:T(8,128)S(1)} fusion(f32[1,64,8,256]{3,2,1,0:T(8,128)S(1)} %pad_maximum_fusion, f32[2,56,8,256]{3,2,1,0:T(8,128)S(1)} %maximum_convert_fusion, f32[1,12,8,256]{3,2,1,0:T(8,128)S(1)} %slice.1202, f32[1,32,8,256]{3,2,1,0:T(8,128)S(1)} %get-tuple-element.15, f32[1,12,8,256]{3,2,1,0:T(8,128)S(1)} %slice.1201, ...), kind=kLoop, calls=%fused_computation.158 | loop fusion | flops 4243456 | bytes 6087168 | tf_op jit(solution)/shard_map/add | solution.py:67
  35.7 0.9 fusion.80
  36.6 0.8 fusion.134
  37.4 0.5 copy-done.2
  37.9 0.7 fusion.237
  38.6 0.6 copy-done.5
  39.7 0.7 slice-done
  40.5 1.0 %fusion.53 = f32[1,56,8,256]{3,2,1,0:T(8,128)S(1)} fusion(f32[1,64,8,256]{3,2,1,0:T(8,128)S(1)} %pad_maximum_fusion.1, f32[2,56,8,256]{3,2,1,0:T(8,128)S(1)} %maximum_convert_fusion, f32[1,12,8,256]{3,2,1,0:T(8,128)S(1)} %slice-done.1, f32[1,32,8,256]{3,2,1,0:T(8,128)S(1)} %get-tuple-element.14, f32[1,12,8,256]{3,2,1,0:T(8,128)S(1)} %slice-done, ...), kind=kLoop, calls=%fused_computation.185 | loop fusion | flops 4243456 | bytes 6087168 | tf_op jit(solution)/shard_map/add | solution.py:67
  41.5 0.9 fusion.107
  42.4 0.8 fusion.161
  43.2 0.7 fusion.234
  44.3 1.1 %reshape.222 = bf16[32,2,2048]{2,1,0:T(2,128)(2,1)} reshape(bf16[32,2,32,64]{3,2,1,0:T(8,128)(2,1)S(1)} %fusion.252) | data formatting | bytes 524288
  45.5 11.8 %all-to-all-start = ((bf16[32,2,2048]{2,1,0:T(2,128)(2,1)}), bf16[32,2,2048]{2,1,0:T(2,128)(2,1)S(1)}, u32[]{:S(2)}, u32[]{:S(2)}) async-start(bf16[32,2,2048]{2,1,0:T(2,128)(2,1)} %reshape.222), calls=%async_computation | async-start | bytes 524288 | tf_op jit(solution)/shard_map/all_to_all | solution.py:123
  58.2 12.7 %all-to-all-done = bf16[32,2,2048]{2,1,0:T(2,128)(2,1)S(1)} async-done(((bf16[32,2,2048]{2,1,0:T(2,128)(2,1)}), bf16[32,2,2048]{2,1,0:T(2,128)(2,1)S(1)}, u32[]{:S(2)}, u32[]{:S(2)}) %all-to-all-start) | async-done | bytes 262176 | tf_op jit(solution)/shard_map/all_to_all | solution.py:123
  71.3 3.3 %fusion.8 = f32[1024,64]{1,0:T(8,128)S(1)} fusion(bf16[2048,64]{1,0:T(8,128)(2,1)S(1)} %bitcast.83, s32[2048]{0:T(1024)S(1)} %sub.49, bf16[2048]{0:T(1024)(128)(2,1)S(1)} %broadcast_in_dim.216, bf16[2048]{0:T(1024)(128)(2,1)S(1)} %broadcast_in_dim.214, bf16[2048]{0:T(1024)(128)(2,1)S(1)} %broadcast_in_dim.212, bf16[2048]{0:T(1024)(128)(2,1)S(1)} %broadcast_in_dim.210), kind=kOutput, calls=%fused_computation.137 | convolution fusion | flops 287309824 | bytes 548864 | tf_op jit(solution)/shard_map/dot_general | solution.py:129
  74.6 1.0 %all_to_all.22 = f32[32,1,2048]{2,1,0:T(1,128)} reshape(f32[1024,64]{1,0:T(8,128)S(1)} %fusion.8) | data formatting | bytes 524288 | tf_op jit(solution)/shard_map/all_to_all | solution.py:133
  75.6 13.2 %all-to-all-start.1 = ((f32[32,1,2048]{2,1,0:T(1,128)}), f32[32,1,2048]{2,1,0:T(1,128)S(1)}, u32[]{:S(2)}, u32[]{:S(2)}) async-start(f32[32,1,2048]{2,1,0:T(1,128)} %all_to_all.22), calls=%async_computation.1 | async-start | bytes 524288 | tf_op jit(solution)/shard_map/all_to_all | solution.py:133
  88.8 0.8 pad_maximum_fusion.2
  89.6 10.7 %all-to-all-done.1 = f32[32,1,2048]{2,1,0:T(1,128)S(1)} async-done(((f32[32,1,2048]{2,1,0:T(1,128)}), f32[32,1,2048]{2,1,0:T(1,128)S(1)}, u32[]{:S(2)}, u32[]{:S(2)}) %all-to-all-start.1) | async-done | bytes 262176 | tf_op jit(solution)/shard_map/all_to_all | solution.py:133
  100.4 0.7 reduce_sum.12
  (85 shorter events, 3.0 us)
Async XLA Ops:
  0.6 19.0 %copy-start.1 = (f32[2,32,8,256]{3,2,1,0:T(8,128)S(1)}, f32[2,32,8,256]{3,2,1,0:T(8,128)}, u32[]{:S(2)}) copy-start(f32[2,32,8,256]{3,2,1,0:T(8,128)} %param.8) | copy-start | bytes 1572868
  1.7 18.0 %copy-start = (f32[2,32,8,256]{3,2,1,0:T(8,128)S(1)}, f32[2,32,8,256]{3,2,1,0:T(8,128)}, u32[]{:S(2)}) copy-start(f32[2,32,8,256]{3,2,1,0:T(8,128)} %param.9) | copy-start | bytes 1572868
  2.8 25.0 %collective-permute-start.3 = (bf16[2,12,12,256]{3,2,1,0:T(8,128)(2,1)S(1)}, bf16[2,12,12,256]{3,2,1,0:T(8,128)(2,1)S(1)}, u32[]{:S(2)}, u32[]{:S(2)}) collective-permute-start(bf16[2,12,12,256]{3,2,1,0:T(8,128)(2,1)S(1)} %pad_maximum_fusion.9), channel_id=1, source_target_pairs={{1,0},{2,1},{3,2},{4,3},{5,4},{6,5},{7,6},{8,7},{9,8},{10,9},{11,1... | collective-permute-start | bytes 442376 | tf_op jit(solution)/shard_map/ppermute | solution.py:45
  17.7 14.0 %collective-permute-start.2 = (bf16[2,12,12,256]{3,2,1,0:T(8,128)(2,1)S(1)}, bf16[2,12,12,256]{3,2,1,0:T(8,128)(2,1)S(1)}, u32[]{:S(2)}, u32[]{:S(2)}) collective-permute-start(bf16[2,12,12,256]{3,2,1,0:T(8,128)(2,1)S(1)} %pad_maximum_fusion.8), channel_id=1, source_target_pairs={{0,1},{1,2},{2,3},{3,4},{4,5},{5,6},{6,7},{7,8},{8,9},{9,10},{10,1... | collective-permute-start | bytes 442376 | tf_op jit(solution)/shard_map/ppermute | solution.py:45
  19.8 14.8 %collective-permute-start = (f32[1,28,8,256]{3,2,1,0:T(8,128)S(1)}, f32[1,28,8,256]{3,2,1,0:T(8,128)S(1)}, u32[]{:S(2)}, u32[]{:S(2)}) collective-permute-start(f32[1,28,8,256]{3,2,1,0:T(8,128)S(1)} %pad_maximum_fusion.4), channel_id=1, source_target_pairs={{0,1},{1,2},{2,3},{3,4},{4,5},{5,6},{6,7},{7,8},{8,9},{9,10},{10,1... | collective-permute-start | bytes 688136 | tf_op jit(solution)/shard_map/ppermute | solution.py:45
  21.8 12.8 %collective-permute-start.1 = (f32[1,28,8,256]{3,2,1,0:T(8,128)S(1)}, f32[1,28,8,256]{3,2,1,0:T(8,128)S(1)}, u32[]{:S(2)}, u32[]{:S(2)}) collective-permute-start(f32[1,28,8,256]{3,2,1,0:T(8,128)S(1)} %pad_maximum_fusion.5), channel_id=1, source_target_pairs={{1,0},{2,1},{3,2},{4,3},{5,4},{6,5},{7,6},{8,7},{9,8},{10,9},{11,1... | collective-permute-start | bytes 688136 | tf_op jit(solution)/shard_map/ppermute | solution.py:45
  25.7 12.9 %collective-permute-start.4 = (f32[1,28,8,256]{3,2,1,0:T(8,128)S(1)}, f32[1,28,8,256]{3,2,1,0:T(8,128)S(1)}, u32[]{:S(2)}, u32[]{:S(2)}) collective-permute-start(f32[1,28,8,256]{3,2,1,0:T(8,128)S(1)} %pad_maximum_fusion.6), channel_id=1, source_target_pairs={{0,1},{1,2},{2,3},{3,4},{4,5},{5,6},{6,7},{7,8},{8,9},{9,10},{10,1... | collective-permute-start | bytes 688136 | tf_op jit(solution)/shard_map/ppermute | solution.py:45
  27.7 4.1 %copy-start.4 = (bf16[4,2,32,256]{3,2,1,0:T(8,128)(2,1)S(1)}, bf16[4,2,32,256]{3,2,1,0:T(8,128)(2,1)}, u32[]{:S(2)}) copy-start(bf16[4,2,32,256]{3,2,1,0:T(8,128)(2,1)} %param.12) | copy-start | bytes 393220
  27.8 10.8 %collective-permute-start.5 = (f32[1,28,8,256]{3,2,1,0:T(8,128)S(1)}, f32[1,28,8,256]{3,2,1,0:T(8,128)S(1)}, u32[]{:S(2)}, u32[]{:S(2)}) collective-permute-start(f32[1,28,8,256]{3,2,1,0:T(8,128)S(1)} %pad_maximum_fusion.7), channel_id=1, source_target_pairs={{1,0},{2,1},{3,2},{4,3},{5,4},{6,5},{7,6},{8,7},{9,8},{10,9},{11,1... | collective-permute-start | bytes 688136 | tf_op jit(solution)/shard_map/ppermute | solution.py:45
  31.8 2.6 %copy-start.3 = (bf16[2,32,8,256]{3,2,1,0:T(8,128)(2,1)S(1)}, bf16[2,32,8,256]{3,2,1,0:T(8,128)(2,1)}, u32[]{:S(2)}) copy-start(bf16[2,32,8,256]{3,2,1,0:T(8,128)(2,1)} %param.10) | copy-start | bytes 786436
  36.6 1.2 %copy-start.2 = (bf16[4,2,32,8,256]{4,3,2,1,0:T(8,128)(2,1)S(1)}, bf16[4,2,32,8,256]{4,3,2,1,0:T(8,128)(2,1)}, u32[]{:S(2)}) copy-start(bf16[4,2,32,8,256]{4,3,2,1,0:T(8,128)(2,1)} %param.11) | copy-start | bytes 3145732
  38.6 0.7 copy-start.5
  38.6 0.7 copy-start.6
  39.5 0.9 slice-start
  39.5 0.9 slice-start.1
  39.6 0.9 copy-start.7
  40.5 1.0 %copy-start.8 = (f32[48,256]{1,0:T(8,128)S(1)}, f32[48,256]{1,0:T(8,128)}, u32[]{:S(2)}) copy-start(f32[48,256]{1,0:T(8,128)} %slice_bitcast_fusion.8) | copy-start | bytes 147460
  41.5 0.9 copy-start.9
  42.4 0.8 copy-start.10
  44.2 13.0 %copy-start.12 = (s32[64,32]{0,1:T(8,128)S(1)}, s32[64,32]{0,1:T(8,128)}, u32[]{:S(2)}) copy-start(s32[64,32]{0,1:T(8,128)} %param.14) | copy-start | bytes 24580
  44.2 13.0 %copy-start.13 = (s32[64,32,1]{0,2,1:T(1,128)S(1)}, s32[64,32,1]{0,2,1:T(1,128)}, u32[]{:S(2)}) copy-start(s32[64,32,1]{0,2,1:T(1,128)} %param.13) | copy-start | bytes 24580
  44.2 13.2 %copy-start.11 = (bf16[64,32,4]{0,2,1:T(4,128)(2,1)S(1)}, bf16[64,32,4]{0,2,1:T(4,128)(2,1)}, u32[]{:S(2)}) copy-start(bf16[64,32,4]{0,2,1:T(4,128)(2,1)} %param.15) | copy-start | bytes 49156
  45.5 25.5 %all-to-all-start = ((bf16[32,2,2048]{2,1,0:T(2,128)(2,1)}), bf16[32,2,2048]{2,1,0:T(2,128)(2,1)S(1)}, u32[]{:S(2)}, u32[]{:S(2)}) async-start(bf16[32,2,2048]{2,1,0:T(2,128)(2,1)} %reshape.222), calls=%async_computation | async-start | bytes 524288 | tf_op jit(solution)/shard_map/all_to_all | solution.py:123
  75.6 24.7 %all-to-all-start.1 = ((f32[32,1,2048]{2,1,0:T(1,128)}), f32[32,1,2048]{2,1,0:T(1,128)S(1)}, u32[]{:S(2)}, u32[]{:S(2)}) async-start(f32[32,1,2048]{2,1,0:T(1,128)} %all_to_all.22), calls=%async_computation.1 | async-start | bytes 524288 | tf_op jit(solution)/shard_map/all_to_all | solution.py:133

commit v8 on v5

--- a/solution.py
+++ b/solution.py
@@ -56,15 +56,18 @@
         jnp.concatenate([receiver_now[:, -halo:], receiver_old[:, -old_halo:]], axis=1),
         jnp.concatenate([receiver_now[:, :halo], receiver_old[:, :old_halo]], axis=1),
     )
-    traces = jnp.moveaxis(recorded, 0, 2)
+    traces = jnp.moveaxis(recorded[: STEPS - 1], 0, 2)
     narrow_before, narrow_after = exchange_halo(
         jnp.concatenate([courant[:, -old_halo:], traces[:, -old_halo:]], axis=2),
         jnp.concatenate([courant[:, :old_halo], traces[:, :old_halo]], axis=2),
     )
     now_b, old_b = wide_before[:, :halo], wide_before[:, halo:]
     now_a, old_a = wide_after[:, :halo], wide_after[:, halo:]
-    c_b, rec_b = narrow_before[:, :, :depth], jnp.moveaxis(narrow_before[:, :, depth:], 2, 0)
-    c_a, rec_a = narrow_after[:, :, :depth], jnp.moveaxis(narrow_after[:, :, depth:], 2, 0)
+    unread = jnp.zeros((1, local_dirs, old_halo, across), recorded.dtype)
+    c_b = narrow_before[:, :, :depth]
+    c_a = narrow_after[:, :, :depth]
+    rec_b = jnp.concatenate([jnp.moveaxis(narrow_before[:, :, depth:], 2, 0), unread], axis=0)
+    rec_a = jnp.concatenate([jnp.moveaxis(narrow_after[:, :, depth:], 2, 0), unread], axis=0)
     field_now = jnp.concatenate([now_b, receiver_now, now_a], axis=1)
     field_old = jnp.concatenate([old_b, receiver_old, old_a], axis=1)
     speed_wide = jnp.concatenate([c_b, courant, c_a], axis=1).astype(jnp.float32)

time: 101 us -> 101 us (level)
    unnamed x19 -> x21, local copies, waits for them, and re-layouts: 3.39 us -> 2.43 us
where the time goes in v8:
time: 101 us; the launch traced here: 100 us
  starting transfers between devices  39.6 us (39%)
  blocking collectives  22.6 us (22%)
  waiting for transfers between devices  18.2 us (18%)
  other arithmetic  8.5 us (8%)
  local copies, waits for them, and re-layouts  7.1 us (7%)
  matrix products  3.29 us (3%)
  between operations  1.08 us (1%)
    all_to_all x1, blocking collectives, per_device(): lax.all_to_all(partial, 'tile', split_axis=0, concat_axis=0, tiled=True)  22.6 us
    ppermute x4, starting transfers between devices, exchange_halo(): return (lax.ppermute(tails, 'tile', up), lax.ppermute(heads, 'tile', down))  22.2 us
    all_to_all x1, starting transfers between devices, per_device(): got = lax.all_to_all(blocks, 'dir', split_axis=2, concat_axis=0, tiled=True)  17.4 us
    all_to_all x1, waiting for transfers between devices, per_device(): got = lax.all_to_all(blocks, 'dir', split_axis=2, concat_axis=0, tiled=True)  13 us
    add x3, other arithmetic, per_device(): field_new = 2.0 * now_mid - old_mid + speed_mid * curvature  5.85 us
    ppermute x4, waiting for transfers between devices, exchange_halo(): return (lax.ppermute(tails, 'tile', up), lax.ppermute(heads, 'tile', down))  5.18 us
    dot_general x1, matrix products, per_device(): lax.dot_general(mt, got, (((0,), (0,)), ((), ())), preferred_element_type...  3.29 us
    unnamed x21, local copies, waits for them, and re-layouts  2.43 us
  transfers between devices with their start and end apart: 5, of which 3 were waited for; matrix products, arithmetic and copies ran while one was open for 1% of the time, Pallas kernels for 0%

profile of v8, /device:TPU:16, one launch (start us, length us, event | category | flops | bytes accessed | tf_op | source)
XLA Modules:
  0.0 100.4 jit_solution(16167050894912667850)
XLA Ops:
  0.6 1.0 slice.469
  1.7 1.0 %fusion.140 = (bf16[2,12,8,256]{3,2,1,0:T(8,128)(2,1)S(1)}, bf16[2,12,8,256]{3,2,1,0:T(8,128)(2,1)S(1)}) fusion(bf16[2,32,8,256]{3,2,1,0:T(8,128)(2,1)} %param.10), kind=kLoop, calls=%fused_computation.243 | loop fusion | bytes 393216 | tf_op jit(solution)/shard_map/slice | solution.py:61
  2.8 3.6 %collective-permute-start.2 = (bf16[2,12,11,256]{3,2,1,0:T(8,128)(2,1)S(1)}, bf16[2,12,11,256]{3,2,1,0:T(8,128)(2,1)S(1)}, u32[]{:S(2)}, u32[]{:S(2)}) collective-permute-start(bf16[2,12,11,256]{3,2,1,0:T(8,128)(2,1)S(1)} %pad_maximum_fusion.3), channel_id=1, source_target_pairs={{0,1},{1,2},{2,3},{3,4},{4,5},{5,6},{6,7},{7,8},{8,9},{9,10},{10,1... | collective-permute-start | bytes 405512 | tf_op jit(solution)/shard_map/ppermute | solution.py:45
  6.4 12.6 %collective-permute-start.3 = (bf16[2,12,11,256]{3,2,1,0:T(8,128)(2,1)S(1)}, bf16[2,12,11,256]{3,2,1,0:T(8,128)(2,1)S(1)}, u32[]{:S(2)}, u32[]{:S(2)}) collective-permute-start(bf16[2,12,11,256]{3,2,1,0:T(8,128)(2,1)S(1)} %pad_maximum_fusion.4), channel_id=1, source_target_pairs={{1,0},{2,1},{3,2},{4,3},{5,4},{6,5},{7,6},{8,7},{9,8},{10,9},{11,1... | collective-permute-start | bytes 405512 | tf_op jit(solution)/shard_map/ppermute | solution.py:45
  19.2 2.1 %collective-permute-start = (f32[2,28,8,256]{3,2,1,0:T(8,128)S(1)}, f32[2,28,8,256]{3,2,1,0:T(8,128)S(1)}, u32[]{:S(2)}, u32[]{:S(2)}) collective-permute-start(f32[2,28,8,256]{3,2,1,0:T(8,128)S(1)} %pad_maximum_fusion.1), channel_id=1, source_target_pairs={{0,1},{1,2},{2,3},{3,4},{4,5},{5,6},{6,7},{7,8},{8,9},{9,10},{10,1... | collective-permute-start | bytes 1376264 | tf_op jit(solution)/shard_map/ppermute | solution.py:45
  21.3 3.9 %collective-permute-start.1 = (f32[2,28,8,256]{3,2,1,0:T(8,128)S(1)}, f32[2,28,8,256]{3,2,1,0:T(8,128)S(1)}, u32[]{:S(2)}, u32[]{:S(2)}) collective-permute-start(f32[2,28,8,256]{3,2,1,0:T(8,128)S(1)} %pad_maximum_fusion.2), channel_id=1, source_target_pairs={{1,0},{2,1},{3,2},{4,3},{5,4},{6,5},{7,6},{8,7},{9,8},{10,9},{11,1... | collective-permute-start | bytes 1376264 | tf_op jit(solution)/shard_map/ppermute | solution.py:45
  25.6 0.8 copy-done.1
  26.5 3.2 %collective-permute-done = f32[2,28,8,256]{3,2,1,0:T(8,128)S(1)} collective-permute-done((f32[2,28,8,256]{3,2,1,0:T(8,128)S(1)}, f32[2,28,8,256]{3,2,1,0:T(8,128)S(1)}, u32[]{:S(2)}, u32[]{:S(2)}) %collective-permute-start) | collective-permute-done | bytes 458784 | tf_op jit(solution)/shard_map/ppermute | solution.py:45
  29.7 1.9 %collective-permute-done.1 = f32[2,28,8,256]{3,2,1,0:T(8,128)S(1)} collective-permute-done((f32[2,28,8,256]{3,2,1,0:T(8,128)S(1)}, f32[2,28,8,256]{3,2,1,0:T(8,128)S(1)}, u32[]{:S(2)}, u32[]{:S(2)}) %collective-permute-start.1) | collective-permute-done | bytes 458784 | tf_op jit(solution)/shard_map/ppermute | solution.py:45
  31.8 2.3 %fusion.26 = f32[2,56,8,256]{3,2,1,0:T(8,128)S(1)} fusion(f32[2,64,8,256]{3,2,1,0:T(8,128)S(1)} %pad_maximum_fusion, f32[2,12,8,256]{3,2,1,0:T(8,128)S(1)} %slice.602, f32[2,32,8,256]{3,2,1,0:T(8,128)S(1)} %copy-done.2, f32[2,12,8,256]{3,2,1,0:T(8,128)S(1)} %slice.601, f32[2,56,256]{2,1,0:T(8,128)S(1)} %get-tuple-element.11, ...), kind=kLoop, calls=%fused_computation.91 | loop fusion | flops 9175040 | bytes 11715072 | tf_op jit(solution)/shard_map/add | solution.py:90
  34.1 1.9 %fusion.53 = f32[2,48,8,256]{3,2,1,0:T(8,128)S(1)} fusion(f32[2,56,8,256]{3,2,1,0:T(8,128)S(1)} %fusion.26, f32[2,56,8,256]{3,2,1,0:T(8,128)S(1)} %maximum_convert_fusion, f32[2,64,8,256]{3,2,1,0:T(8,128)S(1)} %pad_maximum_fusion, f32[2,48,256]{2,1,0:T(8,128)S(1)} %slice.630, pred[8]{0:T(512)(128)(4,1)S(1)} %iota_compare_fusion.2), kind=kLoop, calls=%fused_computation.123 | loop fusion | flops 6881280 | bytes 10453504 | tf_op jit(solution)/shard_map/add | solution.py:90
  36.1 1.6 %fusion.80 = f32[2,40,8,256]{3,2,1,0:T(8,128)S(1)} fusion(f32[2,48,8,256]{3,2,1,0:T(8,128)S(1)} %fusion.53, f32[2,56,8,256]{3,2,1,0:T(8,128)S(1)} %maximum_convert_fusion, f32[2,56,8,256]{3,2,1,0:T(8,128)S(1)} %fusion.26, f32[2,40,256]{2,1,0:T(8,128)S(1)} %slice.643, pred[8]{0:T(512)(128)(4,1)S(1)} %iota_compare_fusion.2), kind=kLoop, calls=%fused_computation.155 | loop fusion | flops 5734400 | bytes 8733184 | tf_op jit(solution)/shard_map/add | solution.py:90
  37.7 2.2 %fusion.126 = (bf16[2,32,8,256]{3,2,1,0:T(8,128)(2,1)S(1)}, f32[2,32,8,256]{3,2,1,0:T(8,128)}) fusion(f32[2,56,8,256]{3,2,1,0:T(8,128)S(1)} %fusion.26, f32[2,48,8,256]{3,2,1,0:T(8,128)S(1)} %fusion.53, f32[2,40,8,256]{3,2,1,0:T(8,128)S(1)} %fusion.80, bf16[4,2,32,8,256]{4,3,2,1,0:T(8,128)(2,1)S(1)} %copy-done.3, f32[2,32,256]{2,1,0:T(8,128)S(1)} %slice.656, ...), kind=kLoop, calls=%fused_computation.207 | loop fusion | flops 6160384 | bytes 8847872 | tf_op jit(solution)/shard_map/convert_element_type | solution.py:95
  39.9 0.2 reshape_reshape.3
  40.1 0.2 copy.44
  40.4 1.1 %reshape.50 = bf16[32,2,2048]{2,1,0:T(2,128)(2,1)} reshape(bf16[32,2,32,64]{3,2,1,0:T(8,128)(2,1)S(1)} %bitcast.50) | data formatting | bytes 524288
  41.5 17.4 %all-to-all-start = ((bf16[32,2,2048]{2,1,0:T(2,128)(2,1)}), bf16[32,2,2048]{2,1,0:T(2,128)(2,1)S(1)}, u32[]{:S(2)}, u32[]{:S(2)}) async-start(bf16[32,2,2048]{2,1,0:T(2,128)(2,1)} %reshape.50), calls=%async_computation | async-start | bytes 524288 | tf_op jit(solution)/shard_map/all_to_all | solution.py:100
  58.9 0.1 copy.30
  59.0 0.1 broadcast_in_dim.139
  59.1 0.1 copy.31
  59.2 0.1 broadcast_in_dim.141
  59.3 0.1 copy.32
  59.4 0.1 broadcast_in_dim.143
  59.5 0.1 copy.33
  59.6 0.1 broadcast_in_dim.145
  59.9 13.0 %all-to-all-done = bf16[32,2,2048]{2,1,0:T(2,128)(2,1)S(1)} async-done(((bf16[32,2,2048]{2,1,0:T(2,128)(2,1)}), bf16[32,2,2048]{2,1,0:T(2,128)(2,1)S(1)}, u32[]{:S(2)}, u32[]{:S(2)}) %all-to-all-start) | async-done | bytes 262176 | tf_op jit(solution)/shard_map/all_to_all | solution.py:100
  72.9 0.4 reshape.51
  73.3 3.3 %fusion.8 = f32[1024,64]{1,0:T(8,128)S(1)} fusion(bf16[2048,64]{1,0:T(8,128)(2,1)S(1)} %bitcast.51, s32[2048]{0:T(1024)S(1)} %sub.33, bf16[2048]{0:T(1024)(128)(2,1)S(1)} %broadcast_in_dim.145, bf16[2048]{0:T(1024)(128)(2,1)S(1)} %broadcast_in_dim.143, bf16[2048]{0:T(1024)(128)(2,1)S(1)} %broadcast_in_dim.141, bf16[2048]{0:T(1024)(128)(2,1)S(1)} %broadcast_in_dim.139), kind=kOutput, calls=%fused_computation.73 | convolution fusion | flops 287309824 | bytes 548864 | tf_op jit(solution)/shard_map/dot_general | solution.py:106
  76.6 0.3 all_to_all.22
  76.9 22.6 %all_to_all.25 = f32[32,1,2048]{2,1,0:T(1,128)S(1)} all-to-all(f32[32,1,2048]{2,1,0:T(1,128)S(1)} %all_to_all.22), channel_id=1, replica_groups=mesh['dir'=32,'tile'=32] {'tile'}, dimensions={0} | all-to-all | bytes 524288 | tf_op jit(solution)/shard_map/all_to_all | solution.py:110
  99.5 0.2 reduce_sum.11
  99.7 0.7 reduce_sum.12
  (47 shorter events, 1.0 us)
Async XLA Ops:
  0.6 18.4 %copy-start = (f32[2,32,8,256]{3,2,1,0:T(8,128)S(1)}, f32[2,32,8,256]{3,2,1,0:T(8,128)}, u32[]{:S(2)}) copy-start(f32[2,32,8,256]{3,2,1,0:T(8,128)} %param.9) | copy-start | bytes 1572868
  1.7 17.4 %copy-start.2 = (f32[2,32,8,256]{3,2,1,0:T(8,128)S(1)}, f32[2,32,8,256]{3,2,1,0:T(8,128)}, u32[]{:S(2)}) copy-start(f32[2,32,8,256]{3,2,1,0:T(8,128)} %param.8) | copy-start | bytes 1572868
  2.8 22.5 %collective-permute-start.2 = (bf16[2,12,11,256]{3,2,1,0:T(8,128)(2,1)S(1)}, bf16[2,12,11,256]{3,2,1,0:T(8,128)(2,1)S(1)}, u32[]{:S(2)}, u32[]{:S(2)}) collective-permute-start(bf16[2,12,11,256]{3,2,1,0:T(8,128)(2,1)S(1)} %pad_maximum_fusion.3), channel_id=1, source_target_pairs={{0,1},{1,2},{2,3},{3,4},{4,5},{5,6},{6,7},{7,8},{8,9},{9,10},{10,1... | collective-permute-start | bytes 405512 | tf_op jit(solution)/shard_map/ppermute | solution.py:45
  6.4 18.9 %collective-permute-start.3 = (bf16[2,12,11,256]{3,2,1,0:T(8,128)(2,1)S(1)}, bf16[2,12,11,256]{3,2,1,0:T(8,128)(2,1)S(1)}, u32[]{:S(2)}, u32[]{:S(2)}) collective-permute-start(bf16[2,12,11,256]{3,2,1,0:T(8,128)(2,1)S(1)} %pad_maximum_fusion.4), channel_id=1, source_target_pairs={{1,0},{2,1},{3,2},{4,3},{5,4},{6,5},{7,6},{8,7},{9,8},{10,9},{11,1... | collective-permute-start | bytes 405512 | tf_op jit(solution)/shard_map/ppermute | solution.py:45
  19.1 6.2 %copy-start.4 = (bf16[4,2,32,256]{3,2,1,0:T(8,128)(2,1)S(1)}, bf16[4,2,32,256]{3,2,1,0:T(8,128)(2,1)}, u32[]{:S(2)}) copy-start(bf16[4,2,32,256]{3,2,1,0:T(8,128)(2,1)} %param.12) | copy-start | bytes 393220
  19.2 10.5 %collective-permute-start = (f32[2,28,8,256]{3,2,1,0:T(8,128)S(1)}, f32[2,28,8,256]{3,2,1,0:T(8,128)S(1)}, u32[]{:S(2)}, u32[]{:S(2)}) collective-permute-start(f32[2,28,8,256]{3,2,1,0:T(8,128)S(1)} %pad_maximum_fusion.1), channel_id=1, source_target_pairs={{0,1},{1,2},{2,3},{3,4},{4,5},{5,6},{6,7},{7,8},{8,9},{9,10},{10,1... | collective-permute-start | bytes 1376264 | tf_op jit(solution)/shard_map/ppermute | solution.py:45
  21.3 10.4 %collective-permute-start.1 = (f32[2,28,8,256]{3,2,1,0:T(8,128)S(1)}, f32[2,28,8,256]{3,2,1,0:T(8,128)S(1)}, u32[]{:S(2)}, u32[]{:S(2)}) collective-permute-start(f32[2,28,8,256]{3,2,1,0:T(8,128)S(1)} %pad_maximum_fusion.2), channel_id=1, source_target_pairs={{1,0},{2,1},{3,2},{4,3},{5,4},{6,5},{7,6},{8,7},{9,8},{10,9},{11,1... | collective-permute-start | bytes 1376264 | tf_op jit(solution)/shard_map/ppermute | solution.py:45
  25.4 1.0 copy-start.1
  36.0 1.7 %copy-start.3 = (bf16[4,2,32,8,256]{4,3,2,1,0:T(8,128)(2,1)S(1)}, bf16[4,2,32,8,256]{4,3,2,1,0:T(8,128)(2,1)}, u32[]{:S(2)}) copy-start(bf16[4,2,32,8,256]{4,3,2,1,0:T(8,128)(2,1)} %param.11) | copy-start | bytes 3145732
  40.1 18.8 %copy-start.5 = (bf16[64,32,4]{0,2,1:T(4,128)(2,1)S(1)}, bf16[64,32,4]{0,2,1:T(4,128)(2,1)}, u32[]{:S(2)}) copy-start(bf16[64,32,4]{0,2,1:T(4,128)(2,1)} %param.15) | copy-start | bytes 49156
  40.3 19.4 %copy-start.6 = (s32[64,32]{0,1:T(8,128)S(1)}, s32[64,32]{0,1:T(8,128)}, u32[]{:S(2)}) copy-start(s32[64,32]{0,1:T(8,128)} %param.14) | copy-start | bytes 24580
  40.4 19.4 %copy-start.7 = (s32[64,32,1]{0,2,1:T(1,128)S(1)}, s32[64,32,1]{0,2,1:T(1,128)}, u32[]{:S(2)}) copy-start(s32[64,32,1]{0,2,1:T(1,128)} %param.13) | copy-start | bytes 24580
  41.5 31.4 %all-to-all-start = ((bf16[32,2,2048]{2,1,0:T(2,128)(2,1)}), bf16[32,2,2048]{2,1,0:T(2,128)(2,1)S(1)}, u32[]{:S(2)}, u32[]{:S(2)}) async-start(bf16[32,2,2048]{2,1,0:T(2,128)(2,1)} %reshape.50), calls=%async_computation | async-start | bytes 524288 | tf_op jit(solution)/shard_map/all_to_all | solution.py:100

commit v9 on v8

--- a/solution.py
+++ b/solution.py
@@ -101,10 +101,25 @@
     all_dirs = got.shape[0]
     got = got.reshape(all_dirs * rows_here, cols)
     owner = row_owner[:, :, 0]
-    mt = band_matrix(owner, band_start, band_weight, n_tiles, rows_here)
-    mt = mt.reshape(all_dirs * rows_here, n_tiles * rows_here)
-    partial = lax.dot_general(
-        mt, got, (((0,), (0,)), ((), ())), preferred_element_type=jnp.float32
+    capacity = max(2, 2 * rows_here // n_tiles)
+    hits = (owner[:, :, None] == jnp.arange(n_tiles, dtype=jnp.int32)[None, None, :]).astype(jnp.int32)
+    rank = jnp.sum((jnp.cumsum(hits, axis=1) - hits) * hits, axis=2)
+    slot = owner * capacity + rank
+    select = (
+        slot[:, None, :] == jnp.arange(n_tiles * capacity, dtype=jnp.int32)[None, :, None]
+    ).astype(jnp.bfloat16)
+    diff = jnp.arange(rows_here, dtype=jnp.int32)[None, None, :] - band_start[:, :, None]
+    wide = band_weight.astype(jnp.bfloat16)
+    band = jnp.where(diff == 0, wide[:, :, 0:1], jnp.zeros((), jnp.bfloat16))
+    for k in range(1, BAND):
+        band = jnp.where(diff == k, wide[:, :, k : k + 1], band)
+    got = got.reshape(all_dirs, rows_here, cols)
+    slot_rows = jnp.einsum("dsr,drc->dsc", select, got, preferred_element_type=jnp.float32)
+    slot_band = jnp.einsum("dsr,drj->dsj", select, band, preferred_element_type=jnp.float32)
+    slot_rows = slot_rows.astype(jnp.bfloat16).reshape(all_dirs, n_tiles, capacity, cols)
+    slot_band = slot_band.astype(jnp.bfloat16).reshape(all_dirs, n_tiles, capacity, rows_here)
+    partial = jnp.einsum(
+        "doqj,doqc->ojc", slot_band, slot_rows, preferred_element_type=jnp.float32
     )
     partial = partial.reshape(n_tiles, rows_here * cols)
     sent = lax.all_to_all(partial, "tile", split_axis=0, concat_axis=0, tiled=True)

time: 101 us -> 99.5 us (0.985)
  waiting for transfers between devices: 18.2 us -> 13.6 us
  other arithmetic: 8.5 us -> 11.4 us
    all_to_all x1, waiting for transfers between devices: 13 us -> 9.68 us  [per_device(): got = lax.all_to_all(blocks, 'dir', split_axis=2, concat_axis=0, tiled=True)]
    select_n x0 -> x1, other arithmetic: none -> 1.67 us  [per_device(): band = jnp.where(diff == k, wide[:, :, k:k + 1], band)]
    ppermute x4, waiting for transfers between devices: 5.18 us -> 3.9 us  [exchange_halo(): return (lax.ppermute(tails, 'tile', up), lax.ppermute(heads, 'tile', down))]
    another operation x0 -> x1, other arithmetic: none -> 1.17 us  [per_device(): rank = jnp.sum((jnp.cumsum(hits, axis=1) - hits) * hits, axis=2)]
    convert_element_type x0 -> x1, local copies, waits for them, and re-layouts: none -> 1.09 us  [per_device(): slot_band.astype(jnp.bfloat16)]
    dot_general x1 -> x3, matrix products: 3.29 us -> 3.55 us  [the longest x1 1.5 us: per_device(): jnp.einsum('dsr,drj->dsj', select, band, preferred_element_type=jnp.float32)]
  transfers between devices with their start and end apart: 5 -> 5, of which waited for: 3 -> 3; matrix products, arithmetic and copies ran while one was open for 1% -> 6% of each run, Pallas kernels for 0% -> 0%
where the time goes in v9:
time: 99.5 us; the launch traced here: 99.2 us
  starting transfers between devices  39.6 us (40%)
  blocking collectives  22.6 us (23%)
  waiting for transfers between devices  13.6 us (14%)
  other arithmetic  11.4 us (11%)
  local copies, waits for them, and re-layouts  7.36 us (7%)
  matrix products  3.55 us (4%)
  between operations  1.11 us (1%)
    all_to_all x1, blocking collectives, per_device(): lax.all_to_all(partial, 'tile', split_axis=0, concat_axis=0, tiled=True)  22.6 us
    ppermute x4, starting transfers between devices, exchange_halo(): return (lax.ppermute(tails, 'tile', up), lax.ppermute(heads, 'tile', down))  22.2 us
    all_to_all x1, starting transfers between devices, per_device(): got = lax.all_to_all(blocks, 'dir', split_axis=2, concat_axis=0, tiled=True)  17.4 us
    all_to_all x1, waiting for transfers between devices, per_device(): got = lax.all_to_all(blocks, 'dir', split_axis=2, concat_axis=0, tiled=True)  9.68 us
    add x3, other arithmetic, per_device(): field_new = 2.0 * now_mid - old_mid + speed_mid * curvature  5.85 us
    ppermute x4, waiting for transfers between devices, exchange_halo(): return (lax.ppermute(tails, 'tile', up), lax.ppermute(heads, 'tile', down))  3.9 us
    unnamed x21, local copies, waits for them, and re-layouts  2.43 us
    convert_element_type x1, other arithmetic, per_device(): image_sum.astype(jnp.bfloat16)  2.17 us
  transfers between devices with their start and end apart: 5, of which 3 were waited for; matrix products, arithmetic and copies ran while one was open for 6% of the time, Pallas kernels for 0%

profile of v9, /device:TPU:16, one launch (start us, length us, event | category | flops | bytes accessed | tf_op | source)
XLA Modules:
  0.0 99.2 jit_solution(4631433501072781703)
XLA Ops:
  0.6 1.0 slice.469
  1.6 0.1 copy.61
  1.7 1.0 %fusion.137 = (bf16[2,12,8,256]{3,2,1,0:T(8,128)(2,1)S(1)}, bf16[2,12,8,256]{3,2,1,0:T(8,128)(2,1)S(1)}) fusion(bf16[2,32,8,256]{3,2,1,0:T(8,128)(2,1)} %param.10), kind=kLoop, calls=%fused_computation.250 | loop fusion | bytes 393216 | tf_op jit(solution)/shard_map/slice | solution.py:61
  2.8 3.6 %collective-permute-start.2 = (bf16[2,12,11,256]{3,2,1,0:T(8,128)(2,1)S(1)}, bf16[2,12,11,256]{3,2,1,0:T(8,128)(2,1)S(1)}, u32[]{:S(2)}, u32[]{:S(2)}) collective-permute-start(bf16[2,12,11,256]{3,2,1,0:T(8,128)(2,1)S(1)} %pad_maximum_fusion.3), channel_id=1, source_target_pairs={{0,1},{1,2},{2,3},{3,4},{4,5},{5,6},{6,7},{7,8},{8,9},{9,10},{10,1... | collective-permute-start | bytes 405512 | tf_op jit(solution)/shard_map/ppermute | solution.py:45
  6.4 12.6 %collective-permute-start.3 = (bf16[2,12,11,256]{3,2,1,0:T(8,128)(2,1)S(1)}, bf16[2,12,11,256]{3,2,1,0:T(8,128)(2,1)S(1)}, u32[]{:S(2)}, u32[]{:S(2)}) collective-permute-start(bf16[2,12,11,256]{3,2,1,0:T(8,128)(2,1)S(1)} %pad_maximum_fusion.4), channel_id=1, source_target_pairs={{1,0},{2,1},{3,2},{4,3},{5,4},{6,5},{7,6},{8,7},{9,8},{10,9},{11,1... | collective-permute-start | bytes 405512 | tf_op jit(solution)/shard_map/ppermute | solution.py:45
  19.2 2.1 %collective-permute-start = (f32[2,28,8,256]{3,2,1,0:T(8,128)S(1)}, f32[2,28,8,256]{3,2,1,0:T(8,128)S(1)}, u32[]{:S(2)}, u32[]{:S(2)}) collective-permute-start(f32[2,28,8,256]{3,2,1,0:T(8,128)S(1)} %pad_maximum_fusion.1), channel_id=1, source_target_pairs={{0,1},{1,2},{2,3},{3,4},{4,5},{5,6},{6,7},{7,8},{8,9},{9,10},{10,1... | collective-permute-start | bytes 1376264 | tf_op jit(solution)/shard_map/ppermute | solution.py:45
  21.3 3.9 %collective-permute-start.1 = (f32[2,28,8,256]{3,2,1,0:T(8,128)S(1)}, f32[2,28,8,256]{3,2,1,0:T(8,128)S(1)}, u32[]{:S(2)}, u32[]{:S(2)}) collective-permute-start(f32[2,28,8,256]{3,2,1,0:T(8,128)S(1)} %pad_maximum_fusion.2), channel_id=1, source_target_pairs={{1,0},{2,1},{3,2},{4,3},{5,4},{6,5},{7,6},{8,7},{9,8},{10,9},{11,1... | collective-permute-start | bytes 1376264 | tf_op jit(solution)/shard_map/ppermute | solution.py:45
  25.3 1.2 %select_reduce_fusion = s32[64,32]{0,1:T(8,128)S(1)} fusion(s32[64,32]{0,1:T(8,128)S(1)} %bitcast.59), kind=kOutput, calls=%fused_computation.78 | output fusion | flops 2488320 | bytes 16384 | tf_op jit(solution)/shard_map/jit(cumsum)/reduce_window_sum | solution.py:106
  26.9 0.8 copy-done.1
  27.8 1.9 %collective-permute-done = f32[2,28,8,256]{3,2,1,0:T(8,128)S(1)} collective-permute-done((f32[2,28,8,256]{3,2,1,0:T(8,128)S(1)}, f32[2,28,8,256]{3,2,1,0:T(8,128)S(1)}, u32[]{:S(2)}, u32[]{:S(2)}) %collective-permute-start) | collective-permute-done | bytes 458784 | tf_op jit(solution)/shard_map/ppermute | solution.py:45
  29.7 1.9 %collective-permute-done.1 = f32[2,28,8,256]{3,2,1,0:T(8,128)S(1)} collective-permute-done((f32[2,28,8,256]{3,2,1,0:T(8,128)S(1)}, f32[2,28,8,256]{3,2,1,0:T(8,128)S(1)}, u32[]{:S(2)}, u32[]{:S(2)}) %collective-permute-start.1) | collective-permute-done | bytes 458784 | tf_op jit(solution)/shard_map/ppermute | solution.py:45
  31.7 0.1 pad_maximum_fusion
  31.8 2.3 %fusion.24 = f32[2,56,8,256]{3,2,1,0:T(8,128)S(1)} fusion(f32[2,64,8,256]{3,2,1,0:T(8,128)S(1)} %pad_maximum_fusion, f32[2,12,8,256]{3,2,1,0:T(8,128)S(1)} %slice.602, f32[2,32,8,256]{3,2,1,0:T(8,128)S(1)} %copy-done.2, f32[2,12,8,256]{3,2,1,0:T(8,128)S(1)} %slice.601, f32[2,56,256]{2,1,0:T(8,128)S(1)} %get-tuple-element.11, ...), kind=kLoop, calls=%fused_computation.95 | loop fusion | flops 9175040 | bytes 11715072 | tf_op jit(solution)/shard_map/add | solution.py:90
  34.1 1.9 %fusion.51 = f32[2,48,8,256]{3,2,1,0:T(8,128)S(1)} fusion(f32[2,56,8,256]{3,2,1,0:T(8,128)S(1)} %fusion.24, f32[2,56,8,256]{3,2,1,0:T(8,128)S(1)} %maximum_convert_fusion, f32[2,64,8,256]{3,2,1,0:T(8,128)S(1)} %pad_maximum_fusion, f32[2,48,256]{2,1,0:T(8,128)S(1)} %slice.630, pred[8]{0:T(512)(128)(4,1)S(1)} %iota_compare_fusion.7), kind=kLoop, calls=%fused_computation.127 | loop fusion | flops 6881280 | bytes 10453504 | tf_op jit(solution)/shard_map/add | solution.py:90
  36.1 1.6 %fusion.78 = f32[2,40,8,256]{3,2,1,0:T(8,128)S(1)} fusion(f32[2,48,8,256]{3,2,1,0:T(8,128)S(1)} %fusion.51, f32[2,56,8,256]{3,2,1,0:T(8,128)S(1)} %maximum_convert_fusion, f32[2,56,8,256]{3,2,1,0:T(8,128)S(1)} %fusion.24, f32[2,40,256]{2,1,0:T(8,128)S(1)} %slice.643, pred[8]{0:T(512)(128)(4,1)S(1)} %iota_compare_fusion.7), kind=kLoop, calls=%fused_computation.159 | loop fusion | flops 5734400 | bytes 8733184 | tf_op jit(solution)/shard_map/add | solution.py:90
  37.7 2.2 %fusion.124 = (bf16[2,32,8,256]{3,2,1,0:T(8,128)(2,1)S(1)}, f32[2,32,8,256]{3,2,1,0:T(8,128)}) fusion(f32[2,56,8,256]{3,2,1,0:T(8,128)S(1)} %fusion.24, f32[2,48,8,256]{3,2,1,0:T(8,128)S(1)} %fusion.51, f32[2,40,8,256]{3,2,1,0:T(8,128)S(1)} %fusion.78, bf16[4,2,32,8,256]{4,3,2,1,0:T(8,128)(2,1)S(1)} %copy-done.3, f32[2,32,256]{2,1,0:T(8,128)S(1)} %slice.656, ...), kind=kLoop, calls=%fused_computation.211 | loop fusion | flops 6160384 | bytes 8847872 | tf_op jit(solution)/shard_map/convert_element_type | solution.py:95
  39.9 0.2 reshape_reshape.6
  40.2 0.2 copy.62
  40.4 1.1 %reshape.50 = bf16[32,2,2048]{2,1,0:T(2,128)(2,1)} reshape(bf16[32,2,32,64]{3,2,1,0:T(8,128)(2,1)S(1)} %bitcast.56) | data formatting | bytes 524288
  41.5 17.4 %all-to-all-start = ((bf16[32,2,2048]{2,1,0:T(2,128)(2,1)}), bf16[32,2,2048]{2,1,0:T(2,128)(2,1)S(1)}, u32[]{:S(2)}, u32[]{:S(2)}) async-start(bf16[32,2,2048]{2,1,0:T(2,128)(2,1)} %reshape.50), calls=%async_computation | async-start | bytes 524288 | tf_op jit(solution)/shard_map/all_to_all | solution.py:100
  58.9 0.1 copy.33
  59.0 1.7 %fusion.9 = bf16[64,32,32]{2,0,1:T(8,128)(2,1)S(1)} fusion(s32[64,32]{0,1:T(8,128)S(1)} %copy-done.7, bf16[64,32]{0,1:T(8,128)(2,1)S(1)} %get-tuple-element.20, bf16[64,32]{0,1:T(8,128)(2,1)S(1)} %get-tuple-element.21, bf16[64,32]{0,1:T(8,128)(2,1)S(1)} %get-tuple-element.22, bf16[64,32]{0,1:T(8,128)(2,1)S(1)} %get-tuple-element.23), kind=kLoop, calls=%fused_computation.80 | loop fusion | flops 589824 | bytes 155648 | tf_op jit(solution)/shard_map/jit(_where)/select_n | solution.py:115
  60.6 1.5 %convolution_convert_fusion.1 = bf16[64,64,32]{1,2,0:T(8,128)(2,1)S(1)} fusion(bf16[64,32,32]{2,0,1:T(8,128)(2,1)S(1)} %fusion.9, s32[64,32]{1,0:T(8,128)S(1)} %copy.33), kind=kOutput, calls=%fused_computation.68 | convolution fusion | flops 8650752 | bytes 401408 | tf_op jit(solution)/shard_map/dsr,drj->dsj/dot_general | solution.py:118
  62.1 1.1 %copy.39 = bf16[64,64,32]{0,2,1:T(8,128)(2,1)S(1)} copy(bf16[64,64,32]{1,2,0:T(8,128)(2,1)S(1)} %convolution_convert_fusion.1) | data formatting | bytes 524288 | tf_op jit(solution)/shard_map/convert_element_type | solution.py:120
  63.2 9.7 %all-to-all-done = bf16[32,2,2048]{2,1,0:T(2,128)(2,1)S(1)} async-done(((bf16[32,2,2048]{2,1,0:T(2,128)(2,1)}), bf16[32,2,2048]{2,1,0:T(2,128)(2,1)S(1)}, u32[]{:S(2)}, u32[]{:S(2)}) %all-to-all-start) | async-done | bytes 262176 | tf_op jit(solution)/shard_map/all_to_all | solution.py:100
  72.9 0.4 reshape.51
  73.3 1.3 %convolution_convert_fusion = bf16[64,64,64]{2,1,0:T(8,128)(2,1)S(1)} fusion(bf16[64,32,64]{2,1,0:T(8,128)(2,1)S(1)} %bitcast.55, s32[64,32]{1,0:T(8,128)S(1)} %copy.33), kind=kOutput, calls=%fused_computation.64 | convolution fusion | flops 17170432 | bytes 794624 | tf_op jit(solution)/shard_map/dsr,drc->dsc/dot_general | solution.py:117
  74.6 0.7 convolution_bitcast_fusion
  75.3 0.3 all_to_all.22
  75.7 22.6 %all_to_all.25 = f32[32,1,2048]{2,1,0:T(1,128)S(1)} all-to-all(f32[32,1,2048]{2,1,0:T(1,128)S(1)} %all_to_all.22), channel_id=1, replica_groups=mesh['dir'=32,'tile'=32] {'tile'}, dimensions={0} | all-to-all | bytes 524288 | tf_op jit(solution)/shard_map/all_to_all | solution.py:125
  98.3 0.2 reduce_sum.21
  98.5 0.7 reduce_sum.22
  (45 shorter events, 0.7 us)
Async XLA Ops:
  0.6 18.4 %copy-start = (f32[2,32,8,256]{3,2,1,0:T(8,128)S(1)}, f32[2,32,8,256]{3,2,1,0:T(8,128)}, u32[]{:S(2)}) copy-start(f32[2,32,8,256]{3,2,1,0:T(8,128)} %param.9) | copy-start | bytes 1572868
  1.7 17.4 %copy-start.2 = (f32[2,32,8,256]{3,2,1,0:T(8,128)S(1)}, f32[2,32,8,256]{3,2,1,0:T(8,128)}, u32[]{:S(2)}) copy-start(f32[2,32,8,256]{3,2,1,0:T(8,128)} %param.8) | copy-start | bytes 1572868
  2.8 23.8 %collective-permute-start.2 = (bf16[2,12,11,256]{3,2,1,0:T(8,128)(2,1)S(1)}, bf16[2,12,11,256]{3,2,1,0:T(8,128)(2,1)S(1)}, u32[]{:S(2)}, u32[]{:S(2)}) collective-permute-start(bf16[2,12,11,256]{3,2,1,0:T(8,128)(2,1)S(1)} %pad_maximum_fusion.3), channel_id=1, source_target_pairs={{0,1},{1,2},{2,3},{3,4},{4,5},{5,6},{6,7},{7,8},{8,9},{9,10},{10,1... | collective-permute-start | bytes 405512 | tf_op jit(solution)/shard_map/ppermute | solution.py:45
  6.4 20.2 %collective-permute-start.3 = (bf16[2,12,11,256]{3,2,1,0:T(8,128)(2,1)S(1)}, bf16[2,12,11,256]{3,2,1,0:T(8,128)(2,1)S(1)}, u32[]{:S(2)}, u32[]{:S(2)}) collective-permute-start(bf16[2,12,11,256]{3,2,1,0:T(8,128)(2,1)S(1)} %pad_maximum_fusion.4), channel_id=1, source_target_pairs={{1,0},{2,1},{3,2},{4,3},{5,4},{6,5},{7,6},{8,7},{9,8},{10,9},{11,1... | collective-permute-start | bytes 405512 | tf_op jit(solution)/shard_map/ppermute | solution.py:45
  19.1 6.1 %copy-start.5 = (s32[64,32,1]{0,2,1:T(1,128)S(1)}, s32[64,32,1]{0,2,1:T(1,128)}, u32[]{:S(2)}) copy-start(s32[64,32,1]{0,2,1:T(1,128)} %param.13) | copy-start | bytes 24580
  19.2 7.3 %copy-start.6 = (bf16[64,32,4]{0,2,1:T(4,128)(2,1)S(1)}, bf16[64,32,4]{0,2,1:T(4,128)(2,1)}, u32[]{:S(2)}) copy-start(bf16[64,32,4]{0,2,1:T(4,128)(2,1)} %param.15) | copy-start | bytes 49156
  19.2 7.5 %copy-start.4 = (bf16[4,2,32,256]{3,2,1,0:T(8,128)(2,1)S(1)}, bf16[4,2,32,256]{3,2,1,0:T(8,128)(2,1)}, u32[]{:S(2)}) copy-start(bf16[4,2,32,256]{3,2,1,0:T(8,128)(2,1)} %param.12) | copy-start | bytes 393220
  19.2 10.5 %collective-permute-start = (f32[2,28,8,256]{3,2,1,0:T(8,128)S(1)}, f32[2,28,8,256]{3,2,1,0:T(8,128)S(1)}, u32[]{:S(2)}, u32[]{:S(2)}) collective-permute-start(f32[2,28,8,256]{3,2,1,0:T(8,128)S(1)} %pad_maximum_fusion.1), channel_id=1, source_target_pairs={{0,1},{1,2},{2,3},{3,4},{4,5},{5,6},{6,7},{7,8},{8,9},{9,10},{10,1... | collective-permute-start | bytes 1376264 | tf_op jit(solution)/shard_map/ppermute | solution.py:45
  21.3 10.4 %collective-permute-start.1 = (f32[2,28,8,256]{3,2,1,0:T(8,128)S(1)}, f32[2,28,8,256]{3,2,1,0:T(8,128)S(1)}, u32[]{:S(2)}, u32[]{:S(2)}) collective-permute-start(f32[2,28,8,256]{3,2,1,0:T(8,128)S(1)} %pad_maximum_fusion.2), channel_id=1, source_target_pairs={{1,0},{2,1},{3,2},{4,3},{5,4},{6,5},{7,6},{8,7},{9,8},{10,9},{11,1... | collective-permute-start | bytes 1376264 | tf_op jit(solution)/shard_map/ppermute | solution.py:45
  26.7 1.0 copy-start.1
  36.1 1.7 %copy-start.3 = (bf16[4,2,32,8,256]{4,3,2,1,0:T(8,128)(2,1)S(1)}, bf16[4,2,32,8,256]{4,3,2,1,0:T(8,128)(2,1)}, u32[]{:S(2)}) copy-start(bf16[4,2,32,8,256]{4,3,2,1,0:T(8,128)(2,1)} %param.11) | copy-start | bytes 3145732
  40.1 18.8 %copy-start.7 = (s32[64,32]{0,1:T(8,128)S(1)}, s32[64,32]{0,1:T(8,128)}, u32[]{:S(2)}) copy-start(s32[64,32]{0,1:T(8,128)} %param.14) | copy-start | bytes 24580
  41.5 31.4 %all-to-all-start = ((bf16[32,2,2048]{2,1,0:T(2,128)(2,1)}), bf16[32,2,2048]{2,1,0:T(2,128)(2,1)S(1)}, u32[]{:S(2)}, u32[]{:S(2)}) async-start(bf16[32,2,2048]{2,1,0:T(2,128)(2,1)} %reshape.50), calls=%async_computation | async-start | bytes 524288 | tf_op jit(solution)/shard_map/all_to_all | solution.py:100
